TPU v7x, 128 devices: a whole 4x4x4 slice. The times are simulated.
128 devices in a mesh: req: 128 (over y, z, x, core).
Axes of the slice: x: 4, y: 4, z: 4, core: 2. Of those that a mesh axis runs over, the one named last changes fastest.
Arguments:
- hidden: bfloat16 [32768, 1024], P('req'), may hold values from -6 to 6
- draft_query: bfloat16 [32768, 1024], P('req'), may hold values from -204 to 204
- draft_key: bfloat16 [32768, 1024], P('req'), may hold values from -6 to 6
- draft_value: bfloat16 [32768, 1024], P('req'), may hold values from -6 to 6
- cache_keys: bfloat16 [12288, 16, 1024], P('req'), may hold values from -6 to 6
- cache_values: bfloat16 [12288, 16, 1024], P('req'), may hold values from -6 to 6
- page_target: int32 [12288, 1], P('req'), may hold values from 0 to 127; in each aligned block of 96 rows (0 to 95, 96 to 191, ...) at most 2 rows name the same one
- page_slot: int32 [12288], P('req'), may hold values from 0 to 3
- page_fill: int32 [12288], P('req'), may hold values from 1 to 16
- tree_parent: int32 [512, 64], P('req'), may hold values from -1 to 62, as said below
- tree_size: int32 [512], P('req'), may hold values from 32 to 64
- accepted_leaf: int32 [512], P('req'), may hold values from 0 to 63
- w_attn_out: bfloat16 [1024, 1024], replicated, may hold values from -0.1875 to 0.1875
- ln_gain: bfloat16 [1024], replicated, may hold values from 0.099609375 to 1.8984375
- w_in: bfloat16 [1024, 5248], replicated, may hold values from -0.1875 to 0.1875
- w_out: bfloat16 [2624, 1024], replicated, may hold values from -0.125 to 0.125
Outputs:
- layer_out: bfloat16 [32768, 1024], P('req')
- kept_keys: bfloat16 [32768, 1024], P('req')
- kept_values: bfloat16 [32768, 1024], P('req')
Inputs may be any that keep to these rules, and one draw needn't show every extreme that they name: `page_target`: among the 96 pages of one device each target device is named at most 2 times, a bound that some block reaches. `tree_parent`: slot 0 of every tree has parent -1; slot i > 0 has a parent below i.
All inputs are finite; a program needn't handle non-finite values.
Results may differ from a plain program's by a relative error of at most 0.011.
Values may be sent and summed in bfloat16 or wider, within the bound.
No kernel may reach another device: no remote copies, remote signals or barrier semaphores. Data moves between devices by JAX's collectives and lax.ppermute only.
A program may use at most 192 MiB of HBM per device.

v0:
```python
import functools

import jax
import jax.numpy as jnp
from jax import lax
from jax.experimental import pallas as pl
from jax.experimental.pallas import tpu as pltpu
from jax.sharding import PartitionSpec as P

HEADS = 16


def ancestor_closure(tree_parent):
    width = tree_parent.shape[1]
    ident = jnp.eye(width, dtype=jnp.float32)
    ancestors = (
        tree_parent[:, :, None] == jnp.arange(width, dtype=jnp.int32)[None, None, :]
    ).astype(jnp.float32) + ident
    for repeat in range((width - 1).bit_length()):
        ancestors = jnp.minimum(
            jnp.einsum("rij,rjk->rik", ancestors, ancestors, precision=lax.Precision.HIGHEST), 1.0
        )
    return ancestors


def rotate_positions(values, positions, heads):
    rows, width = values.shape
    head_size = width // heads
    half = head_size // 2
    inverse = jnp.power(160000.0, -(2.0 * jnp.arange(half, dtype=jnp.float32)) / head_size)
    angle = positions.astype(jnp.float32)[:, None] * inverse[None, :]
    cosine = jnp.cos(angle)[:, None, :]
    sine = jnp.sin(angle)[:, None, :]
    shaped = values.astype(jnp.float32).reshape(rows, heads, head_size)
    first = shaped[..., :half]
    second = shaped[..., half:]
    turned = jnp.concatenate(
        [first * cosine - second * sine, second * cosine + first * sine], axis=-1
    )
    return turned.reshape(rows, width).astype(jnp.bfloat16)


def _attend_kernel(q_ref, kc_ref, vc_ref, kd_ref, vd_ref, kown_ref, tmask_ref, o_ref, *,
                   tree_width, head_size, scale):
    rows, lanes = q_ref.shape
    q = q_ref[...]
    kc = kc_ref[...].reshape(-1, lanes)
    vc = vc_ref[...].reshape(-1, lanes)
    kd = kd_ref[...]
    vd = vd_ref[...]
    lane = lax.broadcasted_iota(jnp.int32, (1, lanes), 1)
    qown = lax.broadcasted_iota(jnp.int32, (rows, 1), 0) // tree_width
    cmask = qown == kown_ref[...]
    tmask = tmask_ref[...] > 0.5
    dims = (((1,), (1,)), ((), ()))
    outs = []
    for part in range(lanes // head_size):
        sel = (lane >= part * head_size) & (lane < (part + 1) * head_size)
        qh = jnp.where(sel, q, jnp.zeros((), q.dtype))
        sc = lax.dot_general(qh, kc, dims, preferred_element_type=jnp.float32) * scale
        sd = lax.dot_general(qh, kd, dims, preferred_element_type=jnp.float32) * scale
        sc = jnp.where(cmask, sc, -1e30)
        sd = jnp.where(tmask, sd, -1e30)
        top = jnp.maximum(jnp.max(sc, axis=1, keepdims=True), jnp.max(sd, axis=1, keepdims=True))
        pc = jnp.where(cmask, jnp.exp(sc - top), 0.0)
        pd = jnp.where(tmask, jnp.exp(sd - top), 0.0)
        inv = 1.0 / (jnp.sum(pc, axis=1, keepdims=True) + jnp.sum(pd, axis=1, keepdims=True))
        ctx = jnp.dot((pc * inv).astype(jnp.bfloat16), vc, preferred_element_type=jnp.float32)
        ctx = ctx + jnp.dot((pd * inv).astype(jnp.bfloat16), vd, preferred_element_type=jnp.float32)
        outs.append((sel, ctx))
    result = outs[0][1]
    for sel, ctx in outs[1:]:
        result = jnp.where(sel, ctx, result)
    o_ref[...] = result.astype(o_ref.dtype)


def attend(query_rot, recv, key_rot, draft_value, key_owner, tree_mask, tree_width):
    rows, width = query_rot.shape
    head_size = width // HEADS
    lanes = 128
    slots, _, page_len, _ = recv.shape
    kernel = functools.partial(
        _attend_kernel, tree_width=tree_width, head_size=head_size, scale=1.0 / head_size**0.5
    )
    return pl.pallas_call(
        kernel,
        grid=(width // lanes,),
        in_specs=[
            pl.BlockSpec((rows, lanes), lambda h: (0, h)),
            pl.BlockSpec((slots, None, page_len, lanes), lambda h: (0, 0, 0, h)),
            pl.BlockSpec((slots, None, page_len, lanes), lambda h: (0, 1, 0, h)),
            pl.BlockSpec((rows, lanes), lambda h: (0, h)),
            pl.BlockSpec((rows, lanes), lambda h: (0, h)),
            pl.BlockSpec((1, slots * page_len), lambda h: (0, 0)),
            pl.BlockSpec((rows, rows), lambda h: (0, 0)),
        ],
        out_specs=pl.BlockSpec((rows, lanes), lambda h: (0, h)),
        out_shape=jax.ShapeDtypeStruct((rows, width), jnp.bfloat16),
        compiler_params=pltpu.CompilerParams(vmem_limit_bytes=60 * 1024 * 1024),
    )(query_rot, recv, recv, key_rot, draft_value, key_owner, tree_mask)


def feed_forward(rows_in, ln_gain, w_in, w_out):
    inner = w_out.shape[0]
    floats = rows_in.astype(jnp.float32)
    mean_value = jnp.mean(floats, axis=1, keepdims=True)
    centred = floats - mean_value
    variance = jnp.mean(centred * centred, axis=1, keepdims=True)
    normed = (centred * lax.rsqrt(variance + 1e-05) * ln_gain.astype(jnp.float32)[None, :]).astype(
        jnp.bfloat16
    )
    both = jnp.dot(normed, w_in, preferred_element_type=jnp.float32)
    middle = (jax.nn.gelu(both[:, :inner], approximate=False) * both[:, inner:]).astype(
        jnp.bfloat16
    )
    return jnp.dot(middle, w_out, preferred_element_type=jnp.float32).astype(jnp.bfloat16)


def local(
    hidden,
    draft_query,
    draft_key,
    draft_value,
    cache_keys,
    cache_values,
    page_target,
    page_slot,
    page_fill,
    tree_parent,
    tree_size,
    accepted_leaf,
    w_attn_out,
    ln_gain,
    w_in,
    w_out,
):
    devices = lax.axis_size("req")
    pages_here, page_len, width = cache_keys.shape
    per_target = max(2, -(-pages_here // devices))
    target = page_target[:, 0]
    onehot = (target[:, None] == jnp.arange(devices, dtype=jnp.int32)[None, :]).astype(jnp.int32)
    within = jnp.sum(jnp.cumsum(onehot, axis=0) * onehot, axis=1) - 1
    dest_slot = target * per_target + within
    slot_count = devices * per_target
    matches = dest_slot[None, :] == jnp.arange(slot_count, dtype=jnp.int32)[:, None]
    filled = jnp.any(matches, axis=1)
    source = jnp.sum(
        jnp.where(matches, jnp.arange(pages_here, dtype=jnp.int32)[None, :], 0), axis=1
    )
    send_kv = jnp.stack([cache_keys[source], cache_values[source]], axis=1)
    send_meta = jnp.stack(
        [jnp.where(filled, page_fill[source], 0), page_slot[source]], axis=1
    ).reshape(devices, per_target * 2)
    recv_meta = lax.all_to_all(send_meta, "req", 0, 0, tiled=True).reshape(slot_count, 2)
    recv = lax.all_to_all(
        send_kv.reshape(devices, per_target * 2, page_len, width), "req", 0, 0, tiled=True
    ).reshape(slot_count, 2, page_len, width)
    recv_fill = recv_meta[:, 0]
    recv_owner = recv_meta[:, 1]
    requests, tree_width = tree_parent.shape
    rows = requests * tree_width
    ancestors = ancestor_closure(tree_parent)
    depth = (jnp.sum(ancestors, axis=2) - 1.0).astype(jnp.int32)
    request_ids = jnp.arange(requests, dtype=jnp.int32)
    cache_len = jnp.sum(
        jnp.where(recv_owner[None, :] == request_ids[:, None], recv_fill[None, :], 0), axis=1
    )
    positions = (cache_len[:, None] + depth).reshape(rows)
    query_rot = rotate_positions(draft_query, positions, HEADS)
    key_rot = rotate_positions(draft_key, positions, HEADS)
    key_owner = jnp.where(
        jnp.arange(page_len, dtype=jnp.int32)[None, :] < recv_fill[:, None], recv_owner[:, None], -1
    ).reshape(1, -1)
    tree_mask = (
        ancestors[:, :, None, :] * jnp.eye(requests, dtype=jnp.float32)[:, None, :, None]
    ).reshape(rows, rows)
    context = attend(query_rot, recv, key_rot, draft_value, key_owner, tree_mask, tree_width)
    attended = (
        hidden.astype(jnp.float32)
        + jnp.dot(context, w_attn_out, preferred_element_type=jnp.float32)
    ).astype(jnp.bfloat16)
    alive_mask = (jnp.arange(tree_width, dtype=jnp.int32)[None, :] < tree_size[:, None]).reshape(
        rows
    )
    ffn_out = feed_forward(attended, ln_gain, w_in, w_out)
    layer_out = jnp.where(
        alive_mask[:, None], attended.astype(jnp.float32) + ffn_out.astype(jnp.float32), 0.0
    ).astype(jnp.bfloat16)
    leaf_index = jnp.minimum(accepted_leaf, tree_size - 1)
    leaf_onehot = (jnp.arange(tree_width, dtype=jnp.int32)[None, :] == leaf_index[:, None]).astype(
        jnp.float32
    )
    path = jnp.einsum("ri,rij->rj", leaf_onehot, ancestors, precision=lax.Precision.HIGHEST)
    select = (
        path[:, None, :]
        * (depth[:, None, :] == jnp.arange(tree_width, dtype=jnp.int32)[None, :, None]).astype(
            jnp.float32
        )
    ).astype(jnp.bfloat16)
    kept_keys = jnp.einsum(
        "rkj,rjd->rkd",
        select,
        key_rot.reshape(requests, tree_width, width),
        preferred_element_type=jnp.float32,
    )
    kept_values = jnp.einsum(
        "rkj,rjd->rkd",
        select,
        draft_value.reshape(requests, tree_width, width),
        preferred_element_type=jnp.float32,
    )
    return (
        layer_out,
        kept_keys.reshape(rows, width).astype(jnp.bfloat16),
        kept_values.reshape(rows, width).astype(jnp.bfloat16),
    )


def solution(mesh):
    placed = (
        P("req", None),
        P("req", None),
        P("req", None),
        P("req", None),
        P("req", None, None),
        P("req", None, None),
        P("req", None),
        P("req"),
        P("req"),
        P("req", None),
        P("req"),
        P("req"),
        P(),
        P(),
        P(),
        P(),
    )
    return jax.shard_map(
        local,
        mesh=mesh,
        in_specs=placed,
        out_specs=(P("req", None), P("req", None), P("req", None)),
        check_vma=False,
    )
```

profile of v0, /device:TPU:12, one launch (start us, length us, event | category | flops | bytes accessed | tf_op | source)
XLA Modules:
  0.0 363.4 jit_solution(2153888995910865553)
XLA Ops:
  0.6 0.9 fusion.51
  1.5 0.1 reduce_window_sum.11
  1.7 0.8 select_reduce_fusion.1
  2.5 0.7 add_add_fusion
  3.3 0.1 fusion.42
  3.4 1.9 gather_fusion.1
  5.3 1.9 gather_fusion
  7.2 0.1 copy.39
  7.4 0.7 all_to_all.9
  8.1 10.4 %all-to-all-start = ((s32[128,1,4]{2,1,0:T(1,128)}), s32[128,1,4]{2,1,0:T(1,128)S(1)}, u32[]{:S(2)}, u32[]{:S(2)}) async-start(s32[128,1,4]{2,1,0:T(1,128)} %bitcast.6), calls=%async_computation | async-start | bytes 131072 | tf_op jit(solution)/shard_map/all_to_all | solution.py:154
  18.5 8.4 %gather_fusion.3 = bf16[256,16,1024]{2,1,0:T(8,128)(2,1)} fusion(bf16[96,16,1024]{2,1,0:T(8,128)(2,1)S(1)} %copy-done, s32[1024]{0:T(1024)S(1)} %pad_clamp_fusion), kind=kCustom, calls=%fused_computation.3 | custom fusion | bytes 16778240 | tf_op jit(solution)/shard_map/gather | solution.py:150
  26.9 10.3 %gather_fusion.2 = bf16[256,16,1024]{2,1,0:T(8,128)(2,1)} fusion(bf16[96,16,1024]{2,1,0:T(8,128)(2,1)} %param.20, s32[1024]{0:T(1024)S(1)} %pad_clamp_fusion), kind=kCustom, calls=%fused_computation.2 | custom fusion | bytes 16778240 | tf_op jit(solution)/shard_map/gather | solution.py:150
  37.2 13.8 %pad_maximum_fusion = bf16[256,2,16,1024]{3,2,1,0:T(8,128)(2,1)} fusion(bf16[256,1,16,1024]{3,2,1,0:T(8,128)(2,1)} %bitcast.43, bf16[256,1,16,1024]{3,2,1,0:T(8,128)(2,1)} %bitcast.44), kind=kLoop, calls=%fused_computation.4 | loop fusion | flops 8388608 | bytes 33554432 | tf_op jit(solution)/shard_map/stack | solution.py:150
  51.0 10.2 %all-to-all-start.1 = ((bf16[128,4,16,1024]{3,2,1,0:T(8,128)(2,1)}), bf16[128,4,16,1024]{3,2,1,0:T(8,128)(2,1)}, u32[]{:S(2)}, u32[]{:S(2)}) async-start(bf16[128,4,16,1024]{3,2,1,0:T(8,128)(2,1)} %bitcast.42), calls=%async_computation.1 | async-start | bytes 33554432 | tf_op jit(solution)/shard_map/all_to_all | solution.py:155
  61.3 0.2 copy.38
  61.5 0.1 convert.10
  61.6 0.7 copy-done.4
  62.3 0.2 copy.43
  62.6 0.1 convert.11
  62.7 0.4 convolution_minimum_fusion.5
  63.1 0.3 convolution_minimum_fusion.4
  63.4 0.3 convolution_minimum_fusion.3
  63.6 0.3 convolution_minimum_fusion.2
  63.9 0.3 convolution_minimum_fusion.1
  64.1 0.4 fusion.89
  64.5 0.2 broadcast_multiply_fusion
  64.7 1.0 mul.182.tmask_ref
  66.0 0.2 fusion.53
  66.2 1.1 convolution_convert_fusion.1
  67.2 0.5 broadcast.242
  67.7 0.8 reduce.7
  68.6 0.2 slice_reduce_fusion.1
  68.9 0.1 select_reduce_fusion.2
  69.1 0.2 multiply_cosine_fusion
  69.4 0.2 subtract_convert_fusion
  69.6 1.0 copy.44.q_ref
  70.6 0.1 multiply_subtract_fusion
  70.8 0.4 reshape.297
  71.2 1.0 copy.45.kd_ref
  72.2 0.1 fusion.41
  72.3 0.7 select_n.59.kown_ref
  73.0 1.3 convolution_convert_fusion
  74.3 225.6 %all-to-all-done.1 = bf16[128,4,16,1024]{3,2,1,0:T(8,128)(2,1)} async-done(((bf16[128,4,16,1024]{3,2,1,0:T(8,128)(2,1)}), bf16[128,4,16,1024]{3,2,1,0:T(8,128)(2,1)}, u32[]{:S(2)}, u32[]{:S(2)}) %all-to-all-start.1) | async-done | bytes 16777248 | tf_op jit(solution)/shard_map/all_to_all | solution.py:155
  299.9 46.2 %shard_map.175 = bf16[256,1024]{1,0:T(8,128)(2,1)} custom-call(bf16[256,1024]{1,0:T(8,128)(2,1)} %copy.44.q_ref, bf16[256,2,16,1024]{3,2,1,0:T(8,128)(2,1)} %bitcast.12.kc_ref.vc_ref, bf16[256,2,16,1024]{3,2,1,0:T(8,128)(2,1)} %bitcast.12.kc_ref.vc_ref, bf16[256,1024]{1,0:T(8,128)(2,1)} %copy.45.kd_ref, bf16[256,1024]{1,0:T(8,128)(2,1)} %vd_ref.1, ...), custom_call_target="tpu_custom_call" | custom-call | tf_op jit(solution)/shard_map/pallas_call | solution.py:85
  346.2 2.0 convert_reduce_fusion
  348.2 0.3 fusion.30
  348.5 6.5 %fusion.34 = f32[256,5248]{1,0:T(8,128)S(1)} fusion(bf16[1024,5248]{1,0:T(8,128)(2,1)} %param.30, bf16[256,1024]{1,0:T(8,128)(2,1)S(1)} %get-tuple-element.14, f32[1024]{0:T(1024)S(1)} %convert_element_type.114, f32[256]{0:T(256)S(1)} %add_rsqrt_fusion, f32[256]{0:T(256)S(1)} %broadcast_multiply_fusion.1), kind=kOutput, calls=%fused_computation.50 | convolution fusion | flops 2752774144 | bytes 16652288 | tf_op jit(solution)/shard_map/dot_general | solution.py:112
  355.1 8.3 %fusion.27 = bf16[256,1024]{1,0:T(8,128)(2,1)} fusion(bf16[2624,1024]{1,0:T(8,128)(2,1)S(1)} %bitcast.61, f32[256,5248]{1,0:T(8,128)S(1)} %fusion.34, bf16[256,1024]{1,0:T(8,128)(2,1)S(1)} %get-tuple-element.14, pred[256]{0:T(512)(128)(4,1)S(1)} %lt.59), kind=kOutput, calls=%fused_computation.38 | convolution fusion | flops 1421639680 | bytes 11928064 | tf_op jit(solution)/shard_map/dot_general | solution.py:116
  (48 shorter events, 0.8 us)
Async XLA Ops:
  0.6 17.9 %copy-start = (bf16[96,16,1024]{2,1,0:T(8,128)(2,1)S(1)}, bf16[96,16,1024]{2,1,0:T(8,128)(2,1)}, u32[]{:S(2)}) copy-start(bf16[96,16,1024]{2,1,0:T(8,128)(2,1)} %param.21) | copy-start | bytes 9437188
  8.1 43.0 %all-to-all-start = ((s32[128,1,4]{2,1,0:T(1,128)}), s32[128,1,4]{2,1,0:T(1,128)S(1)}, u32[]{:S(2)}, u32[]{:S(2)}) async-start(s32[128,1,4]{2,1,0:T(1,128)} %bitcast.6), calls=%async_computation | async-start | bytes 131072 | tf_op jit(solution)/shard_map/all_to_all | solution.py:154
  51.0 10.2 %copy-start.3 = (bf16[256,1024]{1,0:T(8,128)(2,1)S(1)}, bf16[256,1024]{1,0:T(8,128)(2,1)}, u32[]{:S(2)}) copy-start(bf16[256,1024]{1,0:T(8,128)(2,1)} %param.17) | copy-start | bytes 1572868
  51.0 248.9 %all-to-all-start.1 = ((bf16[128,4,16,1024]{3,2,1,0:T(8,128)(2,1)}), bf16[128,4,16,1024]{3,2,1,0:T(8,128)(2,1)}, u32[]{:S(2)}, u32[]{:S(2)}) async-start(bf16[128,4,16,1024]{3,2,1,0:T(8,128)(2,1)} %bitcast.42), calls=%async_computation.1 | async-start | bytes 33554432 | tf_op jit(solution)/shard_map/all_to_all | solution.py:155
  61.3 1.0 copy-start.4
  61.3 1.4 copy-start.6
  62.5 3.2 copy-start.5
  62.5 3.2 copy-start.9
  62.6 3.3 copy-start.10
  62.6 3.6 copy-start.2
  299.9 46.2 %copy-start.7 = (bf16[1024,1024]{1,0:T(8,128)(2,1)S(1)}, bf16[1024,1024]{1,0:T(8,128)(2,1)}, u32[]{:S(2)}) copy-start(bf16[1024,1024]{1,0:T(8,128)(2,1)} %param.28) | copy-start | bytes 6291460
  299.9 46.2 %copy-start.8 = (bf16[256,1024]{1,0:T(8,128)(2,1)S(1)}, bf16[256,1024]{1,0:T(8,128)(2,1)}, u32[]{:S(2)}) copy-start(bf16[256,1024]{1,0:T(8,128)(2,1)} %param.16) | copy-start | bytes 1572868
  346.2 8.9 %slice-start = ((s8[5373952]{0:T(1024)(128)(4,1)}), s8[4194304]{0:T(1024)(128)(4,1)S(1)}, s32[]{:S(2)}) async-start(s8[5373952]{0:T(1024)(128)(4,1)} %bitcast.60), calls=%async_computation.2 | async-start | bytes 8388608
  348.5 6.6 %slice-start.1 = ((s8[5373952]{0:T(1024)(128)(4,1)}), s8[1179648]{0:T(1024)(128)(4,1)S(1)}, s32[]{:S(2)}) async-start(s8[5373952]{0:T(1024)(128)(4,1)} %bitcast.60), calls=%async_computation.3 | async-start | bytes 2359296
  355.1 8.3 %copy-start.1 = (bf16[96,16,1024]{2,1,0:T(8,128)(2,1)S(1)}, bf16[96,16,1024]{2,1,0:T(8,128)(2,1)}, u32[]{:S(2)}) copy-start(bf16[96,16,1024]{2,1,0:T(8,128)(2,1)} %param.21) | copy-start | bytes 9437188
where the time goes:
time: 364 us; the launch traced here: 363 us
  waiting for transfers between devices  226 us (62%)
  Pallas kernels  46.2 us (13%)
  local copies, waits for them, and re-layouts  29.7 us (8%)
  matrix products  21.1 us (6%)
  starting transfers between devices  20.6 us (6%)
  other arithmetic  19.1 us (5%)
    all_to_all x1, waiting for transfers between devices, local(): lax.all_to_all(send_kv.reshape(devices, per_target * 2, page_len, width),...  226 us
    pallas_call x1, Pallas kernels, attend(): pl.pallas_call(kernel, grid=(width // lanes,), in_specs=[pl.BlockSpec((ro...  46.2 us
    gather x2, local copies, waits for them, and re-layouts, local(): send_kv = jnp.stack([cache_keys[source], cache_values[source]], axis=1)  18.7 us
    another operation x1, other arithmetic, local(): send_kv = jnp.stack([cache_keys[source], cache_values[source]], axis=1)  13.8 us
    all_to_all x1, starting transfers between devices, local(): lax.all_to_all(send_meta, 'req', 0, 0, tiled=True).reshape(slot_count, 2)  10.4 us
    all_to_all x1, starting transfers between devices, local(): lax.all_to_all(send_kv.reshape(devices, per_target * 2, page_len, width),...  10.2 us
    dot_general x1, matrix products, feed_forward(): jnp.dot(middle, w_out, preferred_element_type=jnp.float32)  8.28 us
  transfers between devices with their start and end apart: 2, of which 1 were waited for; matrix products, arithmetic and copies ran while one was open for 12% of the time, Pallas kernels for 0%

commit v1 on v0

--- a/solution.py
+++ b/solution.py
@@ -40,20 +40,17 @@
     return turned.reshape(rows, width).astype(jnp.bfloat16)
 
 
-def _attend_kernel(q_ref, kc_ref, vc_ref, kd_ref, vd_ref, kown_ref, tmask_ref, o_ref, *,
-                   tree_width, head_size, scale):
+def _probs_kernel(q_ref, kc_ref, kd_ref, kown_ref, tmask_ref, pc_ref, pd_ref, *,
+                  tree_width, head_size, scale):
     rows, lanes = q_ref.shape
     q = q_ref[...]
     kc = kc_ref[...].reshape(-1, lanes)
-    vc = vc_ref[...].reshape(-1, lanes)
     kd = kd_ref[...]
-    vd = vd_ref[...]
     lane = lax.broadcasted_iota(jnp.int32, (1, lanes), 1)
     qown = lax.broadcasted_iota(jnp.int32, (rows, 1), 0) // tree_width
     cmask = qown == kown_ref[...]
     tmask = tmask_ref[...] > 0.5
     dims = (((1,), (1,)), ((), ()))
-    outs = []
     for part in range(lanes // head_size):
         sel = (lane >= part * head_size) & (lane < (part + 1) * head_size)
         qh = jnp.where(sel, q, jnp.zeros((), q.dtype))
@@ -62,42 +59,74 @@
         sc = jnp.where(cmask, sc, -1e30)
         sd = jnp.where(tmask, sd, -1e30)
         top = jnp.maximum(jnp.max(sc, axis=1, keepdims=True), jnp.max(sd, axis=1, keepdims=True))
-        pc = jnp.where(cmask, jnp.exp(sc - top), 0.0)
-        pd = jnp.where(tmask, jnp.exp(sd - top), 0.0)
+        pc = jnp.exp(sc - top)
+        pd = jnp.exp(sd - top)
         inv = 1.0 / (jnp.sum(pc, axis=1, keepdims=True) + jnp.sum(pd, axis=1, keepdims=True))
-        ctx = jnp.dot((pc * inv).astype(jnp.bfloat16), vc, preferred_element_type=jnp.float32)
-        ctx = ctx + jnp.dot((pd * inv).astype(jnp.bfloat16), vd, preferred_element_type=jnp.float32)
-        outs.append((sel, ctx))
-    result = outs[0][1]
-    for sel, ctx in outs[1:]:
-        result = jnp.where(sel, ctx, result)
+        pc_ref[part] = (pc * inv).astype(pc_ref.dtype)
+        pd_ref[part] = (pd * inv).astype(pd_ref.dtype)
+
+
+def _context_kernel(pc_ref, pd_ref, vc_ref, vd_ref, o_ref, *, head_size):
+    rows, lanes = o_ref.shape
+    vc = vc_ref[...].reshape(-1, lanes)
+    vd = vd_ref[...]
+    lane = lax.broadcasted_iota(jnp.int32, (1, lanes), 1)
+    result = None
+    for part in range(lanes // head_size):
+        ctx = jnp.dot(pc_ref[part], vc, preferred_element_type=jnp.float32)
+        ctx = ctx + jnp.dot(pd_ref[part], vd, preferred_element_type=jnp.float32)
+        if result is None:
+            result = ctx
+        else:
+            sel = (lane >= part * head_size) & (lane < (part + 1) * head_size)
+            result = jnp.where(sel, ctx, result)
     o_ref[...] = result.astype(o_ref.dtype)
 
 
-def attend(query_rot, recv, key_rot, draft_value, key_owner, tree_mask, tree_width):
+def attend(query_rot, recv_k, recv_v, key_rot, draft_value, key_owner, tree_mask, tree_width):
     rows, width = query_rot.shape
     head_size = width // HEADS
     lanes = 128
-    slots, _, page_len, _ = recv.shape
-    kernel = functools.partial(
-        _attend_kernel, tree_width=tree_width, head_size=head_size, scale=1.0 / head_size**0.5
-    )
-    return pl.pallas_call(
-        kernel,
-        grid=(width // lanes,),
+    per = lanes // head_size
+    groups = width // lanes
+    slots, page_len, _ = recv_k.shape
+    keys = slots * page_len
+    params = pltpu.CompilerParams(vmem_limit_bytes=60 * 1024 * 1024)
+    probs_c, probs_d = pl.pallas_call(
+        functools.partial(
+            _probs_kernel, tree_width=tree_width, head_size=head_size, scale=1.0 / head_size**0.5
+        ),
+        grid=(groups,),
         in_specs=[
             pl.BlockSpec((rows, lanes), lambda h: (0, h)),
-            pl.BlockSpec((slots, None, page_len, lanes), lambda h: (0, 0, 0, h)),
-            pl.BlockSpec((slots, None, page_len, lanes), lambda h: (0, 1, 0, h)),
+            pl.BlockSpec((slots, page_len, lanes), lambda h: (0, 0, h)),
             pl.BlockSpec((rows, lanes), lambda h: (0, h)),
+            pl.BlockSpec((1, keys), lambda h: (0, 0)),
+            pl.BlockSpec((rows, rows), lambda h: (0, 0)),
+        ],
+        out_specs=[
+            pl.BlockSpec((None, per, rows, keys), lambda h: (h, 0, 0, 0)),
+            pl.BlockSpec((None, per, rows, rows), lambda h: (h, 0, 0, 0)),
+        ],
+        out_shape=[
+            jax.ShapeDtypeStruct((groups, per, rows, keys), jnp.bfloat16),
+            jax.ShapeDtypeStruct((groups, per, rows, rows), jnp.bfloat16),
+        ],
+        compiler_params=params,
+    )(query_rot, recv_k, key_rot, key_owner, tree_mask)
+    return pl.pallas_call(
+        functools.partial(_context_kernel, head_size=head_size),
+        grid=(groups,),
+        in_specs=[
+            pl.BlockSpec((None, per, rows, keys), lambda h: (h, 0, 0, 0)),
+            pl.BlockSpec((None, per, rows, rows), lambda h: (h, 0, 0, 0)),
+            pl.BlockSpec((slots, page_len, lanes), lambda h: (0, 0, h)),
             pl.BlockSpec((rows, lanes), lambda h: (0, h)),
-            pl.BlockSpec((1, slots * page_len), lambda h: (0, 0)),
-            pl.BlockSpec((rows, rows), lambda h: (0, 0)),
         ],
         out_specs=pl.BlockSpec((rows, lanes), lambda h: (0, h)),
         out_shape=jax.ShapeDtypeStruct((rows, width), jnp.bfloat16),
-        compiler_params=pltpu.CompilerParams(vmem_limit_bytes=60 * 1024 * 1024),
-    )(query_rot, recv, recv, key_rot, draft_value, key_owner, tree_mask)
+        compiler_params=params,
+    )(probs_c, probs_d, recv_v, draft_value)
 
 
 def feed_forward(rows_in, ln_gain, w_in, w_out):
@@ -147,14 +176,16 @@
     source = jnp.sum(
         jnp.where(matches, jnp.arange(pages_here, dtype=jnp.int32)[None, :], 0), axis=1
     )
-    send_kv = jnp.stack([cache_keys[source], cache_values[source]], axis=1)
     send_meta = jnp.stack(
         [jnp.where(filled, page_fill[source], 0), page_slot[source]], axis=1
     ).reshape(devices, per_target * 2)
+    recv_k = lax.all_to_all(
+        cache_keys[source].reshape(devices, per_target, page_len, width), "req", 0, 0, tiled=True
+    ).reshape(slot_count, page_len, width)
+    recv_v = lax.all_to_all(
+        cache_values[source].reshape(devices, per_target, page_len, width), "req", 0, 0, tiled=True
+    ).reshape(slot_count, page_len, width)
     recv_meta = lax.all_to_all(send_meta, "req", 0, 0, tiled=True).reshape(slot_count, 2)
-    recv = lax.all_to_all(
-        send_kv.reshape(devices, per_target * 2, page_len, width), "req", 0, 0, tiled=True
-    ).reshape(slot_count, 2, page_len, width)
     recv_fill = recv_meta[:, 0]
     recv_owner = recv_meta[:, 1]
     requests, tree_width = tree_parent.shape
@@ -174,7 +205,7 @@
     tree_mask = (
         ancestors[:, :, None, :] * jnp.eye(requests, dtype=jnp.float32)[:, None, :, None]
     ).reshape(rows, rows)
-    context = attend(query_rot, recv, key_rot, draft_value, key_owner, tree_mask, tree_width)
+    context = attend(query_rot, recv_k, recv_v, key_rot, draft_value, key_owner, tree_mask, tree_width)
     attended = (
         hidden.astype(jnp.float32)
         + jnp.dot(context, w_attn_out, preferred_element_type=jnp.float32)

time: 364 us -> 290 us (0.80)
  waiting for transfers between devices: 226 us -> 149 us
  other arithmetic: 19.1 us -> 5.3 us
  starting transfers between devices: 20.6 us -> 31.6 us
  Pallas kernels: 46.2 us -> 52.3 us
    all_to_all x1 -> x2, waiting for transfers between devices: 226 us -> 149 us  [the longest x1 93.1 us: local(): lax.all_to_all(cache_keys[source].reshape(devices, per_target, page_len,...]
    another operation x2 -> x1, other arithmetic: 14 us -> 0.15 us  [the longest x1 13.8 us: local(): send_kv = jnp.stack([cache_keys[source], cache_values[source]], axis=1)]
    all_to_all x1 -> x2, starting transfers between devices: 10.2 us -> 21.2 us  [the longest x1 11 us: local(): lax.all_to_all(cache_values[source].reshape(devices, per_target, page_len...]
    pallas_call x1 -> x2, Pallas kernels: 46.2 us -> 52.3 us  [the longest x1 33.8 us: attend(): pl.pallas_call(functools.partial(_probs_kernel, tree_width=tree_width, he...]
  transfers between devices with their start and end apart: 2 -> 3, of which waited for: 1 -> 2; matrix products, arithmetic and copies ran while one was open for 12% -> 10% of each run, Pallas kernels for 0% -> 12%
where the time goes in v1:
time: 290 us; the launch traced here: 288 us
  waiting for transfers between devices  149 us (51%)
  Pallas kernels  52.3 us (18%)
  starting transfers between devices  31.6 us (11%)
  local copies, waits for them, and re-layouts  27.8 us (10%)
  matrix products  21.1 us (7%)
  other arithmetic  5.3 us (2%)
    all_to_all x1, waiting for transfers between devices, local(): lax.all_to_all(cache_keys[source].reshape(devices, per_target, page_len,...  93.1 us
    all_to_all x1, waiting for transfers between devices, local(): lax.all_to_all(cache_values[source].reshape(devices, per_target, page_len...  56.2 us
    pallas_call x1, Pallas kernels, attend(): pl.pallas_call(functools.partial(_probs_kernel, tree_width=tree_width, he...  33.8 us
    pallas_call x1, Pallas kernels, attend(): pl.pallas_call(functools.partial(_context_kernel, head_size=head_size), g...  18.6 us
    all_to_all x1, starting transfers between devices, local(): lax.all_to_all(cache_values[source].reshape(devices, per_target, page_len...  11 us
    all_to_all x1, starting transfers between devices, local(): lax.all_to_all(send_meta, 'req', 0, 0, tiled=True).reshape(slot_count, 2)  10.4 us
    all_to_all x1, starting transfers between devices, local(): lax.all_to_all(cache_keys[source].reshape(devices, per_target, page_len,...  10.2 us
    gather x1, local copies, waits for them, and re-layouts, local(): cache_values[source].reshape(devices, per_target, page_len, width)  8.4 us
  transfers between devices with their start and end apart: 3, of which 2 were waited for; matrix products, arithmetic and copies ran while one was open for 10% of the time, Pallas kernels for 12%

profile of v1, /device:TPU:12, one launch (start us, length us, event | category | flops | bytes accessed | tf_op | source)
XLA Modules:
  0.0 288.4 jit_solution(17300100722578234978)
XLA Ops:
  0.6 0.9 fusion.51
  1.5 0.1 reduce_window_sum.11
  1.7 0.8 select_reduce_fusion.1
  2.5 0.7 add_add_fusion
  3.4 1.9 gather_fusion
  5.3 1.9 gather_fusion.1
  7.2 0.1 copy.39
  7.4 0.7 all_to_all.12
  8.1 10.4 %all-to-all-start = ((s32[128,1,4]{2,1,0:T(1,128)}), s32[128,1,4]{2,1,0:T(1,128)S(1)}, u32[]{:S(2)}, u32[]{:S(2)}) async-start(s32[128,1,4]{2,1,0:T(1,128)} %bitcast.6), calls=%async_computation | async-start | bytes 131072 | tf_op jit(solution)/shard_map/all_to_all | solution.py:188
  18.5 8.4 %gather_fusion.2 = bf16[256,16,1024]{2,1,0:T(8,128)(2,1)} fusion(bf16[96,16,1024]{2,1,0:T(8,128)(2,1)S(1)} %copy-done, s32[1024]{0:T(1024)S(1)} %pad_clamp_fusion), kind=kCustom, calls=%fused_computation.2 | custom fusion | bytes 16778240 | tf_op jit(solution)/shard_map/gather | solution.py:183
  26.9 10.2 %all-to-all-start.1 = ((bf16[128,2,16,1024]{3,2,1,0:T(8,128)(2,1)}), bf16[128,2,16,1024]{3,2,1,0:T(8,128)(2,1)}, u32[]{:S(2)}, u32[]{:S(2)}) async-start(bf16[128,2,16,1024]{3,2,1,0:T(8,128)(2,1)} %bitcast.43), calls=%async_computation.1 | async-start | bytes 16777216 | tf_op jit(solution)/shard_map/all_to_all | solution.py:182
  37.1 8.4 %gather_fusion.3 = bf16[256,16,1024]{2,1,0:T(8,128)(2,1)} fusion(bf16[96,16,1024]{2,1,0:T(8,128)(2,1)S(1)} %copy-done.2, s32[1024]{0:T(1024)S(1)} %pad_clamp_fusion), kind=kCustom, calls=%fused_computation.3 | custom fusion | bytes 16778240 | tf_op jit(solution)/shard_map/gather | solution.py:186
  45.5 93.1 %all-to-all-done.1 = bf16[128,2,16,1024]{3,2,1,0:T(8,128)(2,1)} async-done(((bf16[128,2,16,1024]{3,2,1,0:T(8,128)(2,1)}), bf16[128,2,16,1024]{3,2,1,0:T(8,128)(2,1)}, u32[]{:S(2)}, u32[]{:S(2)}) %all-to-all-start.1) | async-done | bytes 8388640 | tf_op jit(solution)/shard_map/all_to_all | solution.py:182
  138.7 11.0 %all-to-all-start.2 = ((bf16[128,2,16,1024]{3,2,1,0:T(8,128)(2,1)}), bf16[128,2,16,1024]{3,2,1,0:T(8,128)(2,1)}, u32[]{:S(2)}, u32[]{:S(2)}) async-start(bf16[128,2,16,1024]{3,2,1,0:T(8,128)(2,1)} %bitcast.42), calls=%async_computation.2 | async-start | bytes 16777216 | tf_op jit(solution)/shard_map/all_to_all | solution.py:185
  149.6 0.2 copy.43
  150.0 0.7 copy-done.5
  150.7 0.2 copy.38
  150.9 0.1 convert.10
  151.1 0.4 convolution_minimum_fusion.5
  151.4 0.3 convolution_minimum_fusion.4
  151.7 0.3 convolution_minimum_fusion.3
  152.0 0.3 convolution_minimum_fusion.2
  152.2 0.3 convolution_minimum_fusion.1
  152.5 0.4 fusion.89
  152.8 0.2 broadcast_multiply_fusion
  153.0 1.1 mul.182.tmask_ref
  154.3 0.2 fusion.53
  154.5 1.1 convolution_convert_fusion.1
  155.6 0.5 broadcast.242
  156.1 0.8 reduce.7
  157.0 0.2 slice_reduce_fusion.1
  157.2 0.1 select_reduce_fusion.2
  157.5 0.2 multiply_cosine_fusion
  157.7 0.2 multiply_subtract_fusion
  157.9 0.4 reshape.305
  158.3 1.0 copy.45.kd_ref
  159.3 0.1 subtract_convert_fusion
  159.5 1.0 copy.44.q_ref
  160.6 0.1 fusion.41
  160.7 0.7 select_n.59.kown_ref
  161.4 1.3 convolution_convert_fusion
  162.7 33.8 %shard_map.175 = (bf16[8,2,256,4096]{3,2,1,0:T(8,128)(2,1)}, bf16[8,2,256,256]{3,2,1,0:T(8,128)(2,1)}) custom-call(bf16[256,1024]{1,0:T(8,128)(2,1)} %copy.44.q_ref, bf16[256,16,1024]{2,1,0:T(8,128)(2,1)} %bitcast.10.kc_ref, bf16[256,1024]{1,0:T(8,128)(2,1)} %copy.45.kd_ref, s32[1,4096]{1,0:T(1,128)} %select_n.59.kown_ref, f32[256,256]{1,0:T(8,128)} %mul.182.tmask_ref), custom_call_target="tpu_custom_call" | custom-call | tf_op jit(solution)/shard_map/pallas_call | solution.py:95
  196.5 56.2 %all-to-all-done.2 = bf16[128,2,16,1024]{3,2,1,0:T(8,128)(2,1)} async-done(((bf16[128,2,16,1024]{3,2,1,0:T(8,128)(2,1)}), bf16[128,2,16,1024]{3,2,1,0:T(8,128)(2,1)}, u32[]{:S(2)}, u32[]{:S(2)}) %all-to-all-start.2) | async-done | bytes 8388640 | tf_op jit(solution)/shard_map/all_to_all | solution.py:185
  252.6 18.6 %shard_map.176 = bf16[256,1024]{1,0:T(8,128)(2,1)} custom-call(bf16[8,2,256,4096]{3,2,1,0:T(8,128)(2,1)} %get-tuple-element.5.pc_ref, bf16[8,2,256,256]{3,2,1,0:T(8,128)(2,1)} %get-tuple-element.6.pd_ref, bf16[256,16,1024]{2,1,0:T(8,128)(2,1)} %bitcast.15.vc_ref, bf16[256,1024]{1,0:T(8,128)(2,1)} %vd_ref.1), custom_call_target="tpu_custom_call" | custom-call | tf_op jit(solution)/shard_map/pallas_call | solution.py:117
  271.2 2.0 convert_reduce_fusion
  273.2 0.3 fusion.30
  273.5 6.5 %fusion.34 = f32[256,5248]{1,0:T(8,128)S(1)} fusion(bf16[1024,5248]{1,0:T(8,128)(2,1)} %param.30, bf16[256,1024]{1,0:T(8,128)(2,1)S(1)} %get-tuple-element.18, f32[1024]{0:T(1024)S(1)} %convert_element_type.114, f32[256]{0:T(256)S(1)} %add_rsqrt_fusion, f32[256]{0:T(256)S(1)} %broadcast_multiply_fusion.1), kind=kOutput, calls=%fused_computation.49 | convolution fusion | flops 2752774144 | bytes 16652288 | tf_op jit(solution)/shard_map/dot_general | solution.py:141
  280.1 8.3 %fusion.27 = bf16[256,1024]{1,0:T(8,128)(2,1)} fusion(bf16[2624,1024]{1,0:T(8,128)(2,1)S(1)} %bitcast.60, f32[256,5248]{1,0:T(8,128)S(1)} %fusion.34, bf16[256,1024]{1,0:T(8,128)(2,1)S(1)} %get-tuple-element.18, pred[256]{0:T(512)(128)(4,1)S(1)} %lt.59), kind=kOutput, calls=%fused_computation.37 | convolution fusion | flops 1421639680 | bytes 11928064 | tf_op jit(solution)/shard_map/dot_general | solution.py:145
  (52 shorter events, 1.0 us)
Async XLA Ops:
  0.6 17.9 %copy-start = (bf16[96,16,1024]{2,1,0:T(8,128)(2,1)S(1)}, bf16[96,16,1024]{2,1,0:T(8,128)(2,1)}, u32[]{:S(2)}) copy-start(bf16[96,16,1024]{2,1,0:T(8,128)(2,1)} %param.20) | copy-start | bytes 9437188
  8.1 18.8 %all-to-all-start = ((s32[128,1,4]{2,1,0:T(1,128)}), s32[128,1,4]{2,1,0:T(1,128)S(1)}, u32[]{:S(2)}, u32[]{:S(2)}) async-start(s32[128,1,4]{2,1,0:T(1,128)} %bitcast.6), calls=%async_computation | async-start | bytes 131072 | tf_op jit(solution)/shard_map/all_to_all | solution.py:188
  26.9 10.2 %copy-start.2 = (bf16[96,16,1024]{2,1,0:T(8,128)(2,1)S(1)}, bf16[96,16,1024]{2,1,0:T(8,128)(2,1)}, u32[]{:S(2)}) copy-start(bf16[96,16,1024]{2,1,0:T(8,128)(2,1)} %param.21) | copy-start | bytes 9437188
  26.9 111.8 %all-to-all-start.1 = ((bf16[128,2,16,1024]{3,2,1,0:T(8,128)(2,1)}), bf16[128,2,16,1024]{3,2,1,0:T(8,128)(2,1)}, u32[]{:S(2)}, u32[]{:S(2)}) async-start(bf16[128,2,16,1024]{3,2,1,0:T(8,128)(2,1)} %bitcast.43), calls=%async_computation.1 | async-start | bytes 16777216 | tf_op jit(solution)/shard_map/all_to_all | solution.py:182
  138.7 11.0 %copy-start.4 = (bf16[256,1024]{1,0:T(8,128)(2,1)S(1)}, bf16[256,1024]{1,0:T(8,128)(2,1)}, u32[]{:S(2)}) copy-start(bf16[256,1024]{1,0:T(8,128)(2,1)} %param.18) | copy-start | bytes 1572868
  138.7 114.0 %all-to-all-start.2 = ((bf16[128,2,16,1024]{3,2,1,0:T(8,128)(2,1)}), bf16[128,2,16,1024]{3,2,1,0:T(8,128)(2,1)}, u32[]{:S(2)}, u32[]{:S(2)}) async-start(bf16[128,2,16,1024]{3,2,1,0:T(8,128)(2,1)} %bitcast.42), calls=%async_computation.2 | async-start | bytes 16777216 | tf_op jit(solution)/shard_map/all_to_all | solution.py:185
  149.6 1.0 copy-start.5
  149.6 1.4 copy-start.7
  150.9 3.2 %copy-start.6 = (bf16[1024]{0:T(1024)(128)(2,1)S(1)}, bf16[1024]{0:T(1024)(128)(2,1)}, u32[]{:S(2)}) copy-start(bf16[1024]{0:T(1024)(128)(2,1)} %param.29) | copy-start | bytes 6148
  150.9 3.2 %copy-start.10 = (s32[4]{0:T(128)S(1)}, s32[4]{0:T(128)}, u32[]{:S(2)}) copy-start(s32[4]{0:T(128)} %param.26) | copy-start | bytes 52
  150.9 3.3 %copy-start.11 = (s32[4]{0:T(128)S(1)}, s32[4]{0:T(128)}, u32[]{:S(2)}) copy-start(s32[4]{0:T(128)} %param.27) | copy-start | bytes 52
  150.9 3.6 %copy-start.3 = (bf16[256,1024]{1,0:T(8,128)(2,1)S(1)}, bf16[256,1024]{1,0:T(8,128)(2,1)}, u32[]{:S(2)}) copy-start(bf16[256,1024]{1,0:T(8,128)(2,1)} %vd_ref.1) | copy-start | bytes 1572868
  252.6 18.6 %copy-start.8 = (bf16[1024,1024]{1,0:T(8,128)(2,1)S(1)}, bf16[1024,1024]{1,0:T(8,128)(2,1)}, u32[]{:S(2)}) copy-start(bf16[1024,1024]{1,0:T(8,128)(2,1)} %param.28) | copy-start | bytes 6291460
  252.6 18.6 %copy-start.9 = (bf16[256,1024]{1,0:T(8,128)(2,1)S(1)}, bf16[256,1024]{1,0:T(8,128)(2,1)}, u32[]{:S(2)}) copy-start(bf16[256,1024]{1,0:T(8,128)(2,1)} %param.16) | copy-start | bytes 1572868
  271.2 8.9 %slice-start = ((s8[5373952]{0:T(1024)(128)(4,1)}), s8[4194304]{0:T(1024)(128)(4,1)S(1)}, s32[]{:S(2)}) async-start(s8[5373952]{0:T(1024)(128)(4,1)} %bitcast.59), calls=%async_computation.3 | async-start | bytes 8388608
  273.5 6.6 %slice-start.1 = ((s8[5373952]{0:T(1024)(128)(4,1)}), s8[1179648]{0:T(1024)(128)(4,1)S(1)}, s32[]{:S(2)}) async-start(s8[5373952]{0:T(1024)(128)(4,1)} %bitcast.59), calls=%async_computation.4 | async-start | bytes 2359296
  280.1 8.3 %copy-start.1 = (bf16[96,16,1024]{2,1,0:T(8,128)(2,1)S(1)}, bf16[96,16,1024]{2,1,0:T(8,128)(2,1)}, u32[]{:S(2)}) copy-start(bf16[96,16,1024]{2,1,0:T(8,128)(2,1)} %param.20) | copy-start | bytes 9437188

commit v2 on v1

--- a/solution.py
+++ b/solution.py
@@ -176,18 +176,20 @@
     source = jnp.sum(
         jnp.where(matches, jnp.arange(pages_here, dtype=jnp.int32)[None, :], 0), axis=1
     )
-    send_meta = jnp.stack(
-        [jnp.where(filled, page_fill[source], 0), page_slot[source]], axis=1
-    ).reshape(devices, per_target * 2)
     recv_k = lax.all_to_all(
         cache_keys[source].reshape(devices, per_target, page_len, width), "req", 0, 0, tiled=True
     ).reshape(slot_count, page_len, width)
     recv_v = lax.all_to_all(
         cache_values[source].reshape(devices, per_target, page_len, width), "req", 0, 0, tiled=True
     ).reshape(slot_count, page_len, width)
-    recv_meta = lax.all_to_all(send_meta, "req", 0, 0, tiled=True).reshape(slot_count, 2)
-    recv_fill = recv_meta[:, 0]
-    recv_owner = recv_meta[:, 1]
+    table = lax.all_gather(
+        jnp.stack([target, page_slot, page_fill], axis=0), "req", axis=0, tiled=False
+    )
+    mine = table[:, 0, :] == lax.axis_index("req")
+    rank = jnp.cumsum(mine.astype(jnp.int32), axis=1) - 1
+    hit = mine[:, None, :] & (rank[:, None, :] == jnp.arange(per_target, dtype=jnp.int32)[None, :, None])
+    recv_fill = jnp.sum(jnp.where(hit, table[:, None, 2, :], 0), axis=2).reshape(slot_count)
+    recv_owner = jnp.sum(jnp.where(hit, table[:, None, 1, :], 0), axis=2).reshape(slot_count)
     requests, tree_width = tree_parent.shape
     rows = requests * tree_width
     ancestors = ancestor_closure(tree_parent)

time: 290 us -> 349 us (1.20)
  blocking collectives: 0 us -> 128 us
  waiting for transfers between devices: 149 us -> 93.1 us
  starting transfers between devices: 31.6 us -> 21.8 us
  local copies, waits for them, and re-layouts: 27.8 us -> 22.5 us
    all_gather x0 -> x1, blocking collectives: none -> 128 us  [local(): lax.all_gather(jnp.stack([target, page_slot, page_fill], axis=0), 'req',...]
    all_to_all x1, waiting for transfers between devices: 56.2 us -> 0.01 us  [local(): lax.all_to_all(cache_values[source].reshape(devices, per_target, page_len...]
    all_to_all x1 -> x0, starting transfers between devices: 10.4 us -> none  [local(): lax.all_to_all(send_meta, 'req', 0, 0, tiled=True).reshape(slot_count, 2)]
    gather x2 -> x0, local copies, waits for them, and re-layouts: 3.79 us -> none  [the longest x1 1.9 us: local(): page_slot[source]]
  transfers between devices with their start and end apart: 3 -> 2, of which waited for: 2 -> 1; matrix products, arithmetic and copies ran while one was open for 10% -> 6% of each run, Pallas kernels for 12% -> 10%
where the time goes in v2:
time: 349 us; the launch traced here: 345 us
  blocking collectives  128 us (37%)
  waiting for transfers between devices  93.1 us (27%)
  Pallas kernels  52.2 us (15%)
  local copies, waits for them, and re-layouts  22.5 us (6%)
  starting transfers between devices  21.8 us (6%)
  matrix products  21.6 us (6%)
  other arithmetic  4.59 us (1%)
    all_gather x1, blocking collectives, local(): lax.all_gather(jnp.stack([target, page_slot, page_fill], axis=0), 'req',...  128 us
    all_to_all x1, waiting for transfers between devices, local(): lax.all_to_all(cache_keys[source].reshape(devices, per_target, page_len,...  93.1 us
    pallas_call x1, Pallas kernels, attend(): pl.pallas_call(functools.partial(_probs_kernel, tree_width=tree_width, he...  33.8 us
    pallas_call x1, Pallas kernels, attend(): pl.pallas_call(functools.partial(_context_kernel, head_size=head_size), g...  18.4 us
    all_to_all x1, starting transfers between devices, local(): lax.all_to_all(cache_values[source].reshape(devices, per_target, page_len...  10.9 us
    all_to_all x1, starting transfers between devices, local(): lax.all_to_all(cache_keys[source].reshape(devices, per_target, page_len,...  10.9 us
    gather x1, local copies, waits for them, and re-layouts, local(): cache_values[source].reshape(devices, per_target, page_len, width)  8.4 us
    gather x1, local copies, waits for them, and re-layouts, local(): cache_keys[source].reshape(devices, per_target, page_len, width)  8.4 us
  transfers between devices with their start and end apart: 2, of which 1 were waited for; matrix products, arithmetic and copies ran while one was open for 6% of the time, Pallas kernels for 10%

profile of v2, /device:TPU:12, one launch (start us, length us, event | category | flops | bytes accessed | tf_op | source)
XLA Modules:
  0.0 345.3 jit_solution(2937012899461305893)
XLA Ops:
  0.6 0.9 fusion.51
  1.5 0.1 reduce_window_sum.26
  1.7 0.8 select_reduce_fusion.3
  2.5 0.7 add_add_fusion
  3.2 0.1 select_reduce_fusion
  3.3 8.4 %gather_fusion = bf16[256,16,1024]{2,1,0:T(8,128)(2,1)} fusion(bf16[96,16,1024]{2,1,0:T(8,128)(2,1)S(1)} %copy-done, s32[1024]{0:T(1024)S(1)} %pad_clamp_fusion), kind=kCustom, calls=%fused_computation | custom fusion | bytes 16778240 | tf_op jit(solution)/shard_map/gather | solution.py:180
  11.7 10.9 %all-to-all-start = ((bf16[128,2,16,1024]{3,2,1,0:T(8,128)(2,1)}), bf16[128,2,16,1024]{3,2,1,0:T(8,128)(2,1)}, u32[]{:S(2)}, u32[]{:S(2)}) async-start(bf16[128,2,16,1024]{3,2,1,0:T(8,128)(2,1)} %bitcast.50), calls=%async_computation | async-start | bytes 16777216 | tf_op jit(solution)/shard_map/all_to_all | solution.py:179
  22.6 8.4 %gather_fusion.1 = bf16[256,16,1024]{2,1,0:T(8,128)(2,1)} fusion(bf16[96,16,1024]{2,1,0:T(8,128)(2,1)S(1)} %copy-done.2, s32[1024]{0:T(1024)S(1)} %pad_clamp_fusion), kind=kCustom, calls=%fused_computation.1 | custom fusion | bytes 16778240 | tf_op jit(solution)/shard_map/gather | solution.py:183
  31.0 93.1 %all-to-all-done = bf16[128,2,16,1024]{3,2,1,0:T(8,128)(2,1)} async-done(((bf16[128,2,16,1024]{3,2,1,0:T(8,128)(2,1)}), bf16[128,2,16,1024]{3,2,1,0:T(8,128)(2,1)}, u32[]{:S(2)}, u32[]{:S(2)}) %all-to-all-start) | async-done | bytes 8388640 | tf_op jit(solution)/shard_map/all_to_all | solution.py:179
  124.1 10.9 %all-to-all-start.1 = ((bf16[128,2,16,1024]{3,2,1,0:T(8,128)(2,1)}), bf16[128,2,16,1024]{3,2,1,0:T(8,128)(2,1)}, u32[]{:S(2)}, u32[]{:S(2)}) async-start(bf16[128,2,16,1024]{3,2,1,0:T(8,128)(2,1)} %bitcast.49), calls=%async_computation.1 | async-start | bytes 16777216 | tf_op jit(solution)/shard_map/all_to_all | solution.py:182
  135.1 128.4 %all-gather.1 = s32[128,3,96]{2,1,0:T(4,128)S(1)} all-gather(s32[1,3,96]{2,1,0:T(4,128)S(1)} %add_bitcast_fusion), channel_id=2, replica_groups=mesh['req'=128] {'req'}, dimensions={0}, use_global_device_ids=true | all-gather | bytes 148608 | tf_op jit(solution)/shard_map/all_gather | solution.py:185
  263.6 0.1 fusion.90
  263.8 0.1 reduce_window_sum.25
  264.2 0.1 copy.48
  264.3 0.1 broadcast_in_dim.113
  264.4 0.1 copy.46
  264.6 0.1 eq.118
  264.7 0.1 select_reduce_fusion.4
  264.8 0.4 convolution_minimum_fusion.5
  265.2 0.3 convolution_minimum_fusion.4
  265.5 0.3 convolution_minimum_fusion.3
  265.7 0.3 convolution_minimum_fusion.2
  266.0 0.3 convolution_minimum_fusion.1
  266.3 0.4 fusion.91
  266.8 0.2 copy.51
  267.0 0.1 convert.12
  267.1 0.2 multiply_cosine_fusion
  267.3 0.2 multiply_subtract_fusion
  267.5 0.4 reshape.280
  267.9 1.0 copy.53.kd_ref
  269.0 0.2 copy.43
  269.2 0.1 convert.11
  269.3 0.2 subtract_convert_fusion
  269.5 1.0 copy.52.q_ref
  270.5 0.1 fusion.41
  270.7 0.7 select_n.50.kown_ref
  271.4 0.2 broadcast_multiply_fusion
  271.5 1.1 mul.182.tmask_ref
  272.7 0.1 lt.57
  272.9 0.2 fusion.53
  273.0 1.1 convolution_convert_fusion.1
  274.1 1.3 convolution_convert_fusion
  275.4 33.8 %shard_map.175 = (bf16[8,2,256,4096]{3,2,1,0:T(8,128)(2,1)}, bf16[8,2,256,256]{3,2,1,0:T(8,128)(2,1)}) custom-call(bf16[256,1024]{1,0:T(8,128)(2,1)} %copy.52.q_ref, bf16[256,16,1024]{2,1,0:T(8,128)(2,1)} %bitcast.14.kc_ref, bf16[256,1024]{1,0:T(8,128)(2,1)} %copy.53.kd_ref, s32[1,4096]{1,0:T(1,128)} %select_n.50.kown_ref, f32[256,256]{1,0:T(8,128)} %mul.182.tmask_ref), custom_call_target="tpu_custom_call" | custom-call | tf_op jit(solution)/shard_map/pallas_call | solution.py:95
  309.2 18.4 %shard_map.176 = bf16[256,1024]{1,0:T(8,128)(2,1)} custom-call(bf16[8,2,256,4096]{3,2,1,0:T(8,128)(2,1)} %get-tuple-element.5.pc_ref, bf16[8,2,256,256]{3,2,1,0:T(8,128)(2,1)} %get-tuple-element.6.pd_ref, bf16[256,16,1024]{2,1,0:T(8,128)(2,1)} %bitcast.19.vc_ref, bf16[256,1024]{1,0:T(8,128)(2,1)} %vd_ref.1), custom_call_target="tpu_custom_call" | custom-call | tf_op jit(solution)/shard_map/pallas_call | solution.py:117
  327.7 2.7 convert_reduce_fusion
  330.4 0.3 fusion.30
  330.7 6.3 %fusion.34 = f32[256,5248]{1,0:T(8,128)S(1)} fusion(bf16[1024,5248]{1,0:T(8,128)(2,1)} %param.30, bf16[256,1024]{1,0:T(8,128)(2,1)S(1)} %get-tuple-element.23, f32[1024]{0:T(1024)S(1)} %convert_element_type.116, f32[256]{0:T(256)S(1)} %add_rsqrt_fusion, f32[256]{0:T(256)S(1)} %broadcast_multiply_fusion.1), kind=kOutput, calls=%fused_computation.47 | convolution fusion | flops 2752774144 | bytes 16652288 | tf_op jit(solution)/shard_map/dot_general | solution.py:141
  337.0 8.3 %fusion.27 = bf16[256,1024]{1,0:T(8,128)(2,1)} fusion(bf16[2624,1024]{1,0:T(8,128)(2,1)S(1)} %bitcast.70, f32[256,5248]{1,0:T(8,128)S(1)} %fusion.34, bf16[256,1024]{1,0:T(8,128)(2,1)S(1)} %get-tuple-element.23, pred[256]{0:T(512)(128)(4,1)S(1)} %lt.57), kind=kOutput, calls=%fused_computation.35 | convolution fusion | flops 1421639680 | bytes 11928064 | tf_op jit(solution)/shard_map/dot_general | solution.py:145
  (57 shorter events, 0.8 us)
Async XLA Ops:
  0.6 2.7 copy-start
  11.7 10.9 %copy-start.2 = (bf16[96,16,1024]{2,1,0:T(8,128)(2,1)S(1)}, bf16[96,16,1024]{2,1,0:T(8,128)(2,1)}, u32[]{:S(2)}) copy-start(bf16[96,16,1024]{2,1,0:T(8,128)(2,1)} %param.21) | copy-start | bytes 9437188
  11.7 112.4 %all-to-all-start = ((bf16[128,2,16,1024]{3,2,1,0:T(8,128)(2,1)}), bf16[128,2,16,1024]{3,2,1,0:T(8,128)(2,1)}, u32[]{:S(2)}, u32[]{:S(2)}) async-start(bf16[128,2,16,1024]{3,2,1,0:T(8,128)(2,1)} %bitcast.50), calls=%async_computation | async-start | bytes 16777216 | tf_op jit(solution)/shard_map/all_to_all | solution.py:179
  124.1 11.0 %copy-start.6 = (s32[96,1]{0,1:T(1,128)S(1)}, s32[96,1]{0,1:T(1,128)}, u32[]{:S(2)}) copy-start(s32[96,1]{0,1:T(1,128)} %param.22) | copy-start | bytes 1156
  124.1 11.0 %copy-start.9 = (s32[96]{0:T(128)S(1)}, s32[96]{0:T(128)}, u32[]{:S(2)}) copy-start(s32[96]{0:T(128)} %param.24) | copy-start | bytes 1156
  124.1 11.0 %copy-start.10 = (s32[96]{0:T(128)S(1)}, s32[96]{0:T(128)}, u32[]{:S(2)}) copy-start(s32[96]{0:T(128)} %param.23) | copy-start | bytes 1156
  124.1 140.7 %copy-start.8 = (s32[4,64]{1,0:T(4,128)S(1)}, s32[4,64]{1,0:T(4,128)}, u32[]{:S(2)}) copy-start(s32[4,64]{1,0:T(4,128)} %param.25) | copy-start | bytes 3076
  124.1 185.1 %all-to-all-start.1 = ((bf16[128,2,16,1024]{3,2,1,0:T(8,128)(2,1)}), bf16[128,2,16,1024]{3,2,1,0:T(8,128)(2,1)}, u32[]{:S(2)}, u32[]{:S(2)}) async-start(bf16[128,2,16,1024]{3,2,1,0:T(8,128)(2,1)} %bitcast.49), calls=%async_computation.1 | async-start | bytes 16777216 | tf_op jit(solution)/shard_map/all_to_all | solution.py:182
  135.1 131.7 %copy-start.4 = (bf16[256,1024]{1,0:T(8,128)(2,1)S(1)}, bf16[256,1024]{1,0:T(8,128)(2,1)}, u32[]{:S(2)}) copy-start(bf16[256,1024]{1,0:T(8,128)(2,1)} %param.18) | copy-start | bytes 1572868
  267.1 1.9 copy-start.5
  269.3 3.3 copy-start.7
  269.3 3.3 copy-start.12
  269.3 3.5 %copy-start.13 = (s32[4]{0:T(128)S(1)}, s32[4]{0:T(128)}, u32[]{:S(2)}) copy-start(s32[4]{0:T(128)} %param.27) | copy-start | bytes 52
  269.3 3.7 %copy-start.3 = (bf16[256,1024]{1,0:T(8,128)(2,1)S(1)}, bf16[256,1024]{1,0:T(8,128)(2,1)}, u32[]{:S(2)}) copy-start(bf16[256,1024]{1,0:T(8,128)(2,1)} %vd_ref.1) | copy-start | bytes 1572868
  309.2 18.5 %copy-start.11 = (bf16[256,1024]{1,0:T(8,128)(2,1)S(1)}, bf16[256,1024]{1,0:T(8,128)(2,1)}, u32[]{:S(2)}) copy-start(bf16[256,1024]{1,0:T(8,128)(2,1)} %param.16) | copy-start | bytes 1572868
  327.6 9.3 %slice-start = ((s8[5373952]{0:T(1024)(128)(4,1)}), s8[4194304]{0:T(1024)(128)(4,1)S(1)}, s32[]{:S(2)}) async-start(s8[5373952]{0:T(1024)(128)(4,1)} %bitcast.69), calls=%async_computation.2 | async-start | bytes 8388608
  330.7 6.3 %slice-start.1 = ((s8[5373952]{0:T(1024)(128)(4,1)}), s8[1179648]{0:T(1024)(128)(4,1)S(1)}, s32[]{:S(2)}) async-start(s8[5373952]{0:T(1024)(128)(4,1)} %bitcast.69), calls=%async_computation.3 | async-start | bytes 2359296
  337.0 8.3 %copy-start.1 = (bf16[96,16,1024]{2,1,0:T(8,128)(2,1)S(1)}, bf16[96,16,1024]{2,1,0:T(8,128)(2,1)}, u32[]{:S(2)}) copy-start(bf16[96,16,1024]{2,1,0:T(8,128)(2,1)} %param.20) | copy-start | bytes 9437188

commit v3 on v1

--- a/solution.py
+++ b/solution.py
@@ -89,8 +89,10 @@
     lanes = 128
     per = lanes // head_size
     groups = width // lanes
-    slots, page_len, _ = recv_k.shape
+    slots, page_len, _ = recv_v.shape
     keys = slots * page_len
+    sources = recv_k.shape[0]
+    block_rows = keys // sources
     params = pltpu.CompilerParams(vmem_limit_bytes=60 * 1024 * 1024)
     probs_c, probs_d = pl.pallas_call(
         functools.partial(
@@ -99,7 +101,7 @@
         grid=(groups,),
         in_specs=[
             pl.BlockSpec((rows, lanes), lambda h: (0, h)),
-            pl.BlockSpec((slots, page_len, lanes), lambda h: (0, 0, h)),
+            pl.BlockSpec((sources, block_rows, lanes), lambda h: (0, 0, h)),
             pl.BlockSpec((rows, lanes), lambda h: (0, h)),
             pl.BlockSpec((1, keys), lambda h: (0, 0)),
             pl.BlockSpec((rows, rows), lambda h: (0, 0)),
@@ -176,16 +178,32 @@
     source = jnp.sum(
         jnp.where(matches, jnp.arange(pages_here, dtype=jnp.int32)[None, :], 0), axis=1
     )
-    send_meta = jnp.stack(
-        [jnp.where(filled, page_fill[source], 0), page_slot[source]], axis=1
-    ).reshape(devices, per_target * 2)
-    recv_k = lax.all_to_all(
-        cache_keys[source].reshape(devices, per_target, page_len, width), "req", 0, 0, tiled=True
-    ).reshape(slot_count, page_len, width)
+    send_fill = jnp.sum(jnp.where(matches, page_fill[None, :], 0), axis=1)
+    send_owner = jnp.sum(jnp.where(matches, page_slot[None, :], 0), axis=1)
+    meta_row = jnp.concatenate(
+        [
+            jnp.stack([send_fill, send_owner], axis=1).reshape(devices, 2 * per_target),
+            jnp.zeros((devices, width - 2 * per_target), jnp.int32),
+        ],
+        axis=1,
+    ).astype(jnp.bfloat16)
+    table = jnp.concatenate([cache_keys.reshape(pages_here * page_len, width), meta_row], axis=0)
+    row_ids = jnp.concatenate(
+        [
+            (source[:, None] * page_len + jnp.arange(page_len, dtype=jnp.int32)[None, :]).reshape(
+                devices, per_target * page_len
+            ),
+            pages_here * page_len + jnp.arange(devices, dtype=jnp.int32)[:, None],
+        ],
+        axis=1,
+    )
+    send_k = table[row_ids]
+    recv_k = lax.all_to_all(send_k, "req", 0, 0, tiled=True)
     recv_v = lax.all_to_all(
         cache_values[source].reshape(devices, per_target, page_len, width), "req", 0, 0, tiled=True
     ).reshape(slot_count, page_len, width)
-    recv_meta = lax.all_to_all(send_meta, "req", 0, 0, tiled=True).reshape(slot_count, 2)
+    recv_meta = recv_k[:, per_target * page_len, : 2 * per_target].astype(jnp.int32)
+    recv_meta = recv_meta.reshape(slot_count, 2)
     recv_fill = recv_meta[:, 0]
     recv_owner = recv_meta[:, 1]
     requests, tree_width = tree_parent.shape

time: 290 us -> 344 us (1.19)
  waiting for transfers between devices: 149 us -> 181 us
  local copies, waits for them, and re-layouts: 27.8 us -> 50.5 us
  starting transfers between devices: 31.6 us -> 25.5 us
  other arithmetic: 5.3 us -> 10.3 us
    all_to_all x2 -> x1, waiting for transfers between devices: 93.1 us -> 123 us  [local(): recv_k = lax.all_to_all(send_k, 'req', 0, 0, tiled=True)]
    gather x3 -> x2, local copies, waits for them, and re-layouts: 12.2 us -> 35.3 us  [local(): send_k = table[row_ids]]
    all_to_all x2 -> x1, starting transfers between devices: 20.6 us -> 10.8 us  [local(): recv_k = lax.all_to_all(send_k, 'req', 0, 0, tiled=True)]
    concatenate x0 -> x2, other arithmetic: none -> 3.97 us  [the longest x1 3.97 us: local(): jnp.concatenate([cache_keys.reshape(pages_here * page_len, width), meta_r...]
    all_to_all x1, starting transfers between devices: 11 us -> 14.7 us  [local(): lax.all_to_all(cache_values[source].reshape(devices, per_target, page_len...]
  transfers between devices with their start and end apart: 3 -> 2, of which waited for: 2 -> 2; matrix products, arithmetic and copies ran while one was open for 10% -> 6% of each run, Pallas kernels for 12% -> 10%
where the time goes in v3:
time: 344 us; the launch traced here: 341 us
  waiting for transfers between devices  181 us (53%)
  Pallas kernels  51.9 us (15%)
  local copies, waits for them, and re-layouts  50.5 us (15%)
  starting transfers between devices  25.5 us (7%)
  matrix products  21.5 us (6%)
  other arithmetic  10.3 us (3%)
    all_to_all x1, waiting for transfers between devices, local(): recv_k = lax.all_to_all(send_k, 'req', 0, 0, tiled=True)  123 us
    all_to_all x1, waiting for transfers between devices, local(): lax.all_to_all(cache_values[source].reshape(devices, per_target, page_len...  58 us
    gather x2, local copies, waits for them, and re-layouts, local(): send_k = table[row_ids]  35.3 us
    pallas_call x1, Pallas kernels, attend(): pl.pallas_call(functools.partial(_probs_kernel, tree_width=tree_width, he...  33.4 us
    pallas_call x1, Pallas kernels, attend(): pl.pallas_call(functools.partial(_context_kernel, head_size=head_size), g...  18.4 us
    all_to_all x1, starting transfers between devices, local(): lax.all_to_all(cache_values[source].reshape(devices, per_target, page_len...  14.7 us
    all_to_all x1, starting transfers between devices, local(): recv_k = lax.all_to_all(send_k, 'req', 0, 0, tiled=True)  10.8 us
    gather x1, local copies, waits for them, and re-layouts, local(): cache_values[source].reshape(devices, per_target, page_len, width)  8.53 us
  transfers between devices with their start and end apart: 2, of which 2 were waited for; matrix products, arithmetic and copies ran while one was open for 6% of the time, Pallas kernels for 10%

profile of v3, /device:TPU:12, one launch (start us, length us, event | category | flops | bytes accessed | tf_op | source)
XLA Modules:
  0.0 341.4 jit_solution(4819470325920448999)
XLA Ops:
  0.7 0.9 fusion.53
  1.5 0.1 reduce_window_sum.11
  1.7 0.8 select_reduce_fusion.3
  2.5 0.7 add_add_fusion
  3.2 0.8 select_reduce_fusion
  4.0 0.1 copy.34
  4.3 0.1 mul.181
  4.7 0.1 copy.37
  4.8 0.2 reshape.377
  5.0 4.0 %fusion.1 = bf16[1664,1024]{1,0:T(8,128)(2,1)} fusion(bf16[128,4]{1,0:T(8,128)(2,1)S(1)} %reshape.364, bf16[1536,1024]{1,0:T(8,128)(2,1)} %bitcast.49), kind=kLoop, calls=%fused_computation.5 | loop fusion | flops 10223616 | bytes 6554624 | tf_op jit(solution)/shard_map/concatenate | solution.py:190
  9.0 22.0 %gather_fusion = bf16[4224,1024]{1,0:T(8,128)(2,1)} fusion(bf16[1664,1024]{1,0:T(8,128)(2,1)} %fusion.1, s32[5120]{0:T(1024)S(1)} %pad_clamp_fusion), kind=kCustom, calls=%fused_computation | custom fusion | bytes 17318400 | tf_op jit(solution)/shard_map/gather | solution.py:200
  31.0 13.4 %reshape.376 = bf16[128,33,1024]{2,1,0:T(8,128)(2,1)} reshape(bf16[4224,1024]{1,0:T(8,128)(2,1)} %gather_fusion) | data formatting | bytes 17301504 | tf_op jit(solution)/shard_map/gather | solution.py:200
  44.3 10.8 %all-to-all-start = ((bf16[128,33,1024]{2,1,0:T(8,128)(2,1)}), bf16[128,33,1024]{2,1,0:T(8,128)(2,1)}, u32[]{:S(2)}, u32[]{:S(2)}) async-start(bf16[128,33,1024]{2,1,0:T(8,128)(2,1)} %reshape.376), calls=%async_computation | async-start | bytes 20971520 | tf_op jit(solution)/shard_map/all_to_all | solution.py:201
  55.2 8.5 %gather_fusion.1 = bf16[256,16,1024]{2,1,0:T(8,128)(2,1)} fusion(bf16[96,16,1024]{2,1,0:T(8,128)(2,1)S(1)} %copy-done, s32[1024]{0:T(1024)S(1)} %pad_clamp_fusion.1), kind=kCustom, calls=%fused_computation.1 | custom fusion | bytes 16778240 | tf_op jit(solution)/shard_map/gather | solution.py:203
  63.7 122.6 %all-to-all-done.kc_ref = bf16[128,33,1024]{2,1,0:T(8,128)(2,1)} async-done(((bf16[128,33,1024]{2,1,0:T(8,128)(2,1)}), bf16[128,33,1024]{2,1,0:T(8,128)(2,1)}, u32[]{:S(2)}, u32[]{:S(2)}) %all-to-all-start) | async-done | bytes 8650784 | tf_op jit(solution)/shard_map/all_to_all | solution.py:201
  186.3 14.7 %all-to-all-start.1 = ((bf16[128,2,16,1024]{3,2,1,0:T(8,128)(2,1)}), bf16[128,2,16,1024]{3,2,1,0:T(8,128)(2,1)}, u32[]{:S(2)}, u32[]{:S(2)}) async-start(bf16[128,2,16,1024]{3,2,1,0:T(8,128)(2,1)} %bitcast.47), calls=%async_computation.1 | async-start | bytes 16777216 | tf_op jit(solution)/shard_map/all_to_all | solution.py:202
  201.1 0.2 copy.40
  201.4 0.7 copy-done.4
  202.1 0.2 copy.33
  202.5 0.4 convolution_minimum_fusion.5
  202.9 0.3 convolution_minimum_fusion.4
  203.1 0.3 convolution_minimum_fusion.3
  203.4 0.3 convolution_minimum_fusion.2
  203.6 0.3 convolution_minimum_fusion.1
  203.9 0.4 fusion.91
  204.3 0.2 broadcast_multiply_fusion
  204.4 1.0 mul.199.tmask_ref
  205.7 0.2 fusion.55
  205.9 1.1 convolution_convert_fusion.1
  207.0 1.2 fusion.44
  208.2 0.2 slice_reduce_fusion.1
  208.5 0.1 select_reduce_fusion.4
  208.7 0.2 multiply_cosine_fusion
  209.0 0.2 multiply_subtract_fusion
  209.2 0.4 reshape.394
  209.6 1.0 copy.42.kd_ref
  210.6 0.1 subtract_convert_fusion
  210.8 1.0 copy.41.q_ref
  211.8 0.1 fusion.43
  211.9 0.7 select_n.58.kown_ref
  212.6 33.4 %shard_map.175 = (bf16[8,2,256,4096]{3,2,1,0:T(8,128)(2,1)}, bf16[8,2,256,256]{3,2,1,0:T(8,128)(2,1)}) custom-call(bf16[256,1024]{1,0:T(8,128)(2,1)} %copy.41.q_ref, bf16[128,33,1024]{2,1,0:T(8,128)(2,1)} %all-to-all-done.kc_ref, bf16[256,1024]{1,0:T(8,128)(2,1)} %copy.42.kd_ref, s32[1,4096]{1,0:T(1,128)} %select_n.58.kown_ref, f32[256,256]{1,0:T(8,128)} %mul.199.tmask_ref), custom_call_target="tpu_custom_call" | custom-call | tf_op jit(solution)/shard_map/pallas_call | solution.py:97
  246.1 58.0 %all-to-all-done.1 = bf16[128,2,16,1024]{3,2,1,0:T(8,128)(2,1)} async-done(((bf16[128,2,16,1024]{3,2,1,0:T(8,128)(2,1)}), bf16[128,2,16,1024]{3,2,1,0:T(8,128)(2,1)}, u32[]{:S(2)}, u32[]{:S(2)}) %all-to-all-start.1) | async-done | bytes 8388640 | tf_op jit(solution)/shard_map/all_to_all | solution.py:202
  304.0 18.4 %shard_map.176 = bf16[256,1024]{1,0:T(8,128)(2,1)} custom-call(bf16[8,2,256,4096]{3,2,1,0:T(8,128)(2,1)} %get-tuple-element.5.pc_ref, bf16[8,2,256,256]{3,2,1,0:T(8,128)(2,1)} %get-tuple-element.6.pd_ref, bf16[256,16,1024]{2,1,0:T(8,128)(2,1)} %bitcast.15.vc_ref, bf16[256,1024]{1,0:T(8,128)(2,1)} %vd_ref.1), custom_call_target="tpu_custom_call" | custom-call | tf_op jit(solution)/shard_map/pallas_call | solution.py:119
  322.5 2.7 convert_reduce_fusion
  325.2 0.3 fusion.32
  325.5 1.3 convolution_convert_fusion
  326.8 6.3 %fusion.36 = f32[256,5248]{1,0:T(8,128)S(1)} fusion(bf16[1024,5248]{1,0:T(8,128)(2,1)} %param.30, bf16[256,1024]{1,0:T(8,128)(2,1)S(1)} %get-tuple-element.21, f32[1024]{0:T(1024)S(1)} %convert_element_type.124, f32[256]{0:T(256)S(1)} %add_rsqrt_fusion, f32[256]{0:T(256)S(1)} %broadcast_multiply_fusion.1), kind=kOutput, calls=%fused_computation.50 | convolution fusion | flops 2752774144 | bytes 16652288 | tf_op jit(solution)/shard_map/dot_general | solution.py:143
  333.1 8.3 %fusion.29 = bf16[256,1024]{1,0:T(8,128)(2,1)} fusion(bf16[2624,1024]{1,0:T(8,128)(2,1)S(1)} %bitcast.64, f32[256,5248]{1,0:T(8,128)S(1)} %fusion.36, bf16[256,1024]{1,0:T(8,128)(2,1)S(1)} %get-tuple-element.21, pred[256]{0:T(512)(128)(4,1)S(1)} %lt.70), kind=kOutput, calls=%fused_computation.38 | convolution fusion | flops 1421639680 | bytes 11928064 | tf_op jit(solution)/shard_map/dot_general | solution.py:147
  (58 shorter events, 1.3 us)
Async XLA Ops:
  0.6 54.5 %copy-start = (bf16[96,16,1024]{2,1,0:T(8,128)(2,1)S(1)}, bf16[96,16,1024]{2,1,0:T(8,128)(2,1)}, u32[]{:S(2)}) copy-start(bf16[96,16,1024]{2,1,0:T(8,128)(2,1)} %param.21) | copy-start | bytes 9437188
  44.3 142.0 %all-to-all-start = ((bf16[128,33,1024]{2,1,0:T(8,128)(2,1)}), bf16[128,33,1024]{2,1,0:T(8,128)(2,1)}, u32[]{:S(2)}, u32[]{:S(2)}) async-start(bf16[128,33,1024]{2,1,0:T(8,128)(2,1)} %reshape.376), calls=%async_computation | async-start | bytes 20971520 | tf_op jit(solution)/shard_map/all_to_all | solution.py:201
  186.3 14.8 %copy-start.3 = (bf16[256,1024]{1,0:T(8,128)(2,1)S(1)}, bf16[256,1024]{1,0:T(8,128)(2,1)}, u32[]{:S(2)}) copy-start(bf16[256,1024]{1,0:T(8,128)(2,1)} %param.18) | copy-start | bytes 1572868
  186.3 117.7 %all-to-all-start.1 = ((bf16[128,2,16,1024]{3,2,1,0:T(8,128)(2,1)}), bf16[128,2,16,1024]{3,2,1,0:T(8,128)(2,1)}, u32[]{:S(2)}, u32[]{:S(2)}) async-start(bf16[128,2,16,1024]{3,2,1,0:T(8,128)(2,1)} %bitcast.47), calls=%async_computation.1 | async-start | bytes 16777216 | tf_op jit(solution)/shard_map/all_to_all | solution.py:202
  201.0 1.0 copy-start.4
  201.1 1.4 copy-start.6
  202.3 3.2 copy-start.5
  202.3 3.2 copy-start.8
  202.3 3.3 copy-start.9
  202.3 3.6 %copy-start.2 = (bf16[256,1024]{1,0:T(8,128)(2,1)S(1)}, bf16[256,1024]{1,0:T(8,128)(2,1)}, u32[]{:S(2)}) copy-start(bf16[256,1024]{1,0:T(8,128)(2,1)} %vd_ref.1) | copy-start | bytes 1572868
  304.0 18.4 %copy-start.7 = (bf16[256,1024]{1,0:T(8,128)(2,1)S(1)}, bf16[256,1024]{1,0:T(8,128)(2,1)}, u32[]{:S(2)}) copy-start(bf16[256,1024]{1,0:T(8,128)(2,1)} %param.16) | copy-start | bytes 1572868
  322.5 10.6 %slice-start = ((s8[5373952]{0:T(1024)(128)(4,1)}), s8[4194304]{0:T(1024)(128)(4,1)S(1)}, s32[]{:S(2)}) async-start(s8[5373952]{0:T(1024)(128)(4,1)} %bitcast.63), calls=%async_computation.2 | async-start | bytes 8388608
  326.8 6.3 %slice-start.1 = ((s8[5373952]{0:T(1024)(128)(4,1)}), s8[1179648]{0:T(1024)(128)(4,1)S(1)}, s32[]{:S(2)}) async-start(s8[5373952]{0:T(1024)(128)(4,1)} %bitcast.63), calls=%async_computation.3 | async-start | bytes 2359296
  333.1 8.3 %copy-start.1 = (bf16[96,16,1024]{2,1,0:T(8,128)(2,1)S(1)}, bf16[96,16,1024]{2,1,0:T(8,128)(2,1)}, u32[]{:S(2)}) copy-start(bf16[96,16,1024]{2,1,0:T(8,128)(2,1)} %param.21) | copy-start | bytes 9437188

commit v4 on v1

--- a/solution.py
+++ b/solution.py
@@ -176,16 +176,19 @@
     source = jnp.sum(
         jnp.where(matches, jnp.arange(pages_here, dtype=jnp.int32)[None, :], 0), axis=1
     )
-    send_meta = jnp.stack(
-        [jnp.where(filled, page_fill[source], 0), page_slot[source]], axis=1
-    ).reshape(devices, per_target * 2)
+    send_fill = jnp.sum(jnp.where(matches, page_fill[None, :], 0), axis=1)
+    send_owner = jnp.sum(jnp.where(matches, page_slot[None, :], 0), axis=1)
+    send_meta = jnp.stack([send_fill, send_owner], axis=1).reshape(devices, 1, per_target * 2)
+    spread = jnp.zeros((devices, devices, per_target * 2), jnp.int32)
+    spread = lax.dynamic_update_slice_in_dim(spread, send_meta, lax.axis_index("req"), axis=1)
+    recv_meta = lax.psum_scatter(spread, "req", scatter_dimension=0, tiled=True)
+    recv_meta = recv_meta.reshape(slot_count, 2)
     recv_k = lax.all_to_all(
         cache_keys[source].reshape(devices, per_target, page_len, width), "req", 0, 0, tiled=True
     ).reshape(slot_count, page_len, width)
     recv_v = lax.all_to_all(
         cache_values[source].reshape(devices, per_target, page_len, width), "req", 0, 0, tiled=True
     ).reshape(slot_count, page_len, width)
-    recv_meta = lax.all_to_all(send_meta, "req", 0, 0, tiled=True).reshape(slot_count, 2)
     recv_fill = recv_meta[:, 0]
     recv_owner = recv_meta[:, 1]
     requests, tree_width = tree_parent.shape

time: 290 us -> 447 us (1.54)
  waiting for transfers between devices: 149 us -> 295 us
  between operations: 1.03 us -> 14.5 us
  starting transfers between devices: 31.6 us -> 21.8 us
  local copies, waits for them, and re-layouts: 27.8 us -> 34.7 us
    unnamed x0 -> x2, waiting for transfers between devices: none -> 202 us
    all_to_all x1, waiting for transfers between devices: 56.2 us -> 0.01 us  [local(): lax.all_to_all(cache_values[source].reshape(devices, per_target, page_len...]
    dynamic_update_slice x0 -> x1, local copies, waits for them, and re-layouts: none -> 10.9 us  [local(): lax.dynamic_update_slice_in_dim(spread, send_meta, lax.axis_index('req'),...]
    all_to_all x1 -> x0, starting transfers between devices: 10.4 us -> none  [local(): lax.all_to_all(send_meta, 'req', 0, 0, tiled=True).reshape(slot_count, 2)]
  transfers between devices with their start and end apart: 3 -> 3, of which waited for: 2 -> 2; matrix products, arithmetic and copies ran while one was open for 10% -> 7% of each run, Pallas kernels for 12% -> 8%
where the time goes in v4:
time: 447 us; the launch traced here: 444 us
  waiting for transfers between devices  295 us (66%)
  Pallas kernels  52.3 us (12%)
  local copies, waits for them, and re-layouts  34.7 us (8%)
  starting transfers between devices  21.8 us (5%)
  matrix products  21.1 us (5%)
  between operations  14.5 us (3%)
  other arithmetic  5.08 us (1%)
    unnamed x2, waiting for transfers between devices  202 us
    all_to_all x1, waiting for transfers between devices, local(): lax.all_to_all(cache_keys[source].reshape(devices, per_target, page_len,...  93.1 us
    pallas_call x1, Pallas kernels, attend(): pl.pallas_call(functools.partial(_probs_kernel, tree_width=tree_width, he...  33.8 us
    pallas_call x1, Pallas kernels, attend(): pl.pallas_call(functools.partial(_context_kernel, head_size=head_size), g...  18.5 us
    all_to_all x1, starting transfers between devices, local(): lax.all_to_all(cache_values[source].reshape(devices, per_target, page_len...  10.9 us
    dynamic_update_slice x1, local copies, waits for them, and re-layouts, local(): lax.dynamic_update_slice_in_dim(spread, send_meta, lax.axis_index('req'),...  10.9 us
    all_to_all x1, starting transfers between devices, local(): lax.all_to_all(cache_keys[source].reshape(devices, per_target, page_len,...  10.8 us
  transfers between devices with their start and end apart: 3, of which 2 were waited for; matrix products, arithmetic and copies ran while one was open for 7% of the time, Pallas kernels for 8%

profile of v4, /device:TPU:12, one launch (start us, length us, event | category | flops | bytes accessed | tf_op | source)
XLA Modules:
  0.0 444.2 jit_solution(14404368231873932737)
XLA Ops:
  7.2 0.9 fusion.50
  8.1 0.1 reduce_window_sum.11
  8.2 0.8 select_reduce_fusion.3
  9.0 0.7 add_add_fusion
  9.7 0.8 select_reduce_fusion
  10.5 8.4 %gather_fusion = bf16[256,16,1024]{2,1,0:T(8,128)(2,1)} fusion(bf16[96,16,1024]{2,1,0:T(8,128)(2,1)S(1)} %copy-done, s32[1024]{0:T(1024)S(1)} %pad_clamp_fusion), kind=kCustom, calls=%fused_computation | custom fusion | bytes 16778240 | tf_op jit(solution)/shard_map/gather | solution.py:187
  18.9 10.8 %all-to-all-start = ((bf16[128,2,16,1024]{3,2,1,0:T(8,128)(2,1)}), bf16[128,2,16,1024]{3,2,1,0:T(8,128)(2,1)}, u32[]{:S(2)}, u32[]{:S(2)}) async-start(bf16[128,2,16,1024]{3,2,1,0:T(8,128)(2,1)} %bitcast.42), calls=%async_computation | async-start | bytes 16777216 | tf_op jit(solution)/shard_map/all_to_all | solution.py:186
  29.8 8.4 %gather_fusion.1 = bf16[256,16,1024]{2,1,0:T(8,128)(2,1)} fusion(bf16[96,16,1024]{2,1,0:T(8,128)(2,1)S(1)} %copy-done.2, s32[1024]{0:T(1024)S(1)} %pad_clamp_fusion), kind=kCustom, calls=%fused_computation.1 | custom fusion | bytes 16778240 | tf_op jit(solution)/shard_map/gather | solution.py:190
  38.2 93.1 %all-to-all-done = bf16[128,2,16,1024]{3,2,1,0:T(8,128)(2,1)} async-done(((bf16[128,2,16,1024]{3,2,1,0:T(8,128)(2,1)}), bf16[128,2,16,1024]{3,2,1,0:T(8,128)(2,1)}, u32[]{:S(2)}, u32[]{:S(2)}) %all-to-all-start) | async-done | bytes 8388640 | tf_op jit(solution)/shard_map/all_to_all | solution.py:186
  131.3 10.9 %all-to-all-start.1 = ((bf16[128,2,16,1024]{3,2,1,0:T(8,128)(2,1)}), bf16[128,2,16,1024]{3,2,1,0:T(8,128)(2,1)}, u32[]{:S(2)}, u32[]{:S(2)}) async-start(bf16[128,2,16,1024]{3,2,1,0:T(8,128)(2,1)} %bitcast.41), calls=%async_computation.1 | async-start | bytes 16777216 | tf_op jit(solution)/shard_map/all_to_all | solution.py:189
  142.3 0.1 copy.41
  142.5 0.2 reshape.277
  142.7 10.9 %dynamic_update_slice.3 = s32[128,128,4]{1,2,0:T(4,128)S(1)} dynamic-update-slice(s32[128,128,4]{1,2,0:T(4,128)S(1)} %broadcast_in_dim.65, s32[128,1,4]{1,2,0:T(4,128)S(1)} %reshape.277, s32[]{:T(128)} %constant.41.clone.1, s32[]{:T(128)S(6)} %select_n.48, s32[]{:T(128)} %constant.41.clone.1) | dynamic-update-slice | bytes 4100 | tf_op jit(solution)/shard_map/dynamic_update_slice | solution.py:183
  153.7 0.7 copy-done.4
  154.5 0.4 convolution_minimum_fusion.5
  154.9 0.3 convolution_minimum_fusion.4
  155.1 0.3 convolution_minimum_fusion.3
  155.4 0.3 convolution_minimum_fusion.2
  155.7 0.3 convolution_minimum_fusion.1
  155.9 0.4 fusion.88
  156.3 0.2 fusion.52
  156.5 0.2 broadcast_multiply_fusion
  156.7 1.1 convolution_convert_fusion.1
  157.8 0.2 copy.46
  158.0 0.1 convert.11
  158.1 0.2 copy.40
  158.4 0.1 convert.10
  158.5 1.1 mul.182.tmask_ref
  159.6 201.6 %all-reduce.3.cloned.1.call-done = s32[128,128,4]{1,2,0:T(4,128)} async-done(((s32[128,128,4]{1,2,0:T(4,128)}), s32[128,128,4]{1,2,0:T(4,128)}) %all-reduce.3.cloned.1.call-update) | async-done | bytes 262160
  361.3 0.7 constant_dynamic-slice_fusion
  361.9 0.1 copy.43
  362.1 0.2 slice_reduce_fusion.1
  362.4 0.1 select_reduce_fusion.4
  362.6 0.2 multiply_cosine_fusion
  362.8 0.2 multiply_subtract_fusion
  363.1 0.4 reshape.278
  363.5 1.0 copy.48.kd_ref
  364.5 0.1 subtract_convert_fusion
  364.7 1.0 copy.47.q_ref
  365.7 0.1 fusion.41
  365.8 0.7 select_n.53.kown_ref
  366.5 1.3 convolution_convert_fusion
  367.8 33.8 %shard_map.175 = (bf16[8,2,256,4096]{3,2,1,0:T(8,128)(2,1)}, bf16[8,2,256,256]{3,2,1,0:T(8,128)(2,1)}) custom-call(bf16[256,1024]{1,0:T(8,128)(2,1)} %copy.47.q_ref, bf16[256,16,1024]{2,1,0:T(8,128)(2,1)} %bitcast.9.kc_ref, bf16[256,1024]{1,0:T(8,128)(2,1)} %copy.48.kd_ref, s32[1,4096]{1,0:T(1,128)} %select_n.53.kown_ref, f32[256,256]{1,0:T(8,128)} %mul.182.tmask_ref), custom_call_target="tpu_custom_call" | custom-call | tf_op jit(solution)/shard_map/pallas_call | solution.py:95
  401.6 18.5 %shard_map.176 = bf16[256,1024]{1,0:T(8,128)(2,1)} custom-call(bf16[8,2,256,4096]{3,2,1,0:T(8,128)(2,1)} %get-tuple-element.5.pc_ref, bf16[8,2,256,256]{3,2,1,0:T(8,128)(2,1)} %get-tuple-element.6.pd_ref, bf16[256,16,1024]{2,1,0:T(8,128)(2,1)} %bitcast.14.vc_ref, bf16[256,1024]{1,0:T(8,128)(2,1)} %vd_ref.1), custom_call_target="tpu_custom_call" | custom-call | tf_op jit(solution)/shard_map/pallas_call | solution.py:117
  420.2 2.0 convert_reduce_fusion
  422.2 0.3 fusion.30
  422.5 6.5 %fusion.34 = f32[256,5248]{1,0:T(8,128)S(1)} fusion(bf16[1024,5248]{1,0:T(8,128)(2,1)} %param.30, bf16[256,1024]{1,0:T(8,128)(2,1)S(1)} %get-tuple-element.21, f32[1024]{0:T(1024)S(1)} %convert_element_type.114, f32[256]{0:T(256)S(1)} %add_rsqrt_fusion, f32[256]{0:T(256)S(1)} %broadcast_multiply_fusion.1), kind=kOutput, calls=%fused_computation.47 | convolution fusion | flops 2752774144 | bytes 16652288 | tf_op jit(solution)/shard_map/dot_general | solution.py:141
  429.1 8.3 %fusion.27 = bf16[256,1024]{1,0:T(8,128)(2,1)} fusion(bf16[2624,1024]{1,0:T(8,128)(2,1)S(1)} %bitcast.59, f32[256,5248]{1,0:T(8,128)S(1)} %fusion.34, bf16[256,1024]{1,0:T(8,128)(2,1)S(1)} %get-tuple-element.21, pred[256]{0:T(512)(128)(4,1)S(1)} %lt.60), kind=kOutput, calls=%fused_computation.35 | convolution fusion | flops 1421639680 | bytes 11928064 | tf_op jit(solution)/shard_map/dot_general | solution.py:145
  (53 shorter events, 0.8 us)
Async XLA Ops:
  7.2 3.4 copy-start
  18.9 10.9 %copy-start.2 = (bf16[96,16,1024]{2,1,0:T(8,128)(2,1)S(1)}, bf16[96,16,1024]{2,1,0:T(8,128)(2,1)}, u32[]{:S(2)}) copy-start(bf16[96,16,1024]{2,1,0:T(8,128)(2,1)} %param.21) | copy-start | bytes 9437188
  18.9 112.4 %all-to-all-start = ((bf16[128,2,16,1024]{3,2,1,0:T(8,128)(2,1)}), bf16[128,2,16,1024]{3,2,1,0:T(8,128)(2,1)}, u32[]{:S(2)}, u32[]{:S(2)}) async-start(bf16[128,2,16,1024]{3,2,1,0:T(8,128)(2,1)} %bitcast.42), calls=%async_computation | async-start | bytes 16777216 | tf_op jit(solution)/shard_map/all_to_all | solution.py:186
  131.3 23.1 %copy-start.11 = (s32[4]{0:T(128)S(1)}, s32[4]{0:T(128)}, u32[]{:S(2)}) copy-start(s32[4]{0:T(128)} %param.27) | copy-start | bytes 52
  131.3 23.1 %copy-start.12 = (s32[4]{0:T(128)S(1)}, s32[4]{0:T(128)}, u32[]{:S(2)}) copy-start(s32[4]{0:T(128)} %param.26) | copy-start | bytes 52
  131.3 23.2 %copy-start.8 = (s32[4,64]{1,0:T(4,128)S(1)}, s32[4,64]{1,0:T(4,128)}, u32[]{:S(2)}) copy-start(s32[4,64]{1,0:T(4,128)} %param.25) | copy-start | bytes 3076
  131.3 270.3 %all-to-all-start.1 = ((bf16[128,2,16,1024]{3,2,1,0:T(8,128)(2,1)}), bf16[128,2,16,1024]{3,2,1,0:T(8,128)(2,1)}, u32[]{:S(2)}, u32[]{:S(2)}) async-start(bf16[128,2,16,1024]{3,2,1,0:T(8,128)(2,1)} %bitcast.41), calls=%async_computation.1 | async-start | bytes 16777216 | tf_op jit(solution)/shard_map/all_to_all | solution.py:189
  142.3 14.4 %copy-start.3 = (bf16[256,1024]{1,0:T(8,128)(2,1)S(1)}, bf16[256,1024]{1,0:T(8,128)(2,1)}, u32[]{:S(2)}) copy-start(bf16[256,1024]{1,0:T(8,128)(2,1)} %vd_ref.1) | copy-start | bytes 1572868
  142.3 219.0 %all-reduce.3.cloned.1.call-start = ((), (), s32[]{:S(2)}) async-start(), calls=%async_computation.2 | async-start | bytes 524288
  142.5 15.3 %copy-start.5 = (bf16[256,1024]{1,0:T(8,128)(2,1)S(1)}, bf16[256,1024]{1,0:T(8,128)(2,1)}, u32[]{:S(2)}) copy-start(bf16[256,1024]{1,0:T(8,128)(2,1)} %param.18) | copy-start | bytes 1572868
  153.6 0.7 copy-start.4
  155.7 2.5 copy-start.6
  158.0 1.5 copy-start.7
  401.6 18.6 %copy-start.9 = (bf16[1024,1024]{1,0:T(8,128)(2,1)S(1)}, bf16[1024,1024]{1,0:T(8,128)(2,1)}, u32[]{:S(2)}) copy-start(bf16[1024,1024]{1,0:T(8,128)(2,1)} %param.28) | copy-start | bytes 6291460
  401.6 18.6 %copy-start.10 = (bf16[256,1024]{1,0:T(8,128)(2,1)S(1)}, bf16[256,1024]{1,0:T(8,128)(2,1)}, u32[]{:S(2)}) copy-start(bf16[256,1024]{1,0:T(8,128)(2,1)} %param.16) | copy-start | bytes 1572868
  420.2 8.9 %slice-start = ((s8[5373952]{0:T(1024)(128)(4,1)}), s8[4194304]{0:T(1024)(128)(4,1)S(1)}, s32[]{:S(2)}) async-start(s8[5373952]{0:T(1024)(128)(4,1)} %bitcast.58), calls=%async_computation.3 | async-start | bytes 8388608
  422.5 6.6 %slice-start.1 = ((s8[5373952]{0:T(1024)(128)(4,1)}), s8[1179648]{0:T(1024)(128)(4,1)S(1)}, s32[]{:S(2)}) async-start(s8[5373952]{0:T(1024)(128)(4,1)} %bitcast.58), calls=%async_computation.4 | async-start | bytes 2359296
  429.1 8.3 %copy-start.1 = (bf16[96,16,1024]{2,1,0:T(8,128)(2,1)S(1)}, bf16[96,16,1024]{2,1,0:T(8,128)(2,1)}, u32[]{:S(2)}) copy-start(bf16[96,16,1024]{2,1,0:T(8,128)(2,1)} %param.20) | copy-start | bytes 9437188
Sparse Core Ops, SparseCore 0:
  154.5 206.7 all-reduce.2

commit v5 on v1

--- a/solution.py
+++ b/solution.py
@@ -68,7 +68,8 @@
 
 def _context_kernel(pc_ref, pd_ref, vc_ref, vd_ref, o_ref, *, head_size):
     rows, lanes = o_ref.shape
-    vc = vc_ref[...].reshape(-1, lanes)
+    start = pl.multiple_of(pl.program_id(0) * lanes, lanes)
+    vc = vc_ref[:, :, pl.ds(start, lanes)].reshape(-1, lanes)
     vd = vd_ref[...]
     lane = lax.broadcasted_iota(jnp.int32, (1, lanes), 1)
     result = None
@@ -120,7 +121,7 @@
         in_specs=[
             pl.BlockSpec((None, per, rows, keys), lambda h: (h, 0, 0, 0)),
             pl.BlockSpec((None, per, rows, rows), lambda h: (h, 0, 0, 0)),
-            pl.BlockSpec((slots, page_len, lanes), lambda h: (0, 0, h)),
+            pl.BlockSpec((slots, page_len, width), lambda h: (0, 0, 0)),
             pl.BlockSpec((rows, lanes), lambda h: (0, h)),
         ],
         out_specs=pl.BlockSpec((rows, lanes), lambda h: (0, h)),
@@ -176,9 +177,9 @@
     source = jnp.sum(
         jnp.where(matches, jnp.arange(pages_here, dtype=jnp.int32)[None, :], 0), axis=1
     )
-    send_meta = jnp.stack(
-        [jnp.where(filled, page_fill[source], 0), page_slot[source]], axis=1
-    ).reshape(devices, per_target * 2)
+    send_fill = jnp.sum(jnp.where(matches, page_fill[None, :], 0), axis=1)
+    send_owner = jnp.sum(jnp.where(matches, page_slot[None, :], 0), axis=1)
+    send_meta = jnp.stack([send_fill, send_owner], axis=1).reshape(devices, per_target * 2)
     recv_k = lax.all_to_all(
         cache_keys[source].reshape(devices, per_target, page_len, width), "req", 0, 0, tiled=True
     ).reshape(slot_count, page_len, width)

time: 290 us -> 289 us (level)
  local copies, waits for them, and re-layouts: 27.8 us -> 24 us
    gather x2 -> x0, local copies, waits for them, and re-layouts: 3.79 us -> none  [the longest x1 1.9 us: local(): page_slot[source]]
where the time goes in v5:
time: 289 us; the launch traced here: 287 us
  waiting for transfers between devices  149 us (52%)
  Pallas kernels  53.8 us (19%)
  starting transfers between devices  31.6 us (11%)
  local copies, waits for them, and re-layouts  24 us (8%)
  matrix products  21.1 us (7%)
  other arithmetic  5.88 us (2%)
    all_to_all x1, waiting for transfers between devices, local(): lax.all_to_all(cache_keys[source].reshape(devices, per_target, page_len,...  93.1 us
    all_to_all x1, waiting for transfers between devices, local(): lax.all_to_all(cache_values[source].reshape(devices, per_target, page_len...  56.1 us
    pallas_call x1, Pallas kernels, attend(): pl.pallas_call(functools.partial(_probs_kernel, tree_width=tree_width, he...  33.8 us
    pallas_call x1, Pallas kernels, attend(): pl.pallas_call(functools.partial(_context_kernel, head_size=head_size), g...  20.1 us
    all_to_all x1, starting transfers between devices, local(): lax.all_to_all(cache_values[source].reshape(devices, per_target, page_len...  11 us
    all_to_all x1, starting transfers between devices, local(): lax.all_to_all(send_meta, 'req', 0, 0, tiled=True).reshape(slot_count, 2)  10.4 us
    all_to_all x1, starting transfers between devices, local(): lax.all_to_all(cache_keys[source].reshape(devices, per_target, page_len,...  10.2 us
    gather x1, local copies, waits for them, and re-layouts, local(): cache_values[source].reshape(devices, per_target, page_len, width)  8.4 us
  transfers between devices with their start and end apart: 3, of which 2 were waited for; matrix products, arithmetic and copies ran while one was open for 10% of the time, Pallas kernels for 12%

profile of v5, /device:TPU:12, one launch (start us, length us, event | category | flops | bytes accessed | tf_op | source)
XLA Modules:
  0.0 286.7 jit_solution(10043047832844262282)
XLA Ops:
  0.6 0.9 fusion.50
  1.5 0.1 reduce_window_sum.11
  1.7 0.8 select_reduce_fusion.3
  2.5 0.7 add_add_fusion
  3.2 0.8 select_reduce_fusion
  4.0 0.1 copy.39
  4.1 0.7 all_to_all.12
  4.9 10.4 %all-to-all-start = ((s32[128,1,4]{2,1,0:T(1,128)}), s32[128,1,4]{2,1,0:T(1,128)S(1)}, u32[]{:S(2)}, u32[]{:S(2)}) async-start(s32[128,1,4]{2,1,0:T(1,128)} %bitcast.4), calls=%async_computation | async-start | bytes 131072 | tf_op jit(solution)/shard_map/all_to_all | solution.py:189
  15.3 8.4 %gather_fusion = bf16[256,16,1024]{2,1,0:T(8,128)(2,1)} fusion(bf16[96,16,1024]{2,1,0:T(8,128)(2,1)S(1)} %copy-done, s32[1024]{0:T(1024)S(1)} %pad_clamp_fusion), kind=kCustom, calls=%fused_computation | custom fusion | bytes 16778240 | tf_op jit(solution)/shard_map/gather | solution.py:184
  23.7 10.2 %all-to-all-start.1 = ((bf16[128,2,16,1024]{3,2,1,0:T(8,128)(2,1)}), bf16[128,2,16,1024]{3,2,1,0:T(8,128)(2,1)}, u32[]{:S(2)}, u32[]{:S(2)}) async-start(bf16[128,2,16,1024]{3,2,1,0:T(8,128)(2,1)} %bitcast.43), calls=%async_computation.1 | async-start | bytes 16777216 | tf_op jit(solution)/shard_map/all_to_all | solution.py:183
  33.9 8.4 %gather_fusion.1 = bf16[256,16,1024]{2,1,0:T(8,128)(2,1)} fusion(bf16[96,16,1024]{2,1,0:T(8,128)(2,1)S(1)} %copy-done.2, s32[1024]{0:T(1024)S(1)} %pad_clamp_fusion), kind=kCustom, calls=%fused_computation.1 | custom fusion | bytes 16778240 | tf_op jit(solution)/shard_map/gather | solution.py:187
  42.3 93.1 %all-to-all-done.1 = bf16[128,2,16,1024]{3,2,1,0:T(8,128)(2,1)} async-done(((bf16[128,2,16,1024]{3,2,1,0:T(8,128)(2,1)}), bf16[128,2,16,1024]{3,2,1,0:T(8,128)(2,1)}, u32[]{:S(2)}, u32[]{:S(2)}) %all-to-all-start.1) | async-done | bytes 8388640 | tf_op jit(solution)/shard_map/all_to_all | solution.py:183
  135.4 11.0 %all-to-all-start.2 = ((bf16[128,2,16,1024]{3,2,1,0:T(8,128)(2,1)}), bf16[128,2,16,1024]{3,2,1,0:T(8,128)(2,1)}, u32[]{:S(2)}, u32[]{:S(2)}) async-start(bf16[128,2,16,1024]{3,2,1,0:T(8,128)(2,1)} %bitcast.42), calls=%async_computation.2 | async-start | bytes 16777216 | tf_op jit(solution)/shard_map/all_to_all | solution.py:186
  146.4 0.2 copy.43
  146.6 0.1 convert.11
  146.7 0.7 copy-done.5
  147.4 0.2 copy.38
  147.7 0.1 convert.10
  147.9 0.4 convolution_minimum_fusion.5
  148.2 0.3 convolution_minimum_fusion.4
  148.5 0.3 convolution_minimum_fusion.3
  148.7 0.3 convolution_minimum_fusion.2
  149.0 0.3 convolution_minimum_fusion.1
  149.3 0.4 fusion.88
  149.6 0.2 broadcast_multiply_fusion
  149.8 1.1 mul.182.tmask_ref
  151.1 0.2 fusion.52
  151.3 1.1 convolution_convert_fusion.1
  152.4 0.5 broadcast.227
  152.9 0.8 reduce.7
  153.8 0.2 slice_reduce_fusion.1
  154.0 0.1 select_reduce_fusion.4
  154.3 0.2 multiply_cosine_fusion
  154.5 0.2 multiply_subtract_fusion
  154.7 0.4 reshape.278
  155.1 1.0 copy.45.kd_ref
  156.1 0.1 subtract_convert_fusion
  156.3 1.0 copy.44.q_ref
  157.3 0.1 fusion.41
  157.5 0.7 select_n.49.kown_ref
  158.2 1.3 convolution_convert_fusion
  159.5 33.8 %shard_map.175 = (bf16[8,2,256,4096]{3,2,1,0:T(8,128)(2,1)}, bf16[8,2,256,256]{3,2,1,0:T(8,128)(2,1)}) custom-call(bf16[256,1024]{1,0:T(8,128)(2,1)} %copy.44.q_ref, bf16[256,16,1024]{2,1,0:T(8,128)(2,1)} %bitcast.10.kc_ref, bf16[256,1024]{1,0:T(8,128)(2,1)} %copy.45.kd_ref, s32[1,4096]{1,0:T(1,128)} %select_n.49.kown_ref, f32[256,256]{1,0:T(8,128)} %mul.182.tmask_ref), custom_call_target="tpu_custom_call" | custom-call | tf_op jit(solution)/shard_map/pallas_call | solution.py:96
  193.2 56.1 %all-to-all-done.2 = bf16[128,2,16,1024]{3,2,1,0:T(8,128)(2,1)} async-done(((bf16[128,2,16,1024]{3,2,1,0:T(8,128)(2,1)}), bf16[128,2,16,1024]{3,2,1,0:T(8,128)(2,1)}, u32[]{:S(2)}, u32[]{:S(2)}) %all-to-all-start.2) | async-done | bytes 8388640 | tf_op jit(solution)/shard_map/all_to_all | solution.py:186
  249.4 20.1 %shard_map.176 = bf16[256,1024]{1,0:T(8,128)(2,1)} custom-call(bf16[8,2,256,4096]{3,2,1,0:T(8,128)(2,1)} %get-tuple-element.5.pc_ref, bf16[8,2,256,256]{3,2,1,0:T(8,128)(2,1)} %get-tuple-element.6.pd_ref, bf16[256,16,1024]{2,1,0:T(8,128)(2,1)} %bitcast.15.vc_ref, bf16[256,1024]{1,0:T(8,128)(2,1)} %vd_ref.1), custom_call_target="tpu_custom_call" | custom-call | tf_op jit(solution)/shard_map/pallas_call | solution.py:118
  269.5 2.0 convert_reduce_fusion
  271.5 0.3 fusion.30
  271.8 6.5 %fusion.34 = f32[256,5248]{1,0:T(8,128)S(1)} fusion(bf16[1024,5248]{1,0:T(8,128)(2,1)} %param.30, bf16[256,1024]{1,0:T(8,128)(2,1)S(1)} %get-tuple-element.21, f32[1024]{0:T(1024)S(1)} %convert_element_type.114, f32[256]{0:T(256)S(1)} %add_rsqrt_fusion, f32[256]{0:T(256)S(1)} %broadcast_multiply_fusion.1), kind=kOutput, calls=%fused_computation.47 | convolution fusion | flops 2752774144 | bytes 16652288 | tf_op jit(solution)/shard_map/dot_general | solution.py:142
  278.4 8.3 %fusion.27 = bf16[256,1024]{1,0:T(8,128)(2,1)} fusion(bf16[2624,1024]{1,0:T(8,128)(2,1)S(1)} %bitcast.60, f32[256,5248]{1,0:T(8,128)S(1)} %fusion.34, bf16[256,1024]{1,0:T(8,128)(2,1)S(1)} %get-tuple-element.21, pred[256]{0:T(512)(128)(4,1)S(1)} %lt.57), kind=kOutput, calls=%fused_computation.35 | convolution fusion | flops 1421639680 | bytes 11928064 | tf_op jit(solution)/shard_map/dot_general | solution.py:146
  (48 shorter events, 0.7 us)
Async XLA Ops:
  0.6 14.6 %copy-start = (bf16[96,16,1024]{2,1,0:T(8,128)(2,1)S(1)}, bf16[96,16,1024]{2,1,0:T(8,128)(2,1)}, u32[]{:S(2)}) copy-start(bf16[96,16,1024]{2,1,0:T(8,128)(2,1)} %param.20) | copy-start | bytes 9437188
  4.9 18.8 %all-to-all-start = ((s32[128,1,4]{2,1,0:T(1,128)}), s32[128,1,4]{2,1,0:T(1,128)S(1)}, u32[]{:S(2)}, u32[]{:S(2)}) async-start(s32[128,1,4]{2,1,0:T(1,128)} %bitcast.4), calls=%async_computation | async-start | bytes 131072 | tf_op jit(solution)/shard_map/all_to_all | solution.py:189
  23.7 10.2 %copy-start.2 = (bf16[96,16,1024]{2,1,0:T(8,128)(2,1)S(1)}, bf16[96,16,1024]{2,1,0:T(8,128)(2,1)}, u32[]{:S(2)}) copy-start(bf16[96,16,1024]{2,1,0:T(8,128)(2,1)} %param.21) | copy-start | bytes 9437188
  23.7 111.7 %all-to-all-start.1 = ((bf16[128,2,16,1024]{3,2,1,0:T(8,128)(2,1)}), bf16[128,2,16,1024]{3,2,1,0:T(8,128)(2,1)}, u32[]{:S(2)}, u32[]{:S(2)}) async-start(bf16[128,2,16,1024]{3,2,1,0:T(8,128)(2,1)} %bitcast.43), calls=%async_computation.1 | async-start | bytes 16777216 | tf_op jit(solution)/shard_map/all_to_all | solution.py:183
  135.4 11.0 %copy-start.4 = (bf16[256,1024]{1,0:T(8,128)(2,1)S(1)}, bf16[256,1024]{1,0:T(8,128)(2,1)}, u32[]{:S(2)}) copy-start(bf16[256,1024]{1,0:T(8,128)(2,1)} %param.18) | copy-start | bytes 1572868
  135.4 114.0 %all-to-all-start.2 = ((bf16[128,2,16,1024]{3,2,1,0:T(8,128)(2,1)}), bf16[128,2,16,1024]{3,2,1,0:T(8,128)(2,1)}, u32[]{:S(2)}, u32[]{:S(2)}) async-start(bf16[128,2,16,1024]{3,2,1,0:T(8,128)(2,1)} %bitcast.42), calls=%async_computation.2 | async-start | bytes 16777216 | tf_op jit(solution)/shard_map/all_to_all | solution.py:186
  146.4 1.0 copy-start.5
  146.4 1.4 copy-start.7
  147.7 3.2 %copy-start.6 = (bf16[1024]{0:T(1024)(128)(2,1)S(1)}, bf16[1024]{0:T(1024)(128)(2,1)}, u32[]{:S(2)}) copy-start(bf16[1024]{0:T(1024)(128)(2,1)} %param.29) | copy-start | bytes 6148
  147.7 3.2 %copy-start.10 = (s32[4]{0:T(128)S(1)}, s32[4]{0:T(128)}, u32[]{:S(2)}) copy-start(s32[4]{0:T(128)} %param.26) | copy-start | bytes 52
  147.7 3.3 %copy-start.11 = (s32[4]{0:T(128)S(1)}, s32[4]{0:T(128)}, u32[]{:S(2)}) copy-start(s32[4]{0:T(128)} %param.27) | copy-start | bytes 52
  147.7 3.6 %copy-start.3 = (bf16[256,1024]{1,0:T(8,128)(2,1)S(1)}, bf16[256,1024]{1,0:T(8,128)(2,1)}, u32[]{:S(2)}) copy-start(bf16[256,1024]{1,0:T(8,128)(2,1)} %vd_ref.1) | copy-start | bytes 1572868
  249.4 20.1 %copy-start.8 = (bf16[1024,1024]{1,0:T(8,128)(2,1)S(1)}, bf16[1024,1024]{1,0:T(8,128)(2,1)}, u32[]{:S(2)}) copy-start(bf16[1024,1024]{1,0:T(8,128)(2,1)} %param.28) | copy-start | bytes 6291460
  249.4 20.1 %copy-start.9 = (bf16[256,1024]{1,0:T(8,128)(2,1)S(1)}, bf16[256,1024]{1,0:T(8,128)(2,1)}, u32[]{:S(2)}) copy-start(bf16[256,1024]{1,0:T(8,128)(2,1)} %param.16) | copy-start | bytes 1572868
  269.5 8.9 %slice-start = ((s8[5373952]{0:T(1024)(128)(4,1)}), s8[4194304]{0:T(1024)(128)(4,1)S(1)}, s32[]{:S(2)}) async-start(s8[5373952]{0:T(1024)(128)(4,1)} %bitcast.59), calls=%async_computation.3 | async-start | bytes 8388608
  271.8 6.6 %slice-start.1 = ((s8[5373952]{0:T(1024)(128)(4,1)}), s8[1179648]{0:T(1024)(128)(4,1)S(1)}, s32[]{:S(2)}) async-start(s8[5373952]{0:T(1024)(128)(4,1)} %bitcast.59), calls=%async_computation.4 | async-start | bytes 2359296
  278.4 8.3 %copy-start.1 = (bf16[96,16,1024]{2,1,0:T(8,128)(2,1)S(1)}, bf16[96,16,1024]{2,1,0:T(8,128)(2,1)}, u32[]{:S(2)}) copy-start(bf16[96,16,1024]{2,1,0:T(8,128)(2,1)} %param.20) | copy-start | bytes 9437188

commit v6 on v5

--- a/solution.py
+++ b/solution.py
@@ -68,8 +68,7 @@
 
 def _context_kernel(pc_ref, pd_ref, vc_ref, vd_ref, o_ref, *, head_size):
     rows, lanes = o_ref.shape
-    start = pl.multiple_of(pl.program_id(0) * lanes, lanes)
-    vc = vc_ref[:, :, pl.ds(start, lanes)].reshape(-1, lanes)
+    vc = vc_ref[...].reshape(-1, lanes)
     vd = vd_ref[...]
     lane = lax.broadcasted_iota(jnp.int32, (1, lanes), 1)
     result = None
@@ -121,7 +120,7 @@
         in_specs=[
             pl.BlockSpec((None, per, rows, keys), lambda h: (h, 0, 0, 0)),
             pl.BlockSpec((None, per, rows, rows), lambda h: (h, 0, 0, 0)),
-            pl.BlockSpec((slots, page_len, width), lambda h: (0, 0, 0)),
+            pl.BlockSpec((slots, page_len, lanes), lambda h: (0, 0, h)),
             pl.BlockSpec((rows, lanes), lambda h: (0, h)),
         ],
         out_specs=pl.BlockSpec((rows, lanes), lambda h: (0, h)),

time: 289 us -> 287 us (level)
  no operation moved by 1% of the time
where the time goes in v6:
time: 287 us; the launch traced here: 285 us
  waiting for transfers between devices  149 us (52%)
  Pallas kernels  52.3 us (18%)
  starting transfers between devices  31.6 us (11%)
  local copies, waits for them, and re-layouts  24 us (8%)
  matrix products  21.1 us (7%)
  other arithmetic  5.88 us (2%)
    all_to_all x1, waiting for transfers between devices, local(): lax.all_to_all(cache_keys[source].reshape(devices, per_target, page_len,...  93.1 us
    all_to_all x1, waiting for transfers between devices, local(): lax.all_to_all(cache_values[source].reshape(devices, per_target, page_len...  56.2 us
    pallas_call x1, Pallas kernels, attend(): pl.pallas_call(functools.partial(_probs_kernel, tree_width=tree_width, he...  33.8 us
    pallas_call x1, Pallas kernels, attend(): pl.pallas_call(functools.partial(_context_kernel, head_size=head_size), g...  18.6 us
    all_to_all x1, starting transfers between devices, local(): lax.all_to_all(cache_values[source].reshape(devices, per_target, page_len...  11 us
    all_to_all x1, starting transfers between devices, local(): lax.all_to_all(send_meta, 'req', 0, 0, tiled=True).reshape(slot_count, 2)  10.4 us
    all_to_all x1, starting transfers between devices, local(): lax.all_to_all(cache_keys[source].reshape(devices, per_target, page_len,...  10.2 us
    gather x1, local copies, waits for them, and re-layouts, local(): cache_values[source].reshape(devices, per_target, page_len, width)  8.4 us
  transfers between devices with their start and end apart: 3, of which 2 were waited for; matrix products, arithmetic and copies ran while one was open for 10% of the time, Pallas kernels for 12%

profile of v6, /device:TPU:12, one launch (start us, length us, event | category | flops | bytes accessed | tf_op | source)
XLA Modules:
  0.0 285.2 jit_solution(11122728463480681082)
XLA Ops:
  0.6 0.9 fusion.50
  1.5 0.1 reduce_window_sum.11
  1.7 0.8 select_reduce_fusion.3
  2.5 0.7 add_add_fusion
  3.2 0.8 select_reduce_fusion
  4.0 0.1 copy.39
  4.1 0.7 all_to_all.12
  4.9 10.4 %all-to-all-start = ((s32[128,1,4]{2,1,0:T(1,128)}), s32[128,1,4]{2,1,0:T(1,128)S(1)}, u32[]{:S(2)}, u32[]{:S(2)}) async-start(s32[128,1,4]{2,1,0:T(1,128)} %bitcast.4), calls=%async_computation | async-start | bytes 131072 | tf_op jit(solution)/shard_map/all_to_all | solution.py:188
  15.3 8.4 %gather_fusion = bf16[256,16,1024]{2,1,0:T(8,128)(2,1)} fusion(bf16[96,16,1024]{2,1,0:T(8,128)(2,1)S(1)} %copy-done, s32[1024]{0:T(1024)S(1)} %pad_clamp_fusion), kind=kCustom, calls=%fused_computation | custom fusion | bytes 16778240 | tf_op jit(solution)/shard_map/gather | solution.py:183
  23.7 10.2 %all-to-all-start.1 = ((bf16[128,2,16,1024]{3,2,1,0:T(8,128)(2,1)}), bf16[128,2,16,1024]{3,2,1,0:T(8,128)(2,1)}, u32[]{:S(2)}, u32[]{:S(2)}) async-start(bf16[128,2,16,1024]{3,2,1,0:T(8,128)(2,1)} %bitcast.43), calls=%async_computation.1 | async-start | bytes 16777216 | tf_op jit(solution)/shard_map/all_to_all | solution.py:182
  33.9 8.4 %gather_fusion.1 = bf16[256,16,1024]{2,1,0:T(8,128)(2,1)} fusion(bf16[96,16,1024]{2,1,0:T(8,128)(2,1)S(1)} %copy-done.2, s32[1024]{0:T(1024)S(1)} %pad_clamp_fusion), kind=kCustom, calls=%fused_computation.1 | custom fusion | bytes 16778240 | tf_op jit(solution)/shard_map/gather | solution.py:186
  42.3 93.1 %all-to-all-done.1 = bf16[128,2,16,1024]{3,2,1,0:T(8,128)(2,1)} async-done(((bf16[128,2,16,1024]{3,2,1,0:T(8,128)(2,1)}), bf16[128,2,16,1024]{3,2,1,0:T(8,128)(2,1)}, u32[]{:S(2)}, u32[]{:S(2)}) %all-to-all-start.1) | async-done | bytes 8388640 | tf_op jit(solution)/shard_map/all_to_all | solution.py:182
  135.4 11.0 %all-to-all-start.2 = ((bf16[128,2,16,1024]{3,2,1,0:T(8,128)(2,1)}), bf16[128,2,16,1024]{3,2,1,0:T(8,128)(2,1)}, u32[]{:S(2)}, u32[]{:S(2)}) async-start(bf16[128,2,16,1024]{3,2,1,0:T(8,128)(2,1)} %bitcast.42), calls=%async_computation.2 | async-start | bytes 16777216 | tf_op jit(solution)/shard_map/all_to_all | solution.py:185
  146.4 0.2 copy.43
  146.6 0.1 convert.11
  146.7 0.7 copy-done.5
  147.4 0.2 copy.38
  147.7 0.1 convert.10
  147.9 0.4 convolution_minimum_fusion.5
  148.2 0.3 convolution_minimum_fusion.4
  148.5 0.3 convolution_minimum_fusion.3
  148.7 0.3 convolution_minimum_fusion.2
  149.0 0.3 convolution_minimum_fusion.1
  149.3 0.4 fusion.88
  149.6 0.2 broadcast_multiply_fusion
  149.8 1.1 mul.182.tmask_ref
  151.1 0.2 fusion.52
  151.3 1.1 convolution_convert_fusion.1
  152.4 0.5 broadcast.227
  152.9 0.8 reduce.7
  153.8 0.2 slice_reduce_fusion.1
  154.0 0.1 select_reduce_fusion.4
  154.3 0.2 multiply_cosine_fusion
  154.5 0.2 multiply_subtract_fusion
  154.7 0.4 reshape.278
  155.1 1.0 copy.45.kd_ref
  156.1 0.1 subtract_convert_fusion
  156.3 1.0 copy.44.q_ref
  157.3 0.1 fusion.41
  157.5 0.7 select_n.49.kown_ref
  158.2 1.3 convolution_convert_fusion
  159.4 33.8 %shard_map.175 = (bf16[8,2,256,4096]{3,2,1,0:T(8,128)(2,1)}, bf16[8,2,256,256]{3,2,1,0:T(8,128)(2,1)}) custom-call(bf16[256,1024]{1,0:T(8,128)(2,1)} %copy.44.q_ref, bf16[256,16,1024]{2,1,0:T(8,128)(2,1)} %bitcast.10.kc_ref, bf16[256,1024]{1,0:T(8,128)(2,1)} %copy.45.kd_ref, s32[1,4096]{1,0:T(1,128)} %select_n.49.kown_ref, f32[256,256]{1,0:T(8,128)} %mul.182.tmask_ref), custom_call_target="tpu_custom_call" | custom-call | tf_op jit(solution)/shard_map/pallas_call | solution.py:95
  193.2 56.2 %all-to-all-done.2 = bf16[128,2,16,1024]{3,2,1,0:T(8,128)(2,1)} async-done(((bf16[128,2,16,1024]{3,2,1,0:T(8,128)(2,1)}), bf16[128,2,16,1024]{3,2,1,0:T(8,128)(2,1)}, u32[]{:S(2)}, u32[]{:S(2)}) %all-to-all-start.2) | async-done | bytes 8388640 | tf_op jit(solution)/shard_map/all_to_all | solution.py:185
  249.4 18.6 %shard_map.176 = bf16[256,1024]{1,0:T(8,128)(2,1)} custom-call(bf16[8,2,256,4096]{3,2,1,0:T(8,128)(2,1)} %get-tuple-element.5.pc_ref, bf16[8,2,256,256]{3,2,1,0:T(8,128)(2,1)} %get-tuple-element.6.pd_ref, bf16[256,16,1024]{2,1,0:T(8,128)(2,1)} %bitcast.15.vc_ref, bf16[256,1024]{1,0:T(8,128)(2,1)} %vd_ref.1), custom_call_target="tpu_custom_call" | custom-call | tf_op jit(solution)/shard_map/pallas_call | solution.py:117
  268.0 2.0 convert_reduce_fusion
  270.0 0.3 fusion.30
  270.3 6.5 %fusion.34 = f32[256,5248]{1,0:T(8,128)S(1)} fusion(bf16[1024,5248]{1,0:T(8,128)(2,1)} %param.30, bf16[256,1024]{1,0:T(8,128)(2,1)S(1)} %get-tuple-element.21, f32[1024]{0:T(1024)S(1)} %convert_element_type.114, f32[256]{0:T(256)S(1)} %add_rsqrt_fusion, f32[256]{0:T(256)S(1)} %broadcast_multiply_fusion.1), kind=kOutput, calls=%fused_computation.47 | convolution fusion | flops 2752774144 | bytes 16652288 | tf_op jit(solution)/shard_map/dot_general | solution.py:141
  276.9 8.3 %fusion.27 = bf16[256,1024]{1,0:T(8,128)(2,1)} fusion(bf16[2624,1024]{1,0:T(8,128)(2,1)S(1)} %bitcast.60, f32[256,5248]{1,0:T(8,128)S(1)} %fusion.34, bf16[256,1024]{1,0:T(8,128)(2,1)S(1)} %get-tuple-element.21, pred[256]{0:T(512)(128)(4,1)S(1)} %lt.57), kind=kOutput, calls=%fused_computation.35 | convolution fusion | flops 1421639680 | bytes 11928064 | tf_op jit(solution)/shard_map/dot_general | solution.py:145
  (48 shorter events, 0.7 us)
Async XLA Ops:
  0.6 14.6 %copy-start = (bf16[96,16,1024]{2,1,0:T(8,128)(2,1)S(1)}, bf16[96,16,1024]{2,1,0:T(8,128)(2,1)}, u32[]{:S(2)}) copy-start(bf16[96,16,1024]{2,1,0:T(8,128)(2,1)} %param.20) | copy-start | bytes 9437188
  4.9 18.8 %all-to-all-start = ((s32[128,1,4]{2,1,0:T(1,128)}), s32[128,1,4]{2,1,0:T(1,128)S(1)}, u32[]{:S(2)}, u32[]{:S(2)}) async-start(s32[128,1,4]{2,1,0:T(1,128)} %bitcast.4), calls=%async_computation | async-start | bytes 131072 | tf_op jit(solution)/shard_map/all_to_all | solution.py:188
  23.7 10.2 %copy-start.2 = (bf16[96,16,1024]{2,1,0:T(8,128)(2,1)S(1)}, bf16[96,16,1024]{2,1,0:T(8,128)(2,1)}, u32[]{:S(2)}) copy-start(bf16[96,16,1024]{2,1,0:T(8,128)(2,1)} %param.21) | copy-start | bytes 9437188
  23.7 111.7 %all-to-all-start.1 = ((bf16[128,2,16,1024]{3,2,1,0:T(8,128)(2,1)}), bf16[128,2,16,1024]{3,2,1,0:T(8,128)(2,1)}, u32[]{:S(2)}, u32[]{:S(2)}) async-start(bf16[128,2,16,1024]{3,2,1,0:T(8,128)(2,1)} %bitcast.43), calls=%async_computation.1 | async-start | bytes 16777216 | tf_op jit(solution)/shard_map/all_to_all | solution.py:182
  135.4 11.0 %copy-start.4 = (bf16[256,1024]{1,0:T(8,128)(2,1)S(1)}, bf16[256,1024]{1,0:T(8,128)(2,1)}, u32[]{:S(2)}) copy-start(bf16[256,1024]{1,0:T(8,128)(2,1)} %param.18) | copy-start | bytes 1572868
  135.4 114.0 %all-to-all-start.2 = ((bf16[128,2,16,1024]{3,2,1,0:T(8,128)(2,1)}), bf16[128,2,16,1024]{3,2,1,0:T(8,128)(2,1)}, u32[]{:S(2)}, u32[]{:S(2)}) async-start(bf16[128,2,16,1024]{3,2,1,0:T(8,128)(2,1)} %bitcast.42), calls=%async_computation.2 | async-start | bytes 16777216 | tf_op jit(solution)/shard_map/all_to_all | solution.py:185
  146.4 1.0 copy-start.5
  146.4 1.4 copy-start.7
  147.7 3.2 %copy-start.6 = (bf16[1024]{0:T(1024)(128)(2,1)S(1)}, bf16[1024]{0:T(1024)(128)(2,1)}, u32[]{:S(2)}) copy-start(bf16[1024]{0:T(1024)(128)(2,1)} %param.29) | copy-start | bytes 6148
  147.7 3.2 %copy-start.10 = (s32[4]{0:T(128)S(1)}, s32[4]{0:T(128)}, u32[]{:S(2)}) copy-start(s32[4]{0:T(128)} %param.26) | copy-start | bytes 52
  147.7 3.3 %copy-start.11 = (s32[4]{0:T(128)S(1)}, s32[4]{0:T(128)}, u32[]{:S(2)}) copy-start(s32[4]{0:T(128)} %param.27) | copy-start | bytes 52
  147.7 3.6 %copy-start.3 = (bf16[256,1024]{1,0:T(8,128)(2,1)S(1)}, bf16[256,1024]{1,0:T(8,128)(2,1)}, u32[]{:S(2)}) copy-start(bf16[256,1024]{1,0:T(8,128)(2,1)} %vd_ref.1) | copy-start | bytes 1572868
  249.4 18.6 %copy-start.8 = (bf16[1024,1024]{1,0:T(8,128)(2,1)S(1)}, bf16[1024,1024]{1,0:T(8,128)(2,1)}, u32[]{:S(2)}) copy-start(bf16[1024,1024]{1,0:T(8,128)(2,1)} %param.28) | copy-start | bytes 6291460
  249.4 18.6 %copy-start.9 = (bf16[256,1024]{1,0:T(8,128)(2,1)S(1)}, bf16[256,1024]{1,0:T(8,128)(2,1)}, u32[]{:S(2)}) copy-start(bf16[256,1024]{1,0:T(8,128)(2,1)} %param.16) | copy-start | bytes 1572868
  268.0 8.9 %slice-start = ((s8[5373952]{0:T(1024)(128)(4,1)}), s8[4194304]{0:T(1024)(128)(4,1)S(1)}, s32[]{:S(2)}) async-start(s8[5373952]{0:T(1024)(128)(4,1)} %bitcast.59), calls=%async_computation.3 | async-start | bytes 8388608
  270.3 6.6 %slice-start.1 = ((s8[5373952]{0:T(1024)(128)(4,1)}), s8[1179648]{0:T(1024)(128)(4,1)S(1)}, s32[]{:S(2)}) async-start(s8[5373952]{0:T(1024)(128)(4,1)} %bitcast.59), calls=%async_computation.4 | async-start | bytes 2359296
  276.9 8.3 %copy-start.1 = (bf16[96,16,1024]{2,1,0:T(8,128)(2,1)S(1)}, bf16[96,16,1024]{2,1,0:T(8,128)(2,1)}, u32[]{:S(2)}) copy-start(bf16[96,16,1024]{2,1,0:T(8,128)(2,1)} %param.20) | copy-start | bytes 9437188

commit v7 on v6

--- a/solution.py
+++ b/solution.py
@@ -138,10 +138,12 @@
     normed = (centred * lax.rsqrt(variance + 1e-05) * ln_gain.astype(jnp.float32)[None, :]).astype(
         jnp.bfloat16
     )
+    normed = lax.optimization_barrier(normed)
     both = jnp.dot(normed, w_in, preferred_element_type=jnp.float32)
     middle = (jax.nn.gelu(both[:, :inner], approximate=False) * both[:, inner:]).astype(
         jnp.bfloat16
     )
+    middle = lax.optimization_barrier(middle)
     return jnp.dot(middle, w_out, preferred_element_type=jnp.float32).astype(jnp.bfloat16)
 
 

time: 287 us -> 288 us (level)
  other arithmetic: 5.88 us -> 12.4 us
  matrix products: 21.1 us -> 15.1 us
    convert_element_type x0 -> x2, other arithmetic: none -> 6.53 us  [the longest x1 6.23 us: feed_forward(): (jax.nn.gelu(both[:, :inner], approximate=False) * both[:, inner:]).astyp...]
    dot_general x1, matrix products: 8.28 us -> 2.56 us  [feed_forward(): jnp.dot(middle, w_out, preferred_element_type=jnp.float32)]
where the time goes in v7:
time: 288 us; the launch traced here: 286 us
  waiting for transfers between devices  149 us (52%)
  Pallas kernels  52.3 us (18%)
  starting transfers between devices  31.5 us (11%)
  local copies, waits for them, and re-layouts  24 us (8%)
  matrix products  15.1 us (5%)
  other arithmetic  12.4 us (4%)
    all_to_all x1, waiting for transfers between devices, local(): lax.all_to_all(cache_keys[source].reshape(devices, per_target, page_len,...  93.1 us
    all_to_all x1, waiting for transfers between devices, local(): lax.all_to_all(cache_values[source].reshape(devices, per_target, page_len...  56.2 us
    pallas_call x1, Pallas kernels, attend(): pl.pallas_call(functools.partial(_probs_kernel, tree_width=tree_width, he...  33.8 us
    pallas_call x1, Pallas kernels, attend(): pl.pallas_call(functools.partial(_context_kernel, head_size=head_size), g...  18.6 us
    all_to_all x1, starting transfers between devices, local(): lax.all_to_all(cache_values[source].reshape(devices, per_target, page_len...  11 us
    all_to_all x1, starting transfers between devices, local(): lax.all_to_all(send_meta, 'req', 0, 0, tiled=True).reshape(slot_count, 2)  10.4 us
    all_to_all x1, starting transfers between devices, local(): lax.all_to_all(cache_keys[source].reshape(devices, per_target, page_len,...  10.2 us
    gather x1, local copies, waits for them, and re-layouts, local(): cache_values[source].reshape(devices, per_target, page_len, width)  8.42 us
  transfers between devices with their start and end apart: 3, of which 2 were waited for; matrix products, arithmetic and copies ran while one was open for 10% of the time, Pallas kernels for 12%

profile of v7, /device:TPU:12, one launch (start us, length us, event | category | flops | bytes accessed | tf_op | source)
XLA Modules:
  0.0 285.8 jit_solution(10412596414002246987)
XLA Ops:
  0.6 0.9 fusion.32
  1.5 0.1 reduce_window_sum.11
  1.7 0.8 select_reduce_fusion.3
  2.5 0.7 add_add_fusion
  3.2 0.8 select_reduce_fusion
  4.0 0.1 copy.39
  4.1 0.7 all_to_all.12
  4.9 10.4 %all-to-all-start = ((s32[128,1,4]{2,1,0:T(1,128)}), s32[128,1,4]{2,1,0:T(1,128)S(1)}, u32[]{:S(2)}, u32[]{:S(2)}) async-start(s32[128,1,4]{2,1,0:T(1,128)} %bitcast.4), calls=%async_computation | async-start | bytes 131072 | tf_op jit(solution)/shard_map/all_to_all | solution.py:190
  15.3 8.4 %gather_fusion = bf16[256,16,1024]{2,1,0:T(8,128)(2,1)} fusion(bf16[96,16,1024]{2,1,0:T(8,128)(2,1)S(1)} %copy-done, s32[1024]{0:T(1024)S(1)} %pad_clamp_fusion), kind=kCustom, calls=%fused_computation | custom fusion | bytes 16778240 | tf_op jit(solution)/shard_map/gather | solution.py:185
  23.7 10.2 %all-to-all-start.1 = ((bf16[128,2,16,1024]{3,2,1,0:T(8,128)(2,1)}), bf16[128,2,16,1024]{3,2,1,0:T(8,128)(2,1)}, u32[]{:S(2)}, u32[]{:S(2)}) async-start(bf16[128,2,16,1024]{3,2,1,0:T(8,128)(2,1)} %bitcast.45), calls=%async_computation.1 | async-start | bytes 16777216 | tf_op jit(solution)/shard_map/all_to_all | solution.py:184
  33.9 8.4 %gather_fusion.1 = bf16[256,16,1024]{2,1,0:T(8,128)(2,1)} fusion(bf16[96,16,1024]{2,1,0:T(8,128)(2,1)S(1)} %copy-done.2, s32[1024]{0:T(1024)S(1)} %pad_clamp_fusion), kind=kCustom, calls=%fused_computation.1 | custom fusion | bytes 16778240 | tf_op jit(solution)/shard_map/gather | solution.py:188
  42.3 93.1 %all-to-all-done.1 = bf16[128,2,16,1024]{3,2,1,0:T(8,128)(2,1)} async-done(((bf16[128,2,16,1024]{3,2,1,0:T(8,128)(2,1)}), bf16[128,2,16,1024]{3,2,1,0:T(8,128)(2,1)}, u32[]{:S(2)}, u32[]{:S(2)}) %all-to-all-start.1) | async-done | bytes 8388640 | tf_op jit(solution)/shard_map/all_to_all | solution.py:184
  135.4 11.0 %all-to-all-start.2 = ((bf16[128,2,16,1024]{3,2,1,0:T(8,128)(2,1)}), bf16[128,2,16,1024]{3,2,1,0:T(8,128)(2,1)}, u32[]{:S(2)}, u32[]{:S(2)}) async-start(bf16[128,2,16,1024]{3,2,1,0:T(8,128)(2,1)} %bitcast.44), calls=%async_computation.2 | async-start | bytes 16777216 | tf_op jit(solution)/shard_map/all_to_all | solution.py:187
  146.4 0.2 copy.43
  146.8 0.7 copy-done.5
  147.5 0.2 copy.38
  147.9 0.4 convolution_minimum_fusion.5
  148.2 0.3 convolution_minimum_fusion.4
  148.5 0.3 convolution_minimum_fusion.3
  148.7 0.3 convolution_minimum_fusion.2
  149.0 0.3 convolution_minimum_fusion.1
  149.3 0.4 fusion.40
  149.6 0.2 broadcast_multiply_fusion
  149.8 1.1 mul.182.tmask_ref
  151.1 0.2 fusion.34
  151.3 1.1 convolution_convert_fusion.1
  152.4 0.5 broadcast.216
  152.9 0.8 reduce.7
  153.8 0.2 slice_reduce_fusion.1
  154.0 0.1 select_reduce_fusion.4
  154.3 0.2 multiply_cosine_fusion
  154.5 0.2 multiply_subtract_fusion
  154.7 0.4 reshape.278
  155.1 1.0 copy.45.kd_ref
  156.1 0.1 subtract_convert_fusion
  156.3 1.0 copy.44.q_ref
  157.3 0.1 fusion.23
  157.5 0.7 select_n.49.kown_ref
  158.2 1.3 convolution_convert_fusion
  159.5 33.8 %shard_map.175 = (bf16[8,2,256,4096]{3,2,1,0:T(8,128)(2,1)}, bf16[8,2,256,256]{3,2,1,0:T(8,128)(2,1)}) custom-call(bf16[256,1024]{1,0:T(8,128)(2,1)} %copy.44.q_ref, bf16[256,16,1024]{2,1,0:T(8,128)(2,1)} %bitcast.10.kc_ref, bf16[256,1024]{1,0:T(8,128)(2,1)} %copy.45.kd_ref, s32[1,4096]{1,0:T(1,128)} %select_n.49.kown_ref, f32[256,256]{1,0:T(8,128)} %mul.182.tmask_ref), custom_call_target="tpu_custom_call" | custom-call | tf_op jit(solution)/shard_map/pallas_call | solution.py:95
  193.2 56.2 %all-to-all-done.2 = bf16[128,2,16,1024]{3,2,1,0:T(8,128)(2,1)} async-done(((bf16[128,2,16,1024]{3,2,1,0:T(8,128)(2,1)}), bf16[128,2,16,1024]{3,2,1,0:T(8,128)(2,1)}, u32[]{:S(2)}, u32[]{:S(2)}) %all-to-all-start.2) | async-done | bytes 8388640 | tf_op jit(solution)/shard_map/all_to_all | solution.py:187
  249.4 18.6 %shard_map.176 = bf16[256,1024]{1,0:T(8,128)(2,1)} custom-call(bf16[8,2,256,4096]{3,2,1,0:T(8,128)(2,1)} %get-tuple-element.5.pc_ref, bf16[8,2,256,256]{3,2,1,0:T(8,128)(2,1)} %get-tuple-element.6.pd_ref, bf16[256,16,1024]{2,1,0:T(8,128)(2,1)} %bitcast.15.vc_ref, bf16[256,1024]{1,0:T(8,128)(2,1)} %vd_ref.1), custom_call_target="tpu_custom_call" | custom-call | tf_op jit(solution)/shard_map/pallas_call | solution.py:117
  268.0 2.0 convert_reduce_fusion
  270.0 0.3 fusion.17
  270.3 0.3 fusion.19
  270.6 6.3 %fusion.41 = f32[256,5248]{1,0:T(8,128)S(1)} fusion(bf16[256,1024]{1,0:T(8,128)(2,1)S(1)} %fusion.19, bf16[1024,5248]{1,0:T(8,128)(2,1)} %param.30), kind=kOutput, calls=%fused_computation.102 | convolution fusion | flops 2751463424 | bytes 16646144 | tf_op jit(solution)/shard_map/dot_general | solution.py:142
  276.9 6.2 %fusion.3 = bf16[256,2624]{1,0:T(8,128)(2,1)S(1)} fusion(f32[256,5248]{1,0:T(8,128)S(1)} %fusion.41), kind=kLoop, calls=%fused_computation.6 | loop fusion | flops 44335104 | bytes 6717440 | tf_op jit(solution)/shard_map/convert_element_type | solution.py:143
  283.2 2.6 fusion.14
  (50 shorter events, 0.9 us)
Async XLA Ops:
  0.6 14.6 %copy-start = (bf16[96,16,1024]{2,1,0:T(8,128)(2,1)S(1)}, bf16[96,16,1024]{2,1,0:T(8,128)(2,1)}, u32[]{:S(2)}) copy-start(bf16[96,16,1024]{2,1,0:T(8,128)(2,1)} %param.20) | copy-start | bytes 9437188
  4.9 18.8 %all-to-all-start = ((s32[128,1,4]{2,1,0:T(1,128)}), s32[128,1,4]{2,1,0:T(1,128)S(1)}, u32[]{:S(2)}, u32[]{:S(2)}) async-start(s32[128,1,4]{2,1,0:T(1,128)} %bitcast.4), calls=%async_computation | async-start | bytes 131072 | tf_op jit(solution)/shard_map/all_to_all | solution.py:190
  23.7 10.2 %copy-start.2 = (bf16[96,16,1024]{2,1,0:T(8,128)(2,1)S(1)}, bf16[96,16,1024]{2,1,0:T(8,128)(2,1)}, u32[]{:S(2)}) copy-start(bf16[96,16,1024]{2,1,0:T(8,128)(2,1)} %param.21) | copy-start | bytes 9437188
  23.7 111.7 %all-to-all-start.1 = ((bf16[128,2,16,1024]{3,2,1,0:T(8,128)(2,1)}), bf16[128,2,16,1024]{3,2,1,0:T(8,128)(2,1)}, u32[]{:S(2)}, u32[]{:S(2)}) async-start(bf16[128,2,16,1024]{3,2,1,0:T(8,128)(2,1)} %bitcast.45), calls=%async_computation.1 | async-start | bytes 16777216 | tf_op jit(solution)/shard_map/all_to_all | solution.py:184
  135.4 11.0 %copy-start.4 = (bf16[256,1024]{1,0:T(8,128)(2,1)S(1)}, bf16[256,1024]{1,0:T(8,128)(2,1)}, u32[]{:S(2)}) copy-start(bf16[256,1024]{1,0:T(8,128)(2,1)} %param.18) | copy-start | bytes 1572868
  135.4 114.0 %all-to-all-start.2 = ((bf16[128,2,16,1024]{3,2,1,0:T(8,128)(2,1)}), bf16[128,2,16,1024]{3,2,1,0:T(8,128)(2,1)}, u32[]{:S(2)}, u32[]{:S(2)}) async-start(bf16[128,2,16,1024]{3,2,1,0:T(8,128)(2,1)} %bitcast.44), calls=%async_computation.2 | async-start | bytes 16777216 | tf_op jit(solution)/shard_map/all_to_all | solution.py:187
  146.4 1.0 copy-start.5
  146.4 1.4 copy-start.7
  147.7 3.2 %copy-start.6 = (bf16[1024]{0:T(1024)(128)(2,1)S(1)}, bf16[1024]{0:T(1024)(128)(2,1)}, u32[]{:S(2)}) copy-start(bf16[1024]{0:T(1024)(128)(2,1)} %param.29) | copy-start | bytes 6148
  147.7 3.2 %copy-start.10 = (s32[4]{0:T(128)S(1)}, s32[4]{0:T(128)}, u32[]{:S(2)}) copy-start(s32[4]{0:T(128)} %param.26) | copy-start | bytes 52
  147.7 3.3 %copy-start.11 = (s32[4]{0:T(128)S(1)}, s32[4]{0:T(128)}, u32[]{:S(2)}) copy-start(s32[4]{0:T(128)} %param.27) | copy-start | bytes 52
  147.7 3.6 %copy-start.3 = (bf16[256,1024]{1,0:T(8,128)(2,1)S(1)}, bf16[256,1024]{1,0:T(8,128)(2,1)}, u32[]{:S(2)}) copy-start(bf16[256,1024]{1,0:T(8,128)(2,1)} %vd_ref.1) | copy-start | bytes 1572868
  249.4 18.6 %copy-start.8 = (bf16[1024,1024]{1,0:T(8,128)(2,1)S(1)}, bf16[1024,1024]{1,0:T(8,128)(2,1)}, u32[]{:S(2)}) copy-start(bf16[1024,1024]{1,0:T(8,128)(2,1)} %param.28) | copy-start | bytes 6291460
  249.4 18.6 %copy-start.9 = (bf16[256,1024]{1,0:T(8,128)(2,1)S(1)}, bf16[256,1024]{1,0:T(8,128)(2,1)}, u32[]{:S(2)}) copy-start(bf16[256,1024]{1,0:T(8,128)(2,1)} %param.16) | copy-start | bytes 1572868
  268.0 15.2 %slice-start = ((s8[5373952]{0:T(1024)(128)(4,1)}), s8[4194304]{0:T(1024)(128)(4,1)S(1)}, s32[]{:S(2)}) async-start(s8[5373952]{0:T(1024)(128)(4,1)} %bitcast.61), calls=%async_computation.3 | async-start | bytes 8388608
  270.6 12.6 %slice-start.1 = ((s8[5373952]{0:T(1024)(128)(4,1)}), s8[1179648]{0:T(1024)(128)(4,1)S(1)}, s32[]{:S(2)}) async-start(s8[5373952]{0:T(1024)(128)(4,1)} %bitcast.61), calls=%async_computation.4 | async-start | bytes 2359296
  283.2 2.6 copy-start.1

commit v8 on v6

--- a/solution.py
+++ b/solution.py
@@ -179,9 +179,9 @@
     send_fill = jnp.sum(jnp.where(matches, page_fill[None, :], 0), axis=1)
     send_owner = jnp.sum(jnp.where(matches, page_slot[None, :], 0), axis=1)
     send_meta = jnp.stack([send_fill, send_owner], axis=1).reshape(devices, per_target * 2)
-    recv_k = lax.all_to_all(
-        cache_keys[source].reshape(devices, per_target, page_len, width), "req", 0, 0, tiled=True
-    ).reshape(slot_count, page_len, width)
+    send_k = cache_keys[source].reshape(devices, per_target, page_len, width)
+    send_meta, send_k = lax.optimization_barrier((send_meta, send_k))
+    recv_k = lax.all_to_all(send_k, "req", 0, 0, tiled=True).reshape(slot_count, page_len, width)
     recv_v = lax.all_to_all(
         cache_values[source].reshape(devices, per_target, page_len, width), "req", 0, 0, tiled=True
     ).reshape(slot_count, page_len, width)

time: 287 us -> 291 us (1.014)
  blocking collectives: 0 us -> 17.3 us
  starting transfers between devices: 31.6 us -> 19.3 us
    all_to_all x0 -> x1, blocking collectives: none -> 17.3 us  [local(): lax.all_to_all(send_meta, 'req', 0, 0, tiled=True).reshape(slot_count, 2)]
    all_to_all x2 -> x1, starting transfers between devices: 20.6 us -> 8.32 us  [local(): lax.all_to_all(send_k, 'req', 0, 0, tiled=True)]
    all_to_all x2 -> x1, waiting for transfers between devices: 93.1 us -> 93.2 us  [local(): lax.all_to_all(send_k, 'req', 0, 0, tiled=True)]
  transfers between devices with their start and end apart: 3 -> 2, of which waited for: 2 -> 2; matrix products, arithmetic and copies ran while one was open for 10% -> 7% of each run, Pallas kernels for 12% -> 12%
where the time goes in v8:
time: 291 us; the launch traced here: 290 us
  waiting for transfers between devices  149 us (51%)
  Pallas kernels  52.3 us (18%)
  local copies, waits for them, and re-layouts  23.4 us (8%)
  matrix products  21.1 us (7%)
  starting transfers between devices  19.3 us (7%)
  blocking collectives  17.3 us (6%)
  other arithmetic  5.88 us (2%)
    all_to_all x1, waiting for transfers between devices, local(): lax.all_to_all(send_k, 'req', 0, 0, tiled=True)  93.2 us
    all_to_all x1, waiting for transfers between devices, local(): lax.all_to_all(cache_values[source].reshape(devices, per_target, page_len...  56.2 us
    pallas_call x1, Pallas kernels, attend(): pl.pallas_call(functools.partial(_probs_kernel, tree_width=tree_width, he...  33.8 us
    pallas_call x1, Pallas kernels, attend(): pl.pallas_call(functools.partial(_context_kernel, head_size=head_size), g...  18.6 us
    all_to_all x1, blocking collectives, local(): lax.all_to_all(send_meta, 'req', 0, 0, tiled=True).reshape(slot_count, 2)  17.3 us
    all_to_all x1, starting transfers between devices, local(): lax.all_to_all(cache_values[source].reshape(devices, per_target, page_len...  11 us
    gather x1, local copies, waits for them, and re-layouts, local(): cache_values[source].reshape(devices, per_target, page_len, width)  8.4 us
    gather x1, local copies, waits for them, and re-layouts, local(): send_k = cache_keys[source].reshape(devices, per_target, page_len, width)  8.39 us
  transfers between devices with their start and end apart: 2, of which 2 were waited for; matrix products, arithmetic and copies ran while one was open for 7% of the time, Pallas kernels for 12%

profile of v8, /device:TPU:12, one launch (start us, length us, event | category | flops | bytes accessed | tf_op | source)
XLA Modules:
  0.0 289.6 jit_solution(14724642893804945583)
XLA Ops:
  0.6 0.9 fusion.50
  1.5 0.1 reduce_window_sum.11
  1.7 0.8 select_reduce_fusion.3
  2.5 0.7 add_add_fusion
  3.2 0.8 select_reduce_fusion
  4.0 0.1 copy.39
  4.3 8.4 %gather_fusion = bf16[256,16,1024]{2,1,0:T(8,128)(2,1)} fusion(bf16[96,16,1024]{2,1,0:T(8,128)(2,1)S(1)} %copy-done, s32[1024]{0:T(1024)S(1)} %pad_clamp_fusion), kind=kCustom, calls=%fused_computation | custom fusion | bytes 16778240 | tf_op jit(solution)/shard_map/gather | solution.py:182
  12.7 17.3 %all_to_all.19 = s32[128,1,4]{2,1,0:T(1,128)S(1)} all-to-all(s32[128,1,4]{2,1,0:T(1,128)S(1)} %bitcast.53), channel_id=1, replica_groups=mesh['req'=128] {'req'}, dimensions={0} | all-to-all | bytes 4096 | tf_op jit(solution)/shard_map/all_to_all | solution.py:188
  30.0 8.3 %all-to-all-start.1 = ((bf16[128,2,16,1024]{3,2,1,0:T(8,128)(2,1)}), bf16[128,2,16,1024]{3,2,1,0:T(8,128)(2,1)}, u32[]{:S(2)}, u32[]{:S(2)}) async-start(bf16[128,2,16,1024]{3,2,1,0:T(8,128)(2,1)} %bitcast.45), calls=%async_computation.1 | async-start | bytes 16777216 | tf_op jit(solution)/shard_map/all_to_all | solution.py:184
  38.3 8.4 %gather_fusion.1 = bf16[256,16,1024]{2,1,0:T(8,128)(2,1)} fusion(bf16[96,16,1024]{2,1,0:T(8,128)(2,1)S(1)} %copy-done.2, s32[1024]{0:T(1024)S(1)} %pad_clamp_fusion), kind=kCustom, calls=%fused_computation.1 | custom fusion | bytes 16778240 | tf_op jit(solution)/shard_map/gather | solution.py:186
  46.7 93.2 %all-to-all-done.1 = bf16[128,2,16,1024]{3,2,1,0:T(8,128)(2,1)} async-done(((bf16[128,2,16,1024]{3,2,1,0:T(8,128)(2,1)}), bf16[128,2,16,1024]{3,2,1,0:T(8,128)(2,1)}, u32[]{:S(2)}, u32[]{:S(2)}) %all-to-all-start.1) | async-done | bytes 8388640 | tf_op jit(solution)/shard_map/all_to_all | solution.py:184
  139.9 11.0 %all-to-all-start.2 = ((bf16[128,2,16,1024]{3,2,1,0:T(8,128)(2,1)}), bf16[128,2,16,1024]{3,2,1,0:T(8,128)(2,1)}, u32[]{:S(2)}, u32[]{:S(2)}) async-start(bf16[128,2,16,1024]{3,2,1,0:T(8,128)(2,1)} %bitcast.44), calls=%async_computation.2 | async-start | bytes 16777216 | tf_op jit(solution)/shard_map/all_to_all | solution.py:185
  150.8 0.2 copy.43
  151.1 0.1 convert.11
  151.2 0.7 copy-done.5
  151.9 0.2 copy.38
  152.1 0.1 convert.10
  152.3 0.4 convolution_minimum_fusion.5
  152.6 0.3 convolution_minimum_fusion.4
  152.9 0.3 convolution_minimum_fusion.3
  153.2 0.3 convolution_minimum_fusion.2
  153.4 0.3 convolution_minimum_fusion.1
  153.7 0.4 fusion.88
  154.0 0.2 broadcast_multiply_fusion
  154.2 1.1 mul.182.tmask_ref
  155.3 0.1 lt.57
  155.5 0.2 fusion.52
  155.7 1.1 convolution_convert_fusion.1
  156.8 0.5 broadcast.227
  157.3 0.8 reduce.7
  158.2 0.2 slice_reduce_fusion.1
  158.4 0.1 select_reduce_fusion.4
  158.7 0.2 multiply_cosine_fusion
  158.9 0.2 multiply_subtract_fusion
  159.1 0.4 reshape.280
  159.5 1.0 copy.45.kd_ref
  160.5 0.1 subtract_convert_fusion
  160.7 1.0 copy.44.q_ref
  161.7 0.1 fusion.41
  161.9 0.7 select_n.49.kown_ref
  162.6 1.3 convolution_convert_fusion
  163.9 33.8 %shard_map.175 = (bf16[8,2,256,4096]{3,2,1,0:T(8,128)(2,1)}, bf16[8,2,256,256]{3,2,1,0:T(8,128)(2,1)}) custom-call(bf16[256,1024]{1,0:T(8,128)(2,1)} %copy.44.q_ref, bf16[256,16,1024]{2,1,0:T(8,128)(2,1)} %bitcast.11.kc_ref, bf16[256,1024]{1,0:T(8,128)(2,1)} %copy.45.kd_ref, s32[1,4096]{1,0:T(1,128)} %select_n.49.kown_ref, f32[256,256]{1,0:T(8,128)} %mul.182.tmask_ref), custom_call_target="tpu_custom_call" | custom-call | tf_op jit(solution)/shard_map/pallas_call | solution.py:95
  197.7 56.2 %all-to-all-done.2 = bf16[128,2,16,1024]{3,2,1,0:T(8,128)(2,1)} async-done(((bf16[128,2,16,1024]{3,2,1,0:T(8,128)(2,1)}), bf16[128,2,16,1024]{3,2,1,0:T(8,128)(2,1)}, u32[]{:S(2)}, u32[]{:S(2)}) %all-to-all-start.2) | async-done | bytes 8388640 | tf_op jit(solution)/shard_map/all_to_all | solution.py:185
  253.8 18.6 %shard_map.176 = bf16[256,1024]{1,0:T(8,128)(2,1)} custom-call(bf16[8,2,256,4096]{3,2,1,0:T(8,128)(2,1)} %get-tuple-element.9.pc_ref, bf16[8,2,256,256]{3,2,1,0:T(8,128)(2,1)} %get-tuple-element.10.pd_ref, bf16[256,16,1024]{2,1,0:T(8,128)(2,1)} %bitcast.16.vc_ref, bf16[256,1024]{1,0:T(8,128)(2,1)} %vd_ref.1), custom_call_target="tpu_custom_call" | custom-call | tf_op jit(solution)/shard_map/pallas_call | solution.py:117
  272.4 2.0 convert_reduce_fusion
  274.4 0.3 fusion.30
  274.7 6.5 %fusion.34 = f32[256,5248]{1,0:T(8,128)S(1)} fusion(bf16[1024,5248]{1,0:T(8,128)(2,1)} %param.30, bf16[256,1024]{1,0:T(8,128)(2,1)S(1)} %get-tuple-element.25, f32[1024]{0:T(1024)S(1)} %convert_element_type.114, f32[256]{0:T(256)S(1)} %add_rsqrt_fusion, f32[256]{0:T(256)S(1)} %broadcast_multiply_fusion.1), kind=kOutput, calls=%fused_computation.47 | convolution fusion | flops 2752774144 | bytes 16652288 | tf_op jit(solution)/shard_map/dot_general | solution.py:141
  281.3 8.3 %fusion.27 = bf16[256,1024]{1,0:T(8,128)(2,1)} fusion(bf16[2624,1024]{1,0:T(8,128)(2,1)S(1)} %bitcast.63, f32[256,5248]{1,0:T(8,128)S(1)} %fusion.34, bf16[256,1024]{1,0:T(8,128)(2,1)S(1)} %get-tuple-element.25, pred[256]{0:T(512)(128)(4,1)S(1)} %lt.57), kind=kOutput, calls=%fused_computation.35 | convolution fusion | flops 1421639680 | bytes 11928064 | tf_op jit(solution)/shard_map/dot_general | solution.py:145
  (47 shorter events, 0.7 us)
Async XLA Ops:
  0.6 3.6 %copy-start = (bf16[96,16,1024]{2,1,0:T(8,128)(2,1)S(1)}, bf16[96,16,1024]{2,1,0:T(8,128)(2,1)}, u32[]{:S(2)}) copy-start(bf16[96,16,1024]{2,1,0:T(8,128)(2,1)} %param.20) | copy-start | bytes 9437188
  29.9 8.3 %copy-start.2 = (bf16[96,16,1024]{2,1,0:T(8,128)(2,1)S(1)}, bf16[96,16,1024]{2,1,0:T(8,128)(2,1)}, u32[]{:S(2)}) copy-start(bf16[96,16,1024]{2,1,0:T(8,128)(2,1)} %param.21) | copy-start | bytes 9437188
  30.0 109.9 %all-to-all-start.1 = ((bf16[128,2,16,1024]{3,2,1,0:T(8,128)(2,1)}), bf16[128,2,16,1024]{3,2,1,0:T(8,128)(2,1)}, u32[]{:S(2)}, u32[]{:S(2)}) async-start(bf16[128,2,16,1024]{3,2,1,0:T(8,128)(2,1)} %bitcast.45), calls=%async_computation.1 | async-start | bytes 16777216 | tf_op jit(solution)/shard_map/all_to_all | solution.py:184
  139.9 11.0 %copy-start.4 = (bf16[256,1024]{1,0:T(8,128)(2,1)S(1)}, bf16[256,1024]{1,0:T(8,128)(2,1)}, u32[]{:S(2)}) copy-start(bf16[256,1024]{1,0:T(8,128)(2,1)} %param.18) | copy-start | bytes 1572868
  139.9 114.0 %all-to-all-start.2 = ((bf16[128,2,16,1024]{3,2,1,0:T(8,128)(2,1)}), bf16[128,2,16,1024]{3,2,1,0:T(8,128)(2,1)}, u32[]{:S(2)}, u32[]{:S(2)}) async-start(bf16[128,2,16,1024]{3,2,1,0:T(8,128)(2,1)} %bitcast.44), calls=%async_computation.2 | async-start | bytes 16777216 | tf_op jit(solution)/shard_map/all_to_all | solution.py:185
  150.8 1.0 copy-start.5
  150.8 1.4 copy-start.7
  152.1 3.2 %copy-start.6 = (bf16[1024]{0:T(1024)(128)(2,1)S(1)}, bf16[1024]{0:T(1024)(128)(2,1)}, u32[]{:S(2)}) copy-start(bf16[1024]{0:T(1024)(128)(2,1)} %param.29) | copy-start | bytes 6148
  152.1 3.2 %copy-start.10 = (s32[4]{0:T(128)S(1)}, s32[4]{0:T(128)}, u32[]{:S(2)}) copy-start(s32[4]{0:T(128)} %param.26) | copy-start | bytes 52
  152.1 3.3 %copy-start.11 = (s32[4]{0:T(128)S(1)}, s32[4]{0:T(128)}, u32[]{:S(2)}) copy-start(s32[4]{0:T(128)} %param.27) | copy-start | bytes 52
  152.1 3.6 %copy-start.3 = (bf16[256,1024]{1,0:T(8,128)(2,1)S(1)}, bf16[256,1024]{1,0:T(8,128)(2,1)}, u32[]{:S(2)}) copy-start(bf16[256,1024]{1,0:T(8,128)(2,1)} %vd_ref.1) | copy-start | bytes 1572868
  253.8 18.6 %copy-start.8 = (bf16[1024,1024]{1,0:T(8,128)(2,1)S(1)}, bf16[1024,1024]{1,0:T(8,128)(2,1)}, u32[]{:S(2)}) copy-start(bf16[1024,1024]{1,0:T(8,128)(2,1)} %param.28) | copy-start | bytes 6291460
  253.8 18.6 %copy-start.9 = (bf16[256,1024]{1,0:T(8,128)(2,1)S(1)}, bf16[256,1024]{1,0:T(8,128)(2,1)}, u32[]{:S(2)}) copy-start(bf16[256,1024]{1,0:T(8,128)(2,1)} %param.16) | copy-start | bytes 1572868
  272.4 8.9 %slice-start = ((s8[5373952]{0:T(1024)(128)(4,1)}), s8[4194304]{0:T(1024)(128)(4,1)S(1)}, s32[]{:S(2)}) async-start(s8[5373952]{0:T(1024)(128)(4,1)} %bitcast.62), calls=%async_computation.3 | async-start | bytes 8388608
  274.7 6.6 %slice-start.1 = ((s8[5373952]{0:T(1024)(128)(4,1)}), s8[1179648]{0:T(1024)(128)(4,1)S(1)}, s32[]{:S(2)}) async-start(s8[5373952]{0:T(1024)(128)(4,1)} %bitcast.62), calls=%async_computation.4 | async-start | bytes 2359296
  281.3 8.3 %copy-start.1 = (bf16[96,16,1024]{2,1,0:T(8,128)(2,1)S(1)}, bf16[96,16,1024]{2,1,0:T(8,128)(2,1)}, u32[]{:S(2)}) copy-start(bf16[96,16,1024]{2,1,0:T(8,128)(2,1)} %param.20) | copy-start | bytes 9437188

commit v9 on v6

--- a/solution.py
+++ b/solution.py
@@ -129,20 +129,41 @@
     )(probs_c, probs_d, recv_v, draft_value)
 
 
-def feed_forward(rows_in, ln_gain, w_in, w_out):
+def _ffn_kernel(x_ref, g_ref, win_ref, wout_ref, alive_ref, o_ref, *, inner):
+    x = x_ref[...].astype(jnp.float32)
+    mean_value = jnp.mean(x, axis=1, keepdims=True)
+    centred = x - mean_value
+    variance = jnp.mean(centred * centred, axis=1, keepdims=True)
+    normed = (centred * lax.rsqrt(variance + 1e-05) * g_ref[...].astype(jnp.float32)).astype(
+        jnp.bfloat16
+    )
+    both = jnp.dot(normed, win_ref[...], preferred_element_type=jnp.float32)
+    gate = both[:, :inner]
+    gelu = 0.5 * gate * (1.0 + lax.erf(gate * (0.5**0.5)))
+    middle = (gelu * both[:, inner:]).astype(jnp.bfloat16)
+    ffn = jnp.dot(middle, wout_ref[...], preferred_element_type=jnp.float32).astype(jnp.bfloat16)
+    out = jnp.where(alive_ref[...] > 0, x + ffn.astype(jnp.float32), 0.0)
+    o_ref[...] = out.astype(o_ref.dtype)
+
+
+def feed_forward_out(attended, ln_gain, w_in, w_out, alive):
+    rows, width = attended.shape
     inner = w_out.shape[0]
-    floats = rows_in.astype(jnp.float32)
-    mean_value = jnp.mean(floats, axis=1, keepdims=True)
-    centred = floats - mean_value
-    variance = jnp.mean(centred * centred, axis=1, keepdims=True)
-    normed = (centred * lax.rsqrt(variance + 1e-05) * ln_gain.astype(jnp.float32)[None, :]).astype(
-        jnp.bfloat16
-    )
-    both = jnp.dot(normed, w_in, preferred_element_type=jnp.float32)
-    middle = (jax.nn.gelu(both[:, :inner], approximate=False) * both[:, inner:]).astype(
-        jnp.bfloat16
-    )
-    return jnp.dot(middle, w_out, preferred_element_type=jnp.float32).astype(jnp.bfloat16)
+    whole = lambda shape: pl.BlockSpec(shape, lambda i: (0,) * len(shape))
+    return pl.pallas_call(
+        functools.partial(_ffn_kernel, inner=inner),
+        grid=(1,),
+        in_specs=[
+            whole((rows, width)),
+            whole((1, width)),
+            whole(w_in.shape),
+            whole(w_out.shape),
+            whole((rows, 1)),
+        ],
+        out_specs=whole((rows, width)),
+        out_shape=jax.ShapeDtypeStruct((rows, width), jnp.bfloat16),
+        compiler_params=pltpu.CompilerParams(vmem_limit_bytes=62 * 1024 * 1024),
+    )(attended, ln_gain.reshape(1, width), w_in, w_out, alive.astype(jnp.int32).reshape(rows, 1))
 
 
 def local(
@@ -213,10 +234,7 @@
     alive_mask = (jnp.arange(tree_width, dtype=jnp.int32)[None, :] < tree_size[:, None]).reshape(
         rows
     )
-    ffn_out = feed_forward(attended, ln_gain, w_in, w_out)
-    layer_out = jnp.where(
-        alive_mask[:, None], attended.astype(jnp.float32) + ffn_out.astype(jnp.float32), 0.0
-    ).astype(jnp.bfloat16)
+    layer_out = feed_forward_out(attended, ln_gain, w_in, w_out, alive_mask)
     leaf_index = jnp.minimum(accepted_leaf, tree_size - 1)
     leaf_onehot = (jnp.arange(tree_width, dtype=jnp.int32)[None, :] == leaf_index[:, None]).astype(
         jnp.float32

time: 287 us -> 286 us (level)
  matrix products: 21.1 us -> 6.81 us
  Pallas kernels: 52.3 us -> 63.8 us
  local copies, waits for them, and re-layouts: 24 us -> 27.5 us
    dot_general x2 -> x0, matrix products: 14.8 us -> none  [the longest x1 8.28 us: feed_forward(): jnp.dot(middle, w_out, preferred_element_type=jnp.float32)]
    pallas_call x0 -> x1, Pallas kernels: none -> 11.4 us  [feed_forward_out(): pl.pallas_call(functools.partial(_ffn_kernel, inner=inner), grid=(1,), in...]
  transfers between devices with their start and end apart: 3 -> 3, of which waited for: 2 -> 2; matrix products, arithmetic and copies ran while one was open for 10% -> 12% of each run, Pallas kernels for 12% -> 12%
where the time goes in v9:
time: 286 us; the launch traced here: 284 us
  waiting for transfers between devices  148 us (52%)
  Pallas kernels  63.8 us (22%)
  starting transfers between devices  31.6 us (11%)
  local copies, waits for them, and re-layouts  27.5 us (10%)
  matrix products  6.81 us (2%)
  other arithmetic  5.42 us (2%)
    all_to_all x1, waiting for transfers between devices, local(): lax.all_to_all(cache_keys[source].reshape(devices, per_target, page_len,...  93.1 us
    all_to_all x1, waiting for transfers between devices, local(): lax.all_to_all(cache_values[source].reshape(devices, per_target, page_len...  54.5 us
    pallas_call x1, Pallas kernels, attend(): pl.pallas_call(functools.partial(_probs_kernel, tree_width=tree_width, he...  33.8 us
    pallas_call x1, Pallas kernels, attend(): pl.pallas_call(functools.partial(_context_kernel, head_size=head_size), g...  18.6 us
    pallas_call x1, Pallas kernels, feed_forward_out(): pl.pallas_call(functools.partial(_ffn_kernel, inner=inner), grid=(1,), in...  11.4 us
    all_to_all x1, starting transfers between devices, local(): lax.all_to_all(cache_values[source].reshape(devices, per_target, page_len...  11 us
    all_to_all x1, starting transfers between devices, local(): lax.all_to_all(send_meta, 'req', 0, 0, tiled=True).reshape(slot_count, 2)  10.4 us
    gather x1, local copies, waits for them, and re-layouts, local(): cache_keys[source].reshape(devices, per_target, page_len, width)  10.3 us
  transfers between devices with their start and end apart: 3, of which 2 were waited for; matrix products, arithmetic and copies ran while one was open for 12% of the time, Pallas kernels for 12%

profile of v9, /device:TPU:12, one launch (start us, length us, event | category | flops | bytes accessed | tf_op | source)
XLA Modules:
  0.0 283.6 jit_solution(7282824710352323785)
XLA Ops:
  0.6 0.7 fusion.13
  1.4 0.1 reduce_window_sum.11
  1.5 0.8 select_reduce_fusion.3
  2.3 0.7 add_add_fusion
  3.0 0.8 select_reduce_fusion
  3.8 0.1 copy.41
  4.0 0.7 all_to_all.12
  4.7 10.4 %all-to-all-start = ((s32[128,1,4]{2,1,0:T(1,128)}), s32[128,1,4]{2,1,0:T(1,128)S(1)}, u32[]{:S(2)}, u32[]{:S(2)}) async-start(s32[128,1,4]{2,1,0:T(1,128)} %bitcast.4), calls=%async_computation | async-start | bytes 131072 | tf_op jit(solution)/shard_map/all_to_all | solution.py:209
  15.1 10.3 %gather_fusion = bf16[256,16,1024]{2,1,0:T(8,128)(2,1)} fusion(bf16[96,16,1024]{2,1,0:T(8,128)(2,1)} %param.20, s32[1024]{0:T(1024)S(1)} %pad_clamp_fusion), kind=kCustom, calls=%fused_computation | custom fusion | bytes 16778240 | tf_op jit(solution)/shard_map/gather | solution.py:204
  25.4 10.2 %all-to-all-start.1 = ((bf16[128,2,16,1024]{3,2,1,0:T(8,128)(2,1)}), bf16[128,2,16,1024]{3,2,1,0:T(8,128)(2,1)}, u32[]{:S(2)}, u32[]{:S(2)}) async-start(bf16[128,2,16,1024]{3,2,1,0:T(8,128)(2,1)} %bitcast.41), calls=%async_computation.1 | async-start | bytes 16777216 | tf_op jit(solution)/shard_map/all_to_all | solution.py:203
  35.6 8.4 %gather_fusion.1 = bf16[256,16,1024]{2,1,0:T(8,128)(2,1)} fusion(bf16[96,16,1024]{2,1,0:T(8,128)(2,1)S(1)} %copy-done, s32[1024]{0:T(1024)S(1)} %pad_clamp_fusion), kind=kCustom, calls=%fused_computation.1 | custom fusion | bytes 16778240 | tf_op jit(solution)/shard_map/gather | solution.py:207
  44.1 93.1 %all-to-all-done.1 = bf16[128,2,16,1024]{3,2,1,0:T(8,128)(2,1)} async-done(((bf16[128,2,16,1024]{3,2,1,0:T(8,128)(2,1)}), bf16[128,2,16,1024]{3,2,1,0:T(8,128)(2,1)}, u32[]{:S(2)}, u32[]{:S(2)}) %all-to-all-start.1) | async-done | bytes 8388640 | tf_op jit(solution)/shard_map/all_to_all | solution.py:203
  137.2 11.0 %all-to-all-start.2 = ((bf16[128,2,16,1024]{3,2,1,0:T(8,128)(2,1)}), bf16[128,2,16,1024]{3,2,1,0:T(8,128)(2,1)}, u32[]{:S(2)}, u32[]{:S(2)}) async-start(bf16[128,2,16,1024]{3,2,1,0:T(8,128)(2,1)} %bitcast.40), calls=%async_computation.2 | async-start | bytes 16777216 | tf_op jit(solution)/shard_map/all_to_all | solution.py:206
  148.2 0.2 copy.45
  148.4 0.1 convert.12
  148.5 1.2 copy.40
  149.7 0.1 convert.11
  149.9 0.4 convolution_minimum_fusion.5
  150.3 0.3 convolution_minimum_fusion.4
  150.5 0.3 convolution_minimum_fusion.3
  150.8 0.3 convolution_minimum_fusion.2
  151.0 0.3 convolution_minimum_fusion.1
  151.3 0.4 fusion.22
  151.7 0.2 broadcast_multiply_fusion
  151.8 1.1 mul.145.tmask_ref
  153.0 0.8 reshape.283.alive_ref
  153.8 0.6 reshape.258.g_ref
  154.5 0.2 fusion.15
  154.6 1.1 convolution_convert_fusion.1
  155.7 0.5 broadcast.185
  156.2 0.8 reduce.7
  157.1 0.2 slice_reduce_fusion.1
  157.4 0.1 select_reduce_fusion.4
  157.5 0.1 convert_element_type.98
  157.6 0.2 multiply_cosine_fusion
  157.8 0.2 multiply_subtract_fusion
  158.0 0.4 reshape.284
  158.5 1.0 copy.47.kd_ref
  159.5 0.1 subtract_convert_fusion
  159.7 1.0 copy.46.q_ref
  160.7 0.1 fusion.4
  160.8 0.7 select_n.45.kown_ref
  161.5 1.3 convolution_convert_fusion
  162.8 33.8 %shard_map.175 = (bf16[8,2,256,4096]{3,2,1,0:T(8,128)(2,1)}, bf16[8,2,256,256]{3,2,1,0:T(8,128)(2,1)}) custom-call(bf16[256,1024]{1,0:T(8,128)(2,1)} %copy.46.q_ref, bf16[256,16,1024]{2,1,0:T(8,128)(2,1)} %bitcast.10.kc_ref, bf16[256,1024]{1,0:T(8,128)(2,1)} %copy.47.kd_ref, s32[1,4096]{1,0:T(1,128)} %select_n.45.kown_ref, f32[256,256]{1,0:T(8,128)} %mul.145.tmask_ref), custom_call_target="tpu_custom_call" | custom-call | tf_op jit(solution)/shard_map/pallas_call | solution.py:95
  196.6 54.5 %all-to-all-done.2 = bf16[128,2,16,1024]{3,2,1,0:T(8,128)(2,1)} async-done(((bf16[128,2,16,1024]{3,2,1,0:T(8,128)(2,1)}), bf16[128,2,16,1024]{3,2,1,0:T(8,128)(2,1)}, u32[]{:S(2)}, u32[]{:S(2)}) %all-to-all-start.2) | async-done | bytes 8388640 | tf_op jit(solution)/shard_map/all_to_all | solution.py:206
  251.1 18.6 %shard_map.176 = bf16[256,1024]{1,0:T(8,128)(2,1)} custom-call(bf16[8,2,256,4096]{3,2,1,0:T(8,128)(2,1)} %get-tuple-element.5.pc_ref, bf16[8,2,256,256]{3,2,1,0:T(8,128)(2,1)} %get-tuple-element.6.pd_ref, bf16[256,16,1024]{2,1,0:T(8,128)(2,1)} %bitcast.15.vc_ref, bf16[256,1024]{1,0:T(8,128)(2,1)} %vd_ref.1), custom_call_target="tpu_custom_call" | custom-call | tf_op jit(solution)/shard_map/pallas_call | solution.py:117
  269.7 2.5 fusion.x_ref
  272.2 11.4 %shard_map.177 = bf16[256,1024]{1,0:T(8,128)(2,1)} custom-call(bf16[256,1024]{1,0:T(8,128)(2,1)} %fusion.x_ref, bf16[1,1024]{1,0:T(2,128)(2,1)} %reshape.258.g_ref, bf16[1024,5248]{1,0:T(8,128)(2,1)} %win_ref.1, bf16[2624,1024]{1,0:T(8,128)(2,1)} %wout_ref.1, s32[256,1]{1,0:T(8,128)} %reshape.283.alive_ref), custom_call_target="tpu_custom_call" | custom-call | tf_op jit(solution)/shard_map/pallas_call | solution.py:153
  (33 shorter events, 0.5 us)
Async XLA Ops:
  4.7 20.7 %all-to-all-start = ((s32[128,1,4]{2,1,0:T(1,128)}), s32[128,1,4]{2,1,0:T(1,128)S(1)}, u32[]{:S(2)}, u32[]{:S(2)}) async-start(s32[128,1,4]{2,1,0:T(1,128)} %bitcast.4), calls=%async_computation | async-start | bytes 131072 | tf_op jit(solution)/shard_map/all_to_all | solution.py:209
  25.4 10.2 %copy-start = (bf16[96,16,1024]{2,1,0:T(8,128)(2,1)S(1)}, bf16[96,16,1024]{2,1,0:T(8,128)(2,1)}, u32[]{:S(2)}) copy-start(bf16[96,16,1024]{2,1,0:T(8,128)(2,1)} %param.21) | copy-start | bytes 9437188
  25.4 111.7 %all-to-all-start.1 = ((bf16[128,2,16,1024]{3,2,1,0:T(8,128)(2,1)}), bf16[128,2,16,1024]{3,2,1,0:T(8,128)(2,1)}, u32[]{:S(2)}, u32[]{:S(2)}) async-start(bf16[128,2,16,1024]{3,2,1,0:T(8,128)(2,1)} %bitcast.41), calls=%async_computation.1 | async-start | bytes 16777216 | tf_op jit(solution)/shard_map/all_to_all | solution.py:203
  137.2 11.0 %copy-start.2 = (bf16[256,1024]{1,0:T(8,128)(2,1)S(1)}, bf16[256,1024]{1,0:T(8,128)(2,1)}, u32[]{:S(2)}) copy-start(bf16[256,1024]{1,0:T(8,128)(2,1)} %param.18) | copy-start | bytes 1572868
  137.2 12.7 %copy-start.4 = (s32[4,64]{1,0:T(4,128)S(1)}, s32[4,64]{1,0:T(4,128)}, u32[]{:S(2)}) copy-start(s32[4,64]{1,0:T(4,128)} %param.25) | copy-start | bytes 3076
  137.2 114.0 %all-to-all-start.2 = ((bf16[128,2,16,1024]{3,2,1,0:T(8,128)(2,1)}), bf16[128,2,16,1024]{3,2,1,0:T(8,128)(2,1)}, u32[]{:S(2)}, u32[]{:S(2)}) async-start(bf16[128,2,16,1024]{3,2,1,0:T(8,128)(2,1)} %bitcast.40), calls=%async_computation.2 | async-start | bytes 16777216 | tf_op jit(solution)/shard_map/all_to_all | solution.py:206
  148.1 4.8 %copy-start.5 = (s32[4]{0:T(128)S(1)}, s32[4]{0:T(128)}, u32[]{:S(2)}) copy-start(s32[4]{0:T(128)} %param.26) | copy-start | bytes 52
  148.1 5.6 %copy-start.3 = (bf16[1024]{0:T(1024)(128)(2,1)S(1)}, bf16[1024]{0:T(1024)(128)(2,1)}, u32[]{:S(2)}) copy-start(bf16[1024]{0:T(1024)(128)(2,1)} %param.29) | copy-start | bytes 6148
  148.1 6.2 %copy-start.8 = (s32[4]{0:T(128)S(1)}, s32[4]{0:T(128)}, u32[]{:S(2)}) copy-start(s32[4]{0:T(128)} %param.27) | copy-start | bytes 52
  148.2 6.5 %copy-start.1 = (bf16[256,1024]{1,0:T(8,128)(2,1)S(1)}, bf16[256,1024]{1,0:T(8,128)(2,1)}, u32[]{:S(2)}) copy-start(bf16[256,1024]{1,0:T(8,128)(2,1)} %vd_ref.1) | copy-start | bytes 1572868
  251.1 18.6 %copy-start.6 = (bf16[1024,1024]{1,0:T(8,128)(2,1)S(1)}, bf16[1024,1024]{1,0:T(8,128)(2,1)}, u32[]{:S(2)}) copy-start(bf16[1024,1024]{1,0:T(8,128)(2,1)} %param.28) | copy-start | bytes 6291460
  251.1 18.6 %copy-start.7 = (bf16[256,1024]{1,0:T(8,128)(2,1)S(1)}, bf16[256,1024]{1,0:T(8,128)(2,1)}, u32[]{:S(2)}) copy-start(bf16[256,1024]{1,0:T(8,128)(2,1)} %param.16) | copy-start | bytes 1572868

commit v10 on v9

--- a/solution.py
+++ b/solution.py
@@ -129,7 +129,19 @@
     )(probs_c, probs_d, recv_v, draft_value)
 
 
-def _ffn_kernel(x_ref, g_ref, win_ref, wout_ref, alive_ref, o_ref, *, inner):
+def _ffn_kernel(x_ref, g_ref, win_hbm, wout_hbm, alive_ref, o_ref, win_v, wout_v, sems, *,
+                inner, parts):
+    step = win_v.shape[0] // parts
+    loads = [
+        pltpu.make_async_copy(
+            win_hbm.at[pl.ds(i * step, step)], win_v.at[pl.ds(i * step, step)], sems.at[i]
+        )
+        for i in range(parts)
+    ]
+    load_out = pltpu.make_async_copy(wout_hbm, wout_v, sems.at[parts])
+    for load in loads:
+        load.start()
+    load_out.start()
     x = x_ref[...].astype(jnp.float32)
     mean_value = jnp.mean(x, axis=1, keepdims=True)
     centred = x - mean_value
@@ -137,11 +149,19 @@
     normed = (centred * lax.rsqrt(variance + 1e-05) * g_ref[...].astype(jnp.float32)).astype(
         jnp.bfloat16
     )
-    both = jnp.dot(normed, win_ref[...], preferred_element_type=jnp.float32)
+    both = None
+    for i, load in enumerate(loads):
+        load.wait()
+        part = jnp.dot(
+            normed[:, i * step:(i + 1) * step], win_v[pl.ds(i * step, step), :],
+            preferred_element_type=jnp.float32,
+        )
+        both = part if both is None else both + part
     gate = both[:, :inner]
     gelu = 0.5 * gate * (1.0 + lax.erf(gate * (0.5**0.5)))
     middle = (gelu * both[:, inner:]).astype(jnp.bfloat16)
-    ffn = jnp.dot(middle, wout_ref[...], preferred_element_type=jnp.float32).astype(jnp.bfloat16)
+    load_out.wait()
+    ffn = jnp.dot(middle, wout_v[...], preferred_element_type=jnp.float32).astype(jnp.bfloat16)
     out = jnp.where(alive_ref[...] > 0, x + ffn.astype(jnp.float32), 0.0)
     o_ref[...] = out.astype(o_ref.dtype)
 
@@ -149,19 +169,25 @@
 def feed_forward_out(attended, ln_gain, w_in, w_out, alive):
     rows, width = attended.shape
     inner = w_out.shape[0]
+    parts = 4
     whole = lambda shape: pl.BlockSpec(shape, lambda i: (0,) * len(shape))
     return pl.pallas_call(
-        functools.partial(_ffn_kernel, inner=inner),
+        functools.partial(_ffn_kernel, inner=inner, parts=parts),
         grid=(1,),
         in_specs=[
             whole((rows, width)),
             whole((1, width)),
-            whole(w_in.shape),
-            whole(w_out.shape),
+            pl.BlockSpec(memory_space=pl.ANY),
+            pl.BlockSpec(memory_space=pl.ANY),
             whole((rows, 1)),
         ],
         out_specs=whole((rows, width)),
         out_shape=jax.ShapeDtypeStruct((rows, width), jnp.bfloat16),
+        scratch_shapes=[
+            pltpu.VMEM(w_in.shape, w_in.dtype),
+            pltpu.VMEM(w_out.shape, w_out.dtype),
+            pltpu.SemaphoreType.DMA((parts + 1,)),
+        ],
         compiler_params=pltpu.CompilerParams(vmem_limit_bytes=62 * 1024 * 1024),
     )(attended, ln_gain.reshape(1, width), w_in, w_out, alive.astype(jnp.int32).reshape(rows, 1))
 

time: 286 us -> 285 us (level)
  no operation moved by 1% of the time
where the time goes in v10:
time: 285 us; the launch traced here: 283 us
  waiting for transfers between devices  148 us (52%)
  Pallas kernels  62.7 us (22%)
  starting transfers between devices  31.6 us (11%)
  local copies, waits for them, and re-layouts  27.5 us (10%)
  matrix products  6.81 us (2%)
  other arithmetic  5.42 us (2%)
    all_to_all x1, waiting for transfers between devices, local(): lax.all_to_all(cache_keys[source].reshape(devices, per_target, page_len,...  93.1 us
    all_to_all x1, waiting for transfers between devices, local(): lax.all_to_all(cache_values[source].reshape(devices, per_target, page_len...  54.5 us
    pallas_call x1, Pallas kernels, attend(): pl.pallas_call(functools.partial(_probs_kernel, tree_width=tree_width, he...  33.8 us
    pallas_call x1, Pallas kernels, attend(): pl.pallas_call(functools.partial(_context_kernel, head_size=head_size), g...  18.6 us
    all_to_all x1, starting transfers between devices, local(): lax.all_to_all(cache_values[source].reshape(devices, per_target, page_len...  11 us
    all_to_all x1, starting transfers between devices, local(): lax.all_to_all(send_meta, 'req', 0, 0, tiled=True).reshape(slot_count, 2)  10.4 us
    pallas_call x1, Pallas kernels, feed_forward_out(): pl.pallas_call(functools.partial(_ffn_kernel, inner=inner, parts=parts),...  10.3 us
    gather x1, local copies, waits for them, and re-layouts, local(): cache_keys[source].reshape(devices, per_target, page_len, width)  10.3 us
  transfers between devices with their start and end apart: 3, of which 2 were waited for; matrix products, arithmetic and copies ran while one was open for 12% of the time, Pallas kernels for 12%

profile of v10, /device:TPU:12, one launch (start us, length us, event | category | flops | bytes accessed | tf_op | source)
XLA Modules:
  0.0 282.7 jit_solution(15655459913442508968)
XLA Ops:
  0.6 0.7 fusion.13
  1.4 0.1 reduce_window_sum.11
  1.5 0.8 select_reduce_fusion.3
  2.3 0.7 add_add_fusion
  3.0 0.8 select_reduce_fusion
  3.8 0.1 copy.41
  4.0 0.7 all_to_all.12
  4.7 10.4 %all-to-all-start = ((s32[128,1,4]{2,1,0:T(1,128)}), s32[128,1,4]{2,1,0:T(1,128)S(1)}, u32[]{:S(2)}, u32[]{:S(2)}) async-start(s32[128,1,4]{2,1,0:T(1,128)} %bitcast.4), calls=%async_computation | async-start | bytes 131072 | tf_op jit(solution)/shard_map/all_to_all | solution.py:235
  15.1 10.3 %gather_fusion = bf16[256,16,1024]{2,1,0:T(8,128)(2,1)} fusion(bf16[96,16,1024]{2,1,0:T(8,128)(2,1)} %param.20, s32[1024]{0:T(1024)S(1)} %pad_clamp_fusion), kind=kCustom, calls=%fused_computation | custom fusion | bytes 16778240 | tf_op jit(solution)/shard_map/gather | solution.py:230
  25.4 10.2 %all-to-all-start.1 = ((bf16[128,2,16,1024]{3,2,1,0:T(8,128)(2,1)}), bf16[128,2,16,1024]{3,2,1,0:T(8,128)(2,1)}, u32[]{:S(2)}, u32[]{:S(2)}) async-start(bf16[128,2,16,1024]{3,2,1,0:T(8,128)(2,1)} %bitcast.41), calls=%async_computation.1 | async-start | bytes 16777216 | tf_op jit(solution)/shard_map/all_to_all | solution.py:229
  35.6 8.4 %gather_fusion.1 = bf16[256,16,1024]{2,1,0:T(8,128)(2,1)} fusion(bf16[96,16,1024]{2,1,0:T(8,128)(2,1)S(1)} %copy-done, s32[1024]{0:T(1024)S(1)} %pad_clamp_fusion), kind=kCustom, calls=%fused_computation.1 | custom fusion | bytes 16778240 | tf_op jit(solution)/shard_map/gather | solution.py:233
  44.1 93.1 %all-to-all-done.1 = bf16[128,2,16,1024]{3,2,1,0:T(8,128)(2,1)} async-done(((bf16[128,2,16,1024]{3,2,1,0:T(8,128)(2,1)}), bf16[128,2,16,1024]{3,2,1,0:T(8,128)(2,1)}, u32[]{:S(2)}, u32[]{:S(2)}) %all-to-all-start.1) | async-done | bytes 8388640 | tf_op jit(solution)/shard_map/all_to_all | solution.py:229
  137.2 11.0 %all-to-all-start.2 = ((bf16[128,2,16,1024]{3,2,1,0:T(8,128)(2,1)}), bf16[128,2,16,1024]{3,2,1,0:T(8,128)(2,1)}, u32[]{:S(2)}, u32[]{:S(2)}) async-start(bf16[128,2,16,1024]{3,2,1,0:T(8,128)(2,1)} %bitcast.40), calls=%async_computation.2 | async-start | bytes 16777216 | tf_op jit(solution)/shard_map/all_to_all | solution.py:232
  148.2 0.2 copy.45
  148.4 0.1 convert.12
  148.5 1.2 copy.40
  149.8 0.1 convert.11
  149.9 0.4 convolution_minimum_fusion.5
  150.3 0.3 convolution_minimum_fusion.4
  150.5 0.3 convolution_minimum_fusion.3
  150.8 0.3 convolution_minimum_fusion.2
  151.1 0.3 convolution_minimum_fusion.1
  151.3 0.4 fusion.22
  151.7 0.2 broadcast_multiply_fusion
  151.8 1.1 mul.145.tmask_ref
  153.0 0.8 reshape.283.alive_ref
  153.8 0.6 reshape.258.g_ref
  154.5 0.2 fusion.15
  154.6 1.1 convolution_convert_fusion.1
  155.7 0.5 broadcast.185
  156.2 0.8 reduce.7
  157.1 0.2 slice_reduce_fusion.1
  157.4 0.1 select_reduce_fusion.4
  157.6 0.1 convert_element_type.98
  157.6 0.2 multiply_cosine_fusion
  157.8 0.2 multiply_subtract_fusion
  158.1 0.4 reshape.284
  158.5 1.0 copy.47.kd_ref
  159.5 0.1 subtract_convert_fusion
  159.7 1.0 copy.46.q_ref
  160.7 0.1 fusion.4
  160.8 0.7 select_n.45.kown_ref
  161.5 1.3 convolution_convert_fusion
  162.8 33.8 %shard_map.175 = (bf16[8,2,256,4096]{3,2,1,0:T(8,128)(2,1)}, bf16[8,2,256,256]{3,2,1,0:T(8,128)(2,1)}) custom-call(bf16[256,1024]{1,0:T(8,128)(2,1)} %copy.46.q_ref, bf16[256,16,1024]{2,1,0:T(8,128)(2,1)} %bitcast.10.kc_ref, bf16[256,1024]{1,0:T(8,128)(2,1)} %copy.47.kd_ref, s32[1,4096]{1,0:T(1,128)} %select_n.45.kown_ref, f32[256,256]{1,0:T(8,128)} %mul.145.tmask_ref), custom_call_target="tpu_custom_call" | custom-call | tf_op jit(solution)/shard_map/pallas_call | solution.py:95
  196.6 54.5 %all-to-all-done.2 = bf16[128,2,16,1024]{3,2,1,0:T(8,128)(2,1)} async-done(((bf16[128,2,16,1024]{3,2,1,0:T(8,128)(2,1)}), bf16[128,2,16,1024]{3,2,1,0:T(8,128)(2,1)}, u32[]{:S(2)}, u32[]{:S(2)}) %all-to-all-start.2) | async-done | bytes 8388640 | tf_op jit(solution)/shard_map/all_to_all | solution.py:232
  251.1 18.6 %shard_map.176 = bf16[256,1024]{1,0:T(8,128)(2,1)} custom-call(bf16[8,2,256,4096]{3,2,1,0:T(8,128)(2,1)} %get-tuple-element.5.pc_ref, bf16[8,2,256,256]{3,2,1,0:T(8,128)(2,1)} %get-tuple-element.6.pd_ref, bf16[256,16,1024]{2,1,0:T(8,128)(2,1)} %bitcast.15.vc_ref, bf16[256,1024]{1,0:T(8,128)(2,1)} %vd_ref.1), custom_call_target="tpu_custom_call" | custom-call | tf_op jit(solution)/shard_map/pallas_call | solution.py:117
  269.7 2.5 fusion.x_ref
  272.2 10.3 %shard_map.177 = bf16[256,1024]{1,0:T(8,128)(2,1)} custom-call(bf16[256,1024]{1,0:T(8,128)(2,1)} %fusion.x_ref, bf16[1,1024]{1,0:T(2,128)(2,1)} %reshape.258.g_ref, bf16[1024,5248]{1,0:T(8,128)(2,1)} %win_hbm.1, bf16[2624,1024]{1,0:T(8,128)(2,1)} %wout_hbm.1, s32[256,1]{1,0:T(8,128)} %reshape.283.alive_ref), custom_call_target="tpu_custom_call" | custom-call | tf_op jit(solution)/shard_map/pallas_call | solution.py:174
  (33 shorter events, 0.5 us)
Async XLA Ops:
  4.7 20.7 %all-to-all-start = ((s32[128,1,4]{2,1,0:T(1,128)}), s32[128,1,4]{2,1,0:T(1,128)S(1)}, u32[]{:S(2)}, u32[]{:S(2)}) async-start(s32[128,1,4]{2,1,0:T(1,128)} %bitcast.4), calls=%async_computation | async-start | bytes 131072 | tf_op jit(solution)/shard_map/all_to_all | solution.py:235
  25.4 10.2 %copy-start = (bf16[96,16,1024]{2,1,0:T(8,128)(2,1)S(1)}, bf16[96,16,1024]{2,1,0:T(8,128)(2,1)}, u32[]{:S(2)}) copy-start(bf16[96,16,1024]{2,1,0:T(8,128)(2,1)} %param.21) | copy-start | bytes 9437188
  25.4 111.8 %all-to-all-start.1 = ((bf16[128,2,16,1024]{3,2,1,0:T(8,128)(2,1)}), bf16[128,2,16,1024]{3,2,1,0:T(8,128)(2,1)}, u32[]{:S(2)}, u32[]{:S(2)}) async-start(bf16[128,2,16,1024]{3,2,1,0:T(8,128)(2,1)} %bitcast.41), calls=%async_computation.1 | async-start | bytes 16777216 | tf_op jit(solution)/shard_map/all_to_all | solution.py:229
  137.2 11.0 %copy-start.2 = (bf16[256,1024]{1,0:T(8,128)(2,1)S(1)}, bf16[256,1024]{1,0:T(8,128)(2,1)}, u32[]{:S(2)}) copy-start(bf16[256,1024]{1,0:T(8,128)(2,1)} %param.18) | copy-start | bytes 1572868
  137.2 12.7 %copy-start.4 = (s32[4,64]{1,0:T(4,128)S(1)}, s32[4,64]{1,0:T(4,128)}, u32[]{:S(2)}) copy-start(s32[4,64]{1,0:T(4,128)} %param.25) | copy-start | bytes 3076
  137.2 114.0 %all-to-all-start.2 = ((bf16[128,2,16,1024]{3,2,1,0:T(8,128)(2,1)}), bf16[128,2,16,1024]{3,2,1,0:T(8,128)(2,1)}, u32[]{:S(2)}, u32[]{:S(2)}) async-start(bf16[128,2,16,1024]{3,2,1,0:T(8,128)(2,1)} %bitcast.40), calls=%async_computation.2 | async-start | bytes 16777216 | tf_op jit(solution)/shard_map/all_to_all | solution.py:232
  148.1 4.8 %copy-start.5 = (s32[4]{0:T(128)S(1)}, s32[4]{0:T(128)}, u32[]{:S(2)}) copy-start(s32[4]{0:T(128)} %param.26) | copy-start | bytes 52
  148.1 5.6 %copy-start.3 = (bf16[1024]{0:T(1024)(128)(2,1)S(1)}, bf16[1024]{0:T(1024)(128)(2,1)}, u32[]{:S(2)}) copy-start(bf16[1024]{0:T(1024)(128)(2,1)} %param.29) | copy-start | bytes 6148
  148.2 6.2 %copy-start.8 = (s32[4]{0:T(128)S(1)}, s32[4]{0:T(128)}, u32[]{:S(2)}) copy-start(s32[4]{0:T(128)} %param.27) | copy-start | bytes 52
  148.2 6.5 %copy-start.1 = (bf16[256,1024]{1,0:T(8,128)(2,1)S(1)}, bf16[256,1024]{1,0:T(8,128)(2,1)}, u32[]{:S(2)}) copy-start(bf16[256,1024]{1,0:T(8,128)(2,1)} %vd_ref.1) | copy-start | bytes 1572868
  251.1 18.6 %copy-start.6 = (bf16[1024,1024]{1,0:T(8,128)(2,1)S(1)}, bf16[1024,1024]{1,0:T(8,128)(2,1)}, u32[]{:S(2)}) copy-start(bf16[1024,1024]{1,0:T(8,128)(2,1)} %param.28) | copy-start | bytes 6291460
  251.1 18.6 %copy-start.7 = (bf16[256,1024]{1,0:T(8,128)(2,1)S(1)}, bf16[256,1024]{1,0:T(8,128)(2,1)}, u32[]{:S(2)}) copy-start(bf16[256,1024]{1,0:T(8,128)(2,1)} %param.16) | copy-start | bytes 1572868

commit v11 on v10

--- a/solution.py
+++ b/solution.py
@@ -129,9 +129,11 @@
     )(probs_c, probs_d, recv_v, draft_value)
 
 
-def _ffn_kernel(x_ref, g_ref, win_hbm, wout_hbm, alive_ref, o_ref, win_v, wout_v, sems, *,
-                inner, parts):
+def _ffn_kernel(h_ref, c_ref, wo_hbm, g_ref, win_hbm, wout_hbm, alive_ref, o_ref, wo_v, win_v,
+                wout_v, sems, *, inner, parts):
     step = win_v.shape[0] // parts
+    load_proj = pltpu.make_async_copy(wo_hbm, wo_v, sems.at[parts + 1])
+    load_proj.start()
     loads = [
         pltpu.make_async_copy(
             win_hbm.at[pl.ds(i * step, step)], win_v.at[pl.ds(i * step, step)], sems.at[i]
@@ -142,7 +144,11 @@
     for load in loads:
         load.start()
     load_out.start()
-    x = x_ref[...].astype(jnp.float32)
+    load_proj.wait()
+    attended = h_ref[...].astype(jnp.float32) + jnp.dot(
+        c_ref[...], wo_v[...], preferred_element_type=jnp.float32
+    )
+    x = attended.astype(jnp.bfloat16).astype(jnp.float32)
     mean_value = jnp.mean(x, axis=1, keepdims=True)
     centred = x - mean_value
     variance = jnp.mean(centred * centred, axis=1, keepdims=True)
@@ -166,8 +172,8 @@
     o_ref[...] = out.astype(o_ref.dtype)
 
 
-def feed_forward_out(attended, ln_gain, w_in, w_out, alive):
-    rows, width = attended.shape
+def feed_forward_out(hidden, context, w_attn_out, ln_gain, w_in, w_out, alive):
+    rows, width = hidden.shape
     inner = w_out.shape[0]
     parts = 4
     whole = lambda shape: pl.BlockSpec(shape, lambda i: (0,) * len(shape))
@@ -176,6 +182,8 @@
         grid=(1,),
         in_specs=[
             whole((rows, width)),
+            whole((rows, width)),
+            pl.BlockSpec(memory_space=pl.ANY),
             whole((1, width)),
             pl.BlockSpec(memory_space=pl.ANY),
             pl.BlockSpec(memory_space=pl.ANY),
@@ -184,12 +192,16 @@
         out_specs=whole((rows, width)),
         out_shape=jax.ShapeDtypeStruct((rows, width), jnp.bfloat16),
         scratch_shapes=[
+            pltpu.VMEM(w_attn_out.shape, w_attn_out.dtype),
             pltpu.VMEM(w_in.shape, w_in.dtype),
             pltpu.VMEM(w_out.shape, w_out.dtype),
-            pltpu.SemaphoreType.DMA((parts + 1,)),
+            pltpu.SemaphoreType.DMA((parts + 2,)),
         ],
         compiler_params=pltpu.CompilerParams(vmem_limit_bytes=62 * 1024 * 1024),
-    )(attended, ln_gain.reshape(1, width), w_in, w_out, alive.astype(jnp.int32).reshape(rows, 1))
+    )(
+        hidden, context, w_attn_out, ln_gain.reshape(1, width), w_in, w_out,
+        alive.astype(jnp.int32).reshape(rows, 1),
+    )
 
 
 def local(
@@ -253,14 +265,10 @@
         ancestors[:, :, None, :] * jnp.eye(requests, dtype=jnp.float32)[:, None, :, None]
     ).reshape(rows, rows)
     context = attend(query_rot, recv_k, recv_v, key_rot, draft_value, key_owner, tree_mask, tree_width)
-    attended = (
-        hidden.astype(jnp.float32)
-        + jnp.dot(context, w_attn_out, preferred_element_type=jnp.float32)
-    ).astype(jnp.bfloat16)
     alive_mask = (jnp.arange(tree_width, dtype=jnp.int32)[None, :] < tree_size[:, None]).reshape(
         rows
     )
-    layer_out = feed_forward_out(attended, ln_gain, w_in, w_out, alive_mask)
+    layer_out = feed_forward_out(hidden, context, w_attn_out, ln_gain, w_in, w_out, alive_mask)
     leaf_index = jnp.minimum(accepted_leaf, tree_size - 1)
     leaf_onehot = (jnp.arange(tree_width, dtype=jnp.int32)[None, :] == leaf_index[:, None]).astype(
         jnp.float32

time: 285 us -> 283 us (level)
  transfers between devices with their start and end apart: 3 -> 3, of which waited for: 2 -> 2; matrix products, arithmetic and copies ran while one was open for 12% -> 11% of each run, Pallas kernels for 12% -> 12%
where the time goes in v11:
time: 283 us; the launch traced here: 281 us
  waiting for transfers between devices  149 us (53%)
  Pallas kernels  63.3 us (22%)
  starting transfers between devices  31.6 us (11%)
  local copies, waits for them, and re-layouts  26.5 us (9%)
  other arithmetic  5.43 us (2%)
  matrix products  4.26 us (2%)
    all_to_all x1, waiting for transfers between devices, local(): lax.all_to_all(cache_keys[source].reshape(devices, per_target, page_len,...  93.1 us
    all_to_all x1, waiting for transfers between devices, local(): lax.all_to_all(cache_values[source].reshape(devices, per_target, page_len...  55.6 us
    pallas_call x1, Pallas kernels, attend(): pl.pallas_call(functools.partial(_probs_kernel, tree_width=tree_width, he...  33.8 us
    pallas_call x1, Pallas kernels, attend(): pl.pallas_call(functools.partial(_context_kernel, head_size=head_size), g...  18.4 us
    pallas_call x1, Pallas kernels, feed_forward_out(): pl.pallas_call(functools.partial(_ffn_kernel, inner=inner, parts=parts),...  11.1 us
    all_to_all x1, starting transfers between devices, local(): lax.all_to_all(cache_values[source].reshape(devices, per_target, page_len...  11 us
    all_to_all x1, starting transfers between devices, local(): lax.all_to_all(send_meta, 'req', 0, 0, tiled=True).reshape(slot_count, 2)  10.4 us
    gather x1, local copies, waits for them, and re-layouts, local(): cache_keys[source].reshape(devices, per_target, page_len, width)  10.3 us
  transfers between devices with their start and end apart: 3, of which 2 were waited for; matrix products, arithmetic and copies ran while one was open for 11% of the time, Pallas kernels for 12%

profile of v11, /device:TPU:12, one launch (start us, length us, event | category | flops | bytes accessed | tf_op | source)
XLA Modules:
  0.0 280.8 jit_solution(1131047158252980587)
XLA Ops:
  0.6 0.7 fusion.12
  1.4 0.1 reduce_window_sum.11
  1.5 0.8 select_reduce_fusion.3
  2.3 0.7 add_add_fusion
  3.0 0.8 select_reduce_fusion
  3.8 0.1 copy.41
  4.0 0.7 all_to_all.12
  4.7 10.4 %all-to-all-start = ((s32[128,1,4]{2,1,0:T(1,128)}), s32[128,1,4]{2,1,0:T(1,128)S(1)}, u32[]{:S(2)}, u32[]{:S(2)}) async-start(s32[128,1,4]{2,1,0:T(1,128)} %bitcast.4), calls=%async_computation | async-start | bytes 131072 | tf_op jit(solution)/shard_map/all_to_all | solution.py:247
  15.1 10.3 %gather_fusion = bf16[256,16,1024]{2,1,0:T(8,128)(2,1)} fusion(bf16[96,16,1024]{2,1,0:T(8,128)(2,1)} %param.20, s32[1024]{0:T(1024)S(1)} %pad_clamp_fusion), kind=kCustom, calls=%fused_computation | custom fusion | bytes 16778240 | tf_op jit(solution)/shard_map/gather | solution.py:242
  25.4 10.2 %all-to-all-start.1 = ((bf16[128,2,16,1024]{3,2,1,0:T(8,128)(2,1)}), bf16[128,2,16,1024]{3,2,1,0:T(8,128)(2,1)}, u32[]{:S(2)}, u32[]{:S(2)}) async-start(bf16[128,2,16,1024]{3,2,1,0:T(8,128)(2,1)} %bitcast.39), calls=%async_computation.1 | async-start | bytes 16777216 | tf_op jit(solution)/shard_map/all_to_all | solution.py:241
  35.7 8.4 %gather_fusion.1 = bf16[256,16,1024]{2,1,0:T(8,128)(2,1)} fusion(bf16[96,16,1024]{2,1,0:T(8,128)(2,1)S(1)} %copy-done, s32[1024]{0:T(1024)S(1)} %pad_clamp_fusion), kind=kCustom, calls=%fused_computation.1 | custom fusion | bytes 16778240 | tf_op jit(solution)/shard_map/gather | solution.py:245
  44.1 93.1 %all-to-all-done.1 = bf16[128,2,16,1024]{3,2,1,0:T(8,128)(2,1)} async-done(((bf16[128,2,16,1024]{3,2,1,0:T(8,128)(2,1)}), bf16[128,2,16,1024]{3,2,1,0:T(8,128)(2,1)}, u32[]{:S(2)}, u32[]{:S(2)}) %all-to-all-start.1) | async-done | bytes 8388640 | tf_op jit(solution)/shard_map/all_to_all | solution.py:241
  137.2 11.0 %all-to-all-start.2 = ((bf16[128,2,16,1024]{3,2,1,0:T(8,128)(2,1)}), bf16[128,2,16,1024]{3,2,1,0:T(8,128)(2,1)}, u32[]{:S(2)}, u32[]{:S(2)}) async-start(bf16[128,2,16,1024]{3,2,1,0:T(8,128)(2,1)} %bitcast.38), calls=%async_computation.2 | async-start | bytes 16777216 | tf_op jit(solution)/shard_map/all_to_all | solution.py:244
  148.2 0.2 copy.45
  148.4 0.1 convert.12
  148.5 0.2 copy.40
  148.7 0.1 convert.11
  148.9 0.4 convolution_minimum_fusion.5
  149.3 0.3 convolution_minimum_fusion.4
  149.5 0.3 convolution_minimum_fusion.3
  149.8 0.3 convolution_minimum_fusion.2
  150.0 0.3 convolution_minimum_fusion.1
  150.3 0.4 fusion.21
  150.7 0.2 broadcast_multiply_fusion
  150.8 1.1 mul.145.tmask_ref
  152.0 0.8 reshape.283.alive_ref
  152.8 0.6 reshape.258.g_ref
  153.5 0.2 fusion.14
  153.6 1.1 convolution_convert_fusion.1
  154.7 0.5 broadcast.185
  155.2 0.8 reduce.7
  156.0 0.1 reshape.251
  156.1 0.2 slice_reduce_fusion.1
  156.3 0.1 select_reduce_fusion.4
  156.5 0.1 convert_element_type.91
  156.6 0.2 multiply_cosine_fusion
  156.8 0.2 multiply_subtract_fusion
  157.0 0.4 reshape.284
  157.5 1.0 copy.47.kd_ref
  158.5 0.1 subtract_convert_fusion
  158.7 1.0 copy.46.q_ref
  159.7 0.1 fusion.3
  159.8 0.7 select_n.45.kown_ref
  160.5 1.3 convolution_convert_fusion
  161.8 33.8 %shard_map.175 = (bf16[8,2,256,4096]{3,2,1,0:T(8,128)(2,1)}, bf16[8,2,256,256]{3,2,1,0:T(8,128)(2,1)}) custom-call(bf16[256,1024]{1,0:T(8,128)(2,1)} %copy.46.q_ref, bf16[256,16,1024]{2,1,0:T(8,128)(2,1)} %bitcast.10.kc_ref, bf16[256,1024]{1,0:T(8,128)(2,1)} %copy.47.kd_ref, s32[1,4096]{1,0:T(1,128)} %select_n.45.kown_ref, f32[256,256]{1,0:T(8,128)} %mul.145.tmask_ref), custom_call_target="tpu_custom_call" | custom-call | tf_op jit(solution)/shard_map/pallas_call | solution.py:95
  195.6 55.6 %all-to-all-done.2 = bf16[128,2,16,1024]{3,2,1,0:T(8,128)(2,1)} async-done(((bf16[128,2,16,1024]{3,2,1,0:T(8,128)(2,1)}), bf16[128,2,16,1024]{3,2,1,0:T(8,128)(2,1)}, u32[]{:S(2)}, u32[]{:S(2)}) %all-to-all-start.2) | async-done | bytes 8388640 | tf_op jit(solution)/shard_map/all_to_all | solution.py:244
  251.1 18.4 %shard_map.176.c_ref = bf16[256,1024]{1,0:T(8,128)(2,1)} custom-call(bf16[8,2,256,4096]{3,2,1,0:T(8,128)(2,1)} %get-tuple-element.5.pc_ref, bf16[8,2,256,256]{3,2,1,0:T(8,128)(2,1)} %get-tuple-element.6.pd_ref, bf16[256,16,1024]{2,1,0:T(8,128)(2,1)} %bitcast.15.vc_ref, bf16[256,1024]{1,0:T(8,128)(2,1)} %vd_ref.1), custom_call_target="tpu_custom_call" | custom-call | tf_op jit(solution)/shard_map/pallas_call | solution.py:117
  269.5 11.1 %shard_map.177 = bf16[256,1024]{1,0:T(8,128)(2,1)} custom-call(bf16[256,1024]{1,0:T(8,128)(2,1)} %h_ref.1, bf16[256,1024]{1,0:T(8,128)(2,1)} %shard_map.176.c_ref, bf16[1024,1024]{1,0:T(8,128)(2,1)} %wo_hbm.1, bf16[1,1024]{1,0:T(2,128)(2,1)} %reshape.258.g_ref, bf16[1024,5248]{1,0:T(8,128)(2,1)} %win_hbm.1, bf16[2624,1024]{1,0:T(8,128)(2,1)} %wout_hbm.1, ...), custom_call_target="tpu_custom_call" | custom-call | tf_op jit(solution)/shard_map/pallas_call | solution.py:180
  (30 shorter events, 0.4 us)
Async XLA Ops:
  4.7 20.7 %all-to-all-start = ((s32[128,1,4]{2,1,0:T(1,128)}), s32[128,1,4]{2,1,0:T(1,128)S(1)}, u32[]{:S(2)}, u32[]{:S(2)}) async-start(s32[128,1,4]{2,1,0:T(1,128)} %bitcast.4), calls=%async_computation | async-start | bytes 131072 | tf_op jit(solution)/shard_map/all_to_all | solution.py:247
  25.4 10.2 %copy-start = (bf16[96,16,1024]{2,1,0:T(8,128)(2,1)S(1)}, bf16[96,16,1024]{2,1,0:T(8,128)(2,1)}, u32[]{:S(2)}) copy-start(bf16[96,16,1024]{2,1,0:T(8,128)(2,1)} %param.21) | copy-start | bytes 9437188
  25.4 111.8 %all-to-all-start.1 = ((bf16[128,2,16,1024]{3,2,1,0:T(8,128)(2,1)}), bf16[128,2,16,1024]{3,2,1,0:T(8,128)(2,1)}, u32[]{:S(2)}, u32[]{:S(2)}) async-start(bf16[128,2,16,1024]{3,2,1,0:T(8,128)(2,1)} %bitcast.39), calls=%async_computation.1 | async-start | bytes 16777216 | tf_op jit(solution)/shard_map/all_to_all | solution.py:241
  137.2 11.0 %copy-start.2 = (bf16[256,1024]{1,0:T(8,128)(2,1)S(1)}, bf16[256,1024]{1,0:T(8,128)(2,1)}, u32[]{:S(2)}) copy-start(bf16[256,1024]{1,0:T(8,128)(2,1)} %param.18) | copy-start | bytes 1572868
  137.2 11.3 %copy-start.3 = (bf16[256,1024]{1,0:T(8,128)(2,1)S(1)}, bf16[256,1024]{1,0:T(8,128)(2,1)}, u32[]{:S(2)}) copy-start(bf16[256,1024]{1,0:T(8,128)(2,1)} %param.17) | copy-start | bytes 1572868
  137.2 11.7 %copy-start.5 = (s32[4,64]{1,0:T(4,128)S(1)}, s32[4,64]{1,0:T(4,128)}, u32[]{:S(2)}) copy-start(s32[4,64]{1,0:T(4,128)} %param.25) | copy-start | bytes 3076
  137.2 114.0 %all-to-all-start.2 = ((bf16[128,2,16,1024]{3,2,1,0:T(8,128)(2,1)}), bf16[128,2,16,1024]{3,2,1,0:T(8,128)(2,1)}, u32[]{:S(2)}, u32[]{:S(2)}) async-start(bf16[128,2,16,1024]{3,2,1,0:T(8,128)(2,1)} %bitcast.38), calls=%async_computation.2 | async-start | bytes 16777216 | tf_op jit(solution)/shard_map/all_to_all | solution.py:244
  148.2 3.7 %copy-start.6 = (s32[4]{0:T(128)S(1)}, s32[4]{0:T(128)}, u32[]{:S(2)}) copy-start(s32[4]{0:T(128)} %param.26) | copy-start | bytes 52
  148.2 4.6 %copy-start.4 = (bf16[1024]{0:T(1024)(128)(2,1)S(1)}, bf16[1024]{0:T(1024)(128)(2,1)}, u32[]{:S(2)}) copy-start(bf16[1024]{0:T(1024)(128)(2,1)} %param.29) | copy-start | bytes 6148
  148.2 5.2 %copy-start.7 = (s32[4]{0:T(128)S(1)}, s32[4]{0:T(128)}, u32[]{:S(2)}) copy-start(s32[4]{0:T(128)} %param.27) | copy-start | bytes 52
  148.2 5.4 %copy-start.1 = (bf16[256,1024]{1,0:T(8,128)(2,1)S(1)}, bf16[256,1024]{1,0:T(8,128)(2,1)}, u32[]{:S(2)}) copy-start(bf16[256,1024]{1,0:T(8,128)(2,1)} %vd_ref.1) | copy-start | bytes 1572868

commit v12 on v11

--- a/solution.py
+++ b/solution.py
@@ -40,7 +40,7 @@
     return turned.reshape(rows, width).astype(jnp.bfloat16)
 
 
-def _probs_kernel(q_ref, kc_ref, kd_ref, kown_ref, tmask_ref, pc_ref, pd_ref, *,
+def _probs_kernel(q_ref, kc_ref, kd_ref, vd_ref, kown_ref, tmask_ref, pc_ref, cd_ref, *,
                   tree_width, head_size, scale):
     rows, lanes = q_ref.shape
     q = q_ref[...]
@@ -50,7 +50,9 @@
     qown = lax.broadcasted_iota(jnp.int32, (rows, 1), 0) // tree_width
     cmask = qown == kown_ref[...]
     tmask = tmask_ref[...] > 0.5
+    vd = vd_ref[...]
     dims = (((1,), (1,)), ((), ()))
+    draft = None
     for part in range(lanes // head_size):
         sel = (lane >= part * head_size) & (lane < (part + 1) * head_size)
         qh = jnp.where(sel, q, jnp.zeros((), q.dtype))
@@ -63,18 +65,20 @@
         pd = jnp.exp(sd - top)
         inv = 1.0 / (jnp.sum(pc, axis=1, keepdims=True) + jnp.sum(pd, axis=1, keepdims=True))
         pc_ref[part] = (pc * inv).astype(pc_ref.dtype)
-        pd_ref[part] = (pd * inv).astype(pd_ref.dtype)
-
-
-def _context_kernel(pc_ref, pd_ref, vc_ref, vd_ref, o_ref, *, head_size):
+        ctx = jnp.dot((pd * inv).astype(jnp.bfloat16), vd, preferred_element_type=jnp.float32)
+        draft = ctx if draft is None else jnp.where(sel, ctx, draft)
+    cd_ref[...] = draft
+
+
+def _context_kernel(pc_ref, cd_ref, vc_ref, o_ref, *, head_size):
     rows, lanes = o_ref.shape
     vc = vc_ref[...].reshape(-1, lanes)
-    vd = vd_ref[...]
+    draft = cd_ref[...]
     lane = lax.broadcasted_iota(jnp.int32, (1, lanes), 1)
     result = None
     for part in range(lanes // head_size):
         ctx = jnp.dot(pc_ref[part], vc, preferred_element_type=jnp.float32)
-        ctx = ctx + jnp.dot(pd_ref[part], vd, preferred_element_type=jnp.float32)
+        ctx = ctx + draft
         if result is None:
             result = ctx
         else:
@@ -92,7 +96,7 @@
     slots, page_len, _ = recv_k.shape
     keys = slots * page_len
     params = pltpu.CompilerParams(vmem_limit_bytes=60 * 1024 * 1024)
-    probs_c, probs_d = pl.pallas_call(
+    probs_c, draft_ctx = pl.pallas_call(
         functools.partial(
             _probs_kernel, tree_width=tree_width, head_size=head_size, scale=1.0 / head_size**0.5
         ),
@@ -101,32 +105,32 @@
             pl.BlockSpec((rows, lanes), lambda h: (0, h)),
             pl.BlockSpec((slots, page_len, lanes), lambda h: (0, 0, h)),
             pl.BlockSpec((rows, lanes), lambda h: (0, h)),
+            pl.BlockSpec((rows, lanes), lambda h: (0, h)),
             pl.BlockSpec((1, keys), lambda h: (0, 0)),
             pl.BlockSpec((rows, rows), lambda h: (0, 0)),
         ],
         out_specs=[
             pl.BlockSpec((None, per, rows, keys), lambda h: (h, 0, 0, 0)),
-            pl.BlockSpec((None, per, rows, rows), lambda h: (h, 0, 0, 0)),
+            pl.BlockSpec((rows, lanes), lambda h: (0, h)),
         ],
         out_shape=[
             jax.ShapeDtypeStruct((groups, per, rows, keys), jnp.bfloat16),
-            jax.ShapeDtypeStruct((groups, per, rows, rows), jnp.bfloat16),
+            jax.ShapeDtypeStruct((rows, width), jnp.float32),
         ],
         compiler_params=params,
-    )(query_rot, recv_k, key_rot, key_owner, tree_mask)
+    )(query_rot, recv_k, key_rot, draft_value, key_owner, tree_mask)
     return pl.pallas_call(
         functools.partial(_context_kernel, head_size=head_size),
         grid=(groups,),
         in_specs=[
             pl.BlockSpec((None, per, rows, keys), lambda h: (h, 0, 0, 0)),
-            pl.BlockSpec((None, per, rows, rows), lambda h: (h, 0, 0, 0)),
+            pl.BlockSpec((rows, lanes), lambda h: (0, h)),
             pl.BlockSpec((slots, page_len, lanes), lambda h: (0, 0, h)),
-            pl.BlockSpec((rows, lanes), lambda h: (0, h)),
         ],
         out_specs=pl.BlockSpec((rows, lanes), lambda h: (0, h)),
         out_shape=jax.ShapeDtypeStruct((rows, width), jnp.bfloat16),
         compiler_params=params,
-    )(probs_c, probs_d, recv_v, draft_value)
+    )(probs_c, draft_ctx, recv_v)
 
 
 def _ffn_kernel(h_ref, c_ref, wo_hbm, g_ref, win_hbm, wout_hbm, alive_ref, o_ref, wo_v, win_v,

time: 283 us -> 282 us (level)
  waiting for transfers between devices: 149 us -> 144 us
  Pallas kernels: 63.3 us -> 67.2 us
    pallas_call x1, Pallas kernels: 33.8 us -> 38.1 us  [attend(): pl.pallas_call(functools.partial(_probs_kernel, tree_width=tree_width, he...]
    all_to_all x1, waiting for transfers between devices: 55.6 us -> 51.2 us  [local(): lax.all_to_all(cache_values[source].reshape(devices, per_target, page_len...]
  transfers between devices with their start and end apart: 3 -> 3, of which waited for: 2 -> 2; matrix products, arithmetic and copies ran while one was open for 11% -> 11% of each run, Pallas kernels for 12% -> 14%
where the time goes in v12:
time: 282 us; the launch traced here: 280 us
  waiting for transfers between devices  144 us (51%)
  Pallas kernels  67.2 us (24%)
  starting transfers between devices  31.6 us (11%)
  local copies, waits for them, and re-layouts  26.4 us (9%)
  other arithmetic  5.43 us (2%)
  matrix products  4.26 us (2%)
    all_to_all x1, waiting for transfers between devices, local(): lax.all_to_all(cache_keys[source].reshape(devices, per_target, page_len,...  93.1 us
    all_to_all x1, waiting for transfers between devices, local(): lax.all_to_all(cache_values[source].reshape(devices, per_target, page_len...  51.2 us
    pallas_call x1, Pallas kernels, attend(): pl.pallas_call(functools.partial(_probs_kernel, tree_width=tree_width, he...  38.1 us
    pallas_call x1, Pallas kernels, attend(): pl.pallas_call(functools.partial(_context_kernel, head_size=head_size), g...  18 us
    pallas_call x1, Pallas kernels, feed_forward_out(): pl.pallas_call(functools.partial(_ffn_kernel, inner=inner, parts=parts),...  11.1 us
    all_to_all x1, starting transfers between devices, local(): lax.all_to_all(cache_values[source].reshape(devices, per_target, page_len...  11 us
    all_to_all x1, starting transfers between devices, local(): lax.all_to_all(send_meta, 'req', 0, 0, tiled=True).reshape(slot_count, 2)  10.4 us
    gather x1, local copies, waits for them, and re-layouts, local(): cache_keys[source].reshape(devices, per_target, page_len, width)  10.3 us
  transfers between devices with their start and end apart: 3, of which 2 were waited for; matrix products, arithmetic and copies ran while one was open for 11% of the time, Pallas kernels for 14%

profile of v12, /device:TPU:12, one launch (start us, length us, event | category | flops | bytes accessed | tf_op | source)
XLA Modules:
  0.0 280.4 jit_solution(3582739654333200858)
XLA Ops:
  0.6 0.7 fusion.12
  1.4 0.1 reduce_window_sum.11
  1.5 0.8 select_reduce_fusion.3
  2.3 0.7 add_add_fusion
  3.0 0.8 select_reduce_fusion
  3.8 0.1 copy.41
  4.0 0.7 all_to_all.12
  4.7 10.4 %all-to-all-start = ((s32[128,1,4]{2,1,0:T(1,128)}), s32[128,1,4]{2,1,0:T(1,128)S(1)}, u32[]{:S(2)}, u32[]{:S(2)}) async-start(s32[128,1,4]{2,1,0:T(1,128)} %bitcast.4), calls=%async_computation | async-start | bytes 131072 | tf_op jit(solution)/shard_map/all_to_all | solution.py:251
  15.1 10.3 %gather_fusion = bf16[256,16,1024]{2,1,0:T(8,128)(2,1)} fusion(bf16[96,16,1024]{2,1,0:T(8,128)(2,1)} %param.20, s32[1024]{0:T(1024)S(1)} %pad_clamp_fusion), kind=kCustom, calls=%fused_computation | custom fusion | bytes 16778240 | tf_op jit(solution)/shard_map/gather | solution.py:246
  25.4 10.2 %all-to-all-start.1 = ((bf16[128,2,16,1024]{3,2,1,0:T(8,128)(2,1)}), bf16[128,2,16,1024]{3,2,1,0:T(8,128)(2,1)}, u32[]{:S(2)}, u32[]{:S(2)}) async-start(bf16[128,2,16,1024]{3,2,1,0:T(8,128)(2,1)} %bitcast.39), calls=%async_computation.1 | async-start | bytes 16777216 | tf_op jit(solution)/shard_map/all_to_all | solution.py:245
  35.6 8.4 %gather_fusion.1 = bf16[256,16,1024]{2,1,0:T(8,128)(2,1)} fusion(bf16[96,16,1024]{2,1,0:T(8,128)(2,1)S(1)} %copy-done, s32[1024]{0:T(1024)S(1)} %pad_clamp_fusion), kind=kCustom, calls=%fused_computation.1 | custom fusion | bytes 16778240 | tf_op jit(solution)/shard_map/gather | solution.py:249
  44.0 93.1 %all-to-all-done.1 = bf16[128,2,16,1024]{3,2,1,0:T(8,128)(2,1)} async-done(((bf16[128,2,16,1024]{3,2,1,0:T(8,128)(2,1)}), bf16[128,2,16,1024]{3,2,1,0:T(8,128)(2,1)}, u32[]{:S(2)}, u32[]{:S(2)}) %all-to-all-start.1) | async-done | bytes 8388640 | tf_op jit(solution)/shard_map/all_to_all | solution.py:245
  137.2 11.0 %all-to-all-start.2 = ((bf16[128,2,16,1024]{3,2,1,0:T(8,128)(2,1)}), bf16[128,2,16,1024]{3,2,1,0:T(8,128)(2,1)}, u32[]{:S(2)}, u32[]{:S(2)}) async-start(bf16[128,2,16,1024]{3,2,1,0:T(8,128)(2,1)} %bitcast.38), calls=%async_computation.2 | async-start | bytes 16777216 | tf_op jit(solution)/shard_map/all_to_all | solution.py:248
  148.2 0.2 copy.45
  148.4 0.1 convert.12
  148.5 0.2 copy.40
  148.7 0.1 convert.11
  148.9 0.4 convolution_minimum_fusion.5
  149.2 0.3 convolution_minimum_fusion.4
  149.5 0.3 convolution_minimum_fusion.3
  149.8 0.3 convolution_minimum_fusion.2
  150.0 0.3 convolution_minimum_fusion.1
  150.3 0.4 fusion.21
  150.6 0.2 broadcast_multiply_fusion
  150.8 1.0 mul.145.tmask_ref
  151.9 0.8 reshape.283.alive_ref
  152.7 0.6 reshape.258.g_ref
  153.4 0.2 fusion.14
  153.6 1.1 convolution_convert_fusion.1
  154.7 0.5 broadcast.185
  155.2 0.8 reduce.7
  156.0 0.1 reshape.251
  156.1 0.2 slice_reduce_fusion.1
  156.3 0.1 select_reduce_fusion.4
  156.5 0.1 convert_element_type.91
  156.6 0.2 multiply_cosine_fusion
  156.8 0.2 multiply_subtract_fusion
  157.0 0.4 reshape.284
  157.4 1.0 copy.47.kd_ref
  158.4 0.1 subtract_convert_fusion
  158.6 1.0 copy.46.q_ref
  159.6 0.1 fusion.3
  159.8 0.7 select_n.45.kown_ref
  160.5 1.3 convolution_convert_fusion
  161.8 38.1 %shard_map.175 = (bf16[8,2,256,4096]{3,2,1,0:T(8,128)(2,1)}, f32[256,1024]{1,0:T(8,128)}) custom-call(bf16[256,1024]{1,0:T(8,128)(2,1)} %copy.46.q_ref, bf16[256,16,1024]{2,1,0:T(8,128)(2,1)} %bitcast.10.kc_ref, bf16[256,1024]{1,0:T(8,128)(2,1)} %copy.47.kd_ref, bf16[256,1024]{1,0:T(8,128)(2,1)} %vd_ref.1, s32[1,4096]{1,0:T(1,128)} %select_n.45.kown_ref, ...), custom_call_target="tpu_custom_call" | custom-call | tf_op jit(solution)/shard_map/pallas_call | solution.py:99
  199.9 51.2 %all-to-all-done.2 = bf16[128,2,16,1024]{3,2,1,0:T(8,128)(2,1)} async-done(((bf16[128,2,16,1024]{3,2,1,0:T(8,128)(2,1)}), bf16[128,2,16,1024]{3,2,1,0:T(8,128)(2,1)}, u32[]{:S(2)}, u32[]{:S(2)}) %all-to-all-start.2) | async-done | bytes 8388640 | tf_op jit(solution)/shard_map/all_to_all | solution.py:248
  251.1 18.0 %shard_map.176.c_ref = bf16[256,1024]{1,0:T(8,128)(2,1)} custom-call(bf16[8,2,256,4096]{3,2,1,0:T(8,128)(2,1)} %get-tuple-element.5.pc_ref, f32[256,1024]{1,0:T(8,128)} %get-tuple-element.6.cd_ref, bf16[256,16,1024]{2,1,0:T(8,128)(2,1)} %bitcast.15.vc_ref), custom_call_target="tpu_custom_call" | custom-call | tf_op jit(solution)/shard_map/pallas_call | solution.py:122
  269.1 11.1 %shard_map.177 = bf16[256,1024]{1,0:T(8,128)(2,1)} custom-call(bf16[256,1024]{1,0:T(8,128)(2,1)} %h_ref.1, bf16[256,1024]{1,0:T(8,128)(2,1)} %shard_map.176.c_ref, bf16[1024,1024]{1,0:T(8,128)(2,1)} %wo_hbm.1, bf16[1,1024]{1,0:T(2,128)(2,1)} %reshape.258.g_ref, bf16[1024,5248]{1,0:T(8,128)(2,1)} %win_hbm.1, bf16[2624,1024]{1,0:T(8,128)(2,1)} %wout_hbm.1, ...), custom_call_target="tpu_custom_call" | custom-call | tf_op jit(solution)/shard_map/pallas_call | solution.py:184
  (30 shorter events, 0.4 us)
Async XLA Ops:
  4.7 20.7 %all-to-all-start = ((s32[128,1,4]{2,1,0:T(1,128)}), s32[128,1,4]{2,1,0:T(1,128)S(1)}, u32[]{:S(2)}, u32[]{:S(2)}) async-start(s32[128,1,4]{2,1,0:T(1,128)} %bitcast.4), calls=%async_computation | async-start | bytes 131072 | tf_op jit(solution)/shard_map/all_to_all | solution.py:251
  25.4 10.2 %copy-start = (bf16[96,16,1024]{2,1,0:T(8,128)(2,1)S(1)}, bf16[96,16,1024]{2,1,0:T(8,128)(2,1)}, u32[]{:S(2)}) copy-start(bf16[96,16,1024]{2,1,0:T(8,128)(2,1)} %param.21) | copy-start | bytes 9437188
  25.4 111.7 %all-to-all-start.1 = ((bf16[128,2,16,1024]{3,2,1,0:T(8,128)(2,1)}), bf16[128,2,16,1024]{3,2,1,0:T(8,128)(2,1)}, u32[]{:S(2)}, u32[]{:S(2)}) async-start(bf16[128,2,16,1024]{3,2,1,0:T(8,128)(2,1)} %bitcast.39), calls=%async_computation.1 | async-start | bytes 16777216 | tf_op jit(solution)/shard_map/all_to_all | solution.py:245
  137.2 11.0 %copy-start.2 = (bf16[256,1024]{1,0:T(8,128)(2,1)S(1)}, bf16[256,1024]{1,0:T(8,128)(2,1)}, u32[]{:S(2)}) copy-start(bf16[256,1024]{1,0:T(8,128)(2,1)} %param.18) | copy-start | bytes 1572868
  137.2 11.3 %copy-start.3 = (bf16[256,1024]{1,0:T(8,128)(2,1)S(1)}, bf16[256,1024]{1,0:T(8,128)(2,1)}, u32[]{:S(2)}) copy-start(bf16[256,1024]{1,0:T(8,128)(2,1)} %param.17) | copy-start | bytes 1572868
  137.2 11.7 %copy-start.5 = (s32[4,64]{1,0:T(4,128)S(1)}, s32[4,64]{1,0:T(4,128)}, u32[]{:S(2)}) copy-start(s32[4,64]{1,0:T(4,128)} %param.25) | copy-start | bytes 3076
  137.2 114.0 %all-to-all-start.2 = ((bf16[128,2,16,1024]{3,2,1,0:T(8,128)(2,1)}), bf16[128,2,16,1024]{3,2,1,0:T(8,128)(2,1)}, u32[]{:S(2)}, u32[]{:S(2)}) async-start(bf16[128,2,16,1024]{3,2,1,0:T(8,128)(2,1)} %bitcast.38), calls=%async_computation.2 | async-start | bytes 16777216 | tf_op jit(solution)/shard_map/all_to_all | solution.py:248
  148.1 3.7 %copy-start.6 = (s32[4]{0:T(128)S(1)}, s32[4]{0:T(128)}, u32[]{:S(2)}) copy-start(s32[4]{0:T(128)} %param.26) | copy-start | bytes 52
  148.1 4.6 %copy-start.4 = (bf16[1024]{0:T(1024)(128)(2,1)S(1)}, bf16[1024]{0:T(1024)(128)(2,1)}, u32[]{:S(2)}) copy-start(bf16[1024]{0:T(1024)(128)(2,1)} %param.29) | copy-start | bytes 6148
  148.2 5.2 %copy-start.7 = (s32[4]{0:T(128)S(1)}, s32[4]{0:T(128)}, u32[]{:S(2)}) copy-start(s32[4]{0:T(128)} %param.27) | copy-start | bytes 52
  148.2 5.4 %copy-start.1 = (bf16[256,1024]{1,0:T(8,128)(2,1)S(1)}, bf16[256,1024]{1,0:T(8,128)(2,1)}, u32[]{:S(2)}) copy-start(bf16[256,1024]{1,0:T(8,128)(2,1)} %vd_ref.1) | copy-start | bytes 1572868

commit v13 on v12

--- a/solution.py
+++ b/solution.py
@@ -72,19 +72,19 @@
 
 def _context_kernel(pc_ref, cd_ref, vc_ref, o_ref, *, head_size):
     rows, lanes = o_ref.shape
+    part = pl.program_id(0) % (lanes // head_size)
     vc = vc_ref[...].reshape(-1, lanes)
-    draft = cd_ref[...]
+    ctx = jnp.dot(pc_ref[...], vc, preferred_element_type=jnp.float32) + cd_ref[...]
     lane = lax.broadcasted_iota(jnp.int32, (1, lanes), 1)
-    result = None
-    for part in range(lanes // head_size):
-        ctx = jnp.dot(pc_ref[part], vc, preferred_element_type=jnp.float32)
-        ctx = ctx + draft
-        if result is None:
-            result = ctx
-        else:
-            sel = (lane >= part * head_size) & (lane < (part + 1) * head_size)
-            result = jnp.where(sel, ctx, result)
-    o_ref[...] = result.astype(o_ref.dtype)
+
+    @pl.when(part == 0)
+    def _():
+        o_ref[...] = ctx.astype(o_ref.dtype)
+
+    @pl.when(part > 0)
+    def _():
+        sel = lane >= part * head_size
+        o_ref[...] = jnp.where(sel, ctx.astype(o_ref.dtype), o_ref[...])
 
 
 def attend(query_rot, recv_k, recv_v, key_rot, draft_value, key_owner, tree_mask, tree_width):
@@ -121,13 +121,13 @@
     )(query_rot, recv_k, key_rot, draft_value, key_owner, tree_mask)
     return pl.pallas_call(
         functools.partial(_context_kernel, head_size=head_size),
-        grid=(groups,),
+        grid=(groups * per,),
         in_specs=[
-            pl.BlockSpec((None, per, rows, keys), lambda h: (h, 0, 0, 0)),
-            pl.BlockSpec((rows, lanes), lambda h: (0, h)),
-            pl.BlockSpec((slots, page_len, lanes), lambda h: (0, 0, h)),
-        ],
-        out_specs=pl.BlockSpec((rows, lanes), lambda h: (0, h)),
+            pl.BlockSpec((None, None, rows, keys), lambda h: (h // per, h % per, 0, 0)),
+            pl.BlockSpec((rows, lanes), lambda h: (0, h // per)),
+            pl.BlockSpec((slots, page_len, lanes), lambda h: (0, 0, h // per)),
+        ],
+        out_specs=pl.BlockSpec((rows, lanes), lambda h: (0, h // per)),
         out_shape=jax.ShapeDtypeStruct((rows, width), jnp.bfloat16),
         compiler_params=params,
     )(probs_c, draft_ctx, recv_v)

time: 282 us -> 287 us (1.018)
  Pallas kernels: 67.2 us -> 72.2 us
    pallas_call x1, Pallas kernels: 18 us -> 23 us  [attend(): pl.pallas_call(functools.partial(_context_kernel, head_size=head_size), g...]
  transfers between devices with their start and end apart: 3 -> 3, of which waited for: 2 -> 2; matrix products, arithmetic and copies ran while one was open for 11% -> 11% of each run, Pallas kernels for 14% -> 13%
where the time goes in v13:
time: 287 us; the launch traced here: 285 us
  waiting for transfers between devices  144 us (50%)
  Pallas kernels  72.2 us (25%)
  starting transfers between devices  31.6 us (11%)
  local copies, waits for them, and re-layouts  26.5 us (9%)
  other arithmetic  5.43 us (2%)
  matrix products  4.26 us (1%)
    all_to_all x1, waiting for transfers between devices, local(): lax.all_to_all(cache_keys[source].reshape(devices, per_target, page_len,...  93.1 us
    all_to_all x1, waiting for transfers between devices, local(): lax.all_to_all(cache_values[source].reshape(devices, per_target, page_len...  51.2 us
    pallas_call x1, Pallas kernels, attend(): pl.pallas_call(functools.partial(_probs_kernel, tree_width=tree_width, he...  38.1 us
    pallas_call x1, Pallas kernels, attend(): pl.pallas_call(functools.partial(_context_kernel, head_size=head_size), g...  23 us
    pallas_call x1, Pallas kernels, feed_forward_out(): pl.pallas_call(functools.partial(_ffn_kernel, inner=inner, parts=parts),...  11.1 us
    all_to_all x1, starting transfers between devices, local(): lax.all_to_all(cache_values[source].reshape(devices, per_target, page_len...  11 us
    all_to_all x1, starting transfers between devices, local(): lax.all_to_all(send_meta, 'req', 0, 0, tiled=True).reshape(slot_count, 2)  10.4 us
    gather x1, local copies, waits for them, and re-layouts, local(): cache_keys[source].reshape(devices, per_target, page_len, width)  10.3 us
  transfers between devices with their start and end apart: 3, of which 2 were waited for; matrix products, arithmetic and copies ran while one was open for 11% of the time, Pallas kernels for 13%

profile of v13, /device:TPU:12, one launch (start us, length us, event | category | flops | bytes accessed | tf_op | source)
XLA Modules:
  0.0 285.4 jit_solution(15642009430936290100)
XLA Ops:
  0.6 0.7 fusion.12
  1.4 0.1 reduce_window_sum.11
  1.5 0.8 select_reduce_fusion.3
  2.3 0.7 add_add_fusion
  3.0 0.8 select_reduce_fusion
  3.8 0.1 copy.41
  4.0 0.7 all_to_all.12
  4.7 10.4 %all-to-all-start = ((s32[128,1,4]{2,1,0:T(1,128)}), s32[128,1,4]{2,1,0:T(1,128)S(1)}, u32[]{:S(2)}, u32[]{:S(2)}) async-start(s32[128,1,4]{2,1,0:T(1,128)} %bitcast.4), calls=%async_computation | async-start | bytes 131072 | tf_op jit(solution)/shard_map/all_to_all | solution.py:251
  15.1 10.3 %gather_fusion = bf16[256,16,1024]{2,1,0:T(8,128)(2,1)} fusion(bf16[96,16,1024]{2,1,0:T(8,128)(2,1)} %param.20, s32[1024]{0:T(1024)S(1)} %pad_clamp_fusion), kind=kCustom, calls=%fused_computation | custom fusion | bytes 16778240 | tf_op jit(solution)/shard_map/gather | solution.py:246
  25.4 10.2 %all-to-all-start.1 = ((bf16[128,2,16,1024]{3,2,1,0:T(8,128)(2,1)}), bf16[128,2,16,1024]{3,2,1,0:T(8,128)(2,1)}, u32[]{:S(2)}, u32[]{:S(2)}) async-start(bf16[128,2,16,1024]{3,2,1,0:T(8,128)(2,1)} %bitcast.39), calls=%async_computation.1 | async-start | bytes 16777216 | tf_op jit(solution)/shard_map/all_to_all | solution.py:245
  35.7 8.4 %gather_fusion.1 = bf16[256,16,1024]{2,1,0:T(8,128)(2,1)} fusion(bf16[96,16,1024]{2,1,0:T(8,128)(2,1)S(1)} %copy-done, s32[1024]{0:T(1024)S(1)} %pad_clamp_fusion), kind=kCustom, calls=%fused_computation.1 | custom fusion | bytes 16778240 | tf_op jit(solution)/shard_map/gather | solution.py:249
  44.1 93.1 %all-to-all-done.1 = bf16[128,2,16,1024]{3,2,1,0:T(8,128)(2,1)} async-done(((bf16[128,2,16,1024]{3,2,1,0:T(8,128)(2,1)}), bf16[128,2,16,1024]{3,2,1,0:T(8,128)(2,1)}, u32[]{:S(2)}, u32[]{:S(2)}) %all-to-all-start.1) | async-done | bytes 8388640 | tf_op jit(solution)/shard_map/all_to_all | solution.py:245
  137.2 11.0 %all-to-all-start.2 = ((bf16[128,2,16,1024]{3,2,1,0:T(8,128)(2,1)}), bf16[128,2,16,1024]{3,2,1,0:T(8,128)(2,1)}, u32[]{:S(2)}, u32[]{:S(2)}) async-start(bf16[128,2,16,1024]{3,2,1,0:T(8,128)(2,1)} %bitcast.38), calls=%async_computation.2 | async-start | bytes 16777216 | tf_op jit(solution)/shard_map/all_to_all | solution.py:248
  148.2 0.2 copy.45
  148.4 0.1 convert.12
  148.5 0.2 copy.40
  148.7 0.1 convert.11
  148.9 0.4 convolution_minimum_fusion.5
  149.3 0.3 convolution_minimum_fusion.4
  149.5 0.3 convolution_minimum_fusion.3
  149.8 0.3 convolution_minimum_fusion.2
  150.0 0.3 convolution_minimum_fusion.1
  150.3 0.4 fusion.21
  150.7 0.2 broadcast_multiply_fusion
  150.8 1.0 mul.145.tmask_ref
  151.9 0.8 reshape.283.alive_ref
  152.7 0.6 reshape.258.g_ref
  153.4 0.2 fusion.14
  153.6 1.1 convolution_convert_fusion.1
  154.7 0.5 broadcast.185
  155.2 0.8 reduce.7
  156.0 0.1 reshape.251
  156.1 0.2 slice_reduce_fusion.1
  156.3 0.1 select_reduce_fusion.4
  156.5 0.1 convert_element_type.91
  156.6 0.2 multiply_cosine_fusion
  156.8 0.2 multiply_subtract_fusion
  157.0 0.4 reshape.284
  157.4 1.0 copy.47.kd_ref
  158.5 0.1 subtract_convert_fusion
  158.7 1.0 copy.46.q_ref
  159.7 0.1 fusion.3
  159.8 0.7 select_n.45.kown_ref
  160.5 1.3 convolution_convert_fusion
  161.8 38.1 %shard_map.175 = (bf16[8,2,256,4096]{3,2,1,0:T(8,128)(2,1)}, f32[256,1024]{1,0:T(8,128)}) custom-call(bf16[256,1024]{1,0:T(8,128)(2,1)} %copy.46.q_ref, bf16[256,16,1024]{2,1,0:T(8,128)(2,1)} %bitcast.10.kc_ref, bf16[256,1024]{1,0:T(8,128)(2,1)} %copy.47.kd_ref, bf16[256,1024]{1,0:T(8,128)(2,1)} %vd_ref.1, s32[1,4096]{1,0:T(1,128)} %select_n.45.kown_ref, ...), custom_call_target="tpu_custom_call" | custom-call | tf_op jit(solution)/shard_map/pallas_call | solution.py:99
  199.9 51.2 %all-to-all-done.2 = bf16[128,2,16,1024]{3,2,1,0:T(8,128)(2,1)} async-done(((bf16[128,2,16,1024]{3,2,1,0:T(8,128)(2,1)}), bf16[128,2,16,1024]{3,2,1,0:T(8,128)(2,1)}, u32[]{:S(2)}, u32[]{:S(2)}) %all-to-all-start.2) | async-done | bytes 8388640 | tf_op jit(solution)/shard_map/all_to_all | solution.py:248
  251.1 23.0 %shard_map.176.c_ref = bf16[256,1024]{1,0:T(8,128)(2,1)} custom-call(bf16[8,2,256,4096]{3,2,1,0:T(8,128)(2,1)} %get-tuple-element.5.pc_ref, f32[256,1024]{1,0:T(8,128)} %get-tuple-element.6.cd_ref, bf16[256,16,1024]{2,1,0:T(8,128)(2,1)} %bitcast.15.vc_ref), custom_call_target="tpu_custom_call" | custom-call | tf_op jit(solution)/shard_map/pallas_call | solution.py:122
  274.1 11.1 %shard_map.177 = bf16[256,1024]{1,0:T(8,128)(2,1)} custom-call(bf16[256,1024]{1,0:T(8,128)(2,1)} %h_ref.1, bf16[256,1024]{1,0:T(8,128)(2,1)} %shard_map.176.c_ref, bf16[1024,1024]{1,0:T(8,128)(2,1)} %wo_hbm.1, bf16[1,1024]{1,0:T(2,128)(2,1)} %reshape.258.g_ref, bf16[1024,5248]{1,0:T(8,128)(2,1)} %win_hbm.1, bf16[2624,1024]{1,0:T(8,128)(2,1)} %wout_hbm.1, ...), custom_call_target="tpu_custom_call" | custom-call | tf_op jit(solution)/shard_map/pallas_call | solution.py:184
  (30 shorter events, 0.4 us)
Async XLA Ops:
  4.7 20.7 %all-to-all-start = ((s32[128,1,4]{2,1,0:T(1,128)}), s32[128,1,4]{2,1,0:T(1,128)S(1)}, u32[]{:S(2)}, u32[]{:S(2)}) async-start(s32[128,1,4]{2,1,0:T(1,128)} %bitcast.4), calls=%async_computation | async-start | bytes 131072 | tf_op jit(solution)/shard_map/all_to_all | solution.py:251
  25.4 10.2 %copy-start = (bf16[96,16,1024]{2,1,0:T(8,128)(2,1)S(1)}, bf16[96,16,1024]{2,1,0:T(8,128)(2,1)}, u32[]{:S(2)}) copy-start(bf16[96,16,1024]{2,1,0:T(8,128)(2,1)} %param.21) | copy-start | bytes 9437188
  25.4 111.8 %all-to-all-start.1 = ((bf16[128,2,16,1024]{3,2,1,0:T(8,128)(2,1)}), bf16[128,2,16,1024]{3,2,1,0:T(8,128)(2,1)}, u32[]{:S(2)}, u32[]{:S(2)}) async-start(bf16[128,2,16,1024]{3,2,1,0:T(8,128)(2,1)} %bitcast.39), calls=%async_computation.1 | async-start | bytes 16777216 | tf_op jit(solution)/shard_map/all_to_all | solution.py:245
  137.2 11.0 %copy-start.2 = (bf16[256,1024]{1,0:T(8,128)(2,1)S(1)}, bf16[256,1024]{1,0:T(8,128)(2,1)}, u32[]{:S(2)}) copy-start(bf16[256,1024]{1,0:T(8,128)(2,1)} %param.18) | copy-start | bytes 1572868
  137.2 11.3 %copy-start.3 = (bf16[256,1024]{1,0:T(8,128)(2,1)S(1)}, bf16[256,1024]{1,0:T(8,128)(2,1)}, u32[]{:S(2)}) copy-start(bf16[256,1024]{1,0:T(8,128)(2,1)} %param.17) | copy-start | bytes 1572868
  137.2 11.7 %copy-start.5 = (s32[4,64]{1,0:T(4,128)S(1)}, s32[4,64]{1,0:T(4,128)}, u32[]{:S(2)}) copy-start(s32[4,64]{1,0:T(4,128)} %param.25) | copy-start | bytes 3076
  137.2 114.0 %all-to-all-start.2 = ((bf16[128,2,16,1024]{3,2,1,0:T(8,128)(2,1)}), bf16[128,2,16,1024]{3,2,1,0:T(8,128)(2,1)}, u32[]{:S(2)}, u32[]{:S(2)}) async-start(bf16[128,2,16,1024]{3,2,1,0:T(8,128)(2,1)} %bitcast.38), calls=%async_computation.2 | async-start | bytes 16777216 | tf_op jit(solution)/shard_map/all_to_all | solution.py:248
  148.2 3.7 %copy-start.6 = (s32[4]{0:T(128)S(1)}, s32[4]{0:T(128)}, u32[]{:S(2)}) copy-start(s32[4]{0:T(128)} %param.26) | copy-start | bytes 52
  148.2 4.6 %copy-start.4 = (bf16[1024]{0:T(1024)(128)(2,1)S(1)}, bf16[1024]{0:T(1024)(128)(2,1)}, u32[]{:S(2)}) copy-start(bf16[1024]{0:T(1024)(128)(2,1)} %param.29) | copy-start | bytes 6148
  148.2 5.2 %copy-start.7 = (s32[4]{0:T(128)S(1)}, s32[4]{0:T(128)}, u32[]{:S(2)}) copy-start(s32[4]{0:T(128)} %param.27) | copy-start | bytes 52
  148.2 5.4 %copy-start.1 = (bf16[256,1024]{1,0:T(8,128)(2,1)S(1)}, bf16[256,1024]{1,0:T(8,128)(2,1)}, u32[]{:S(2)}) copy-start(bf16[256,1024]{1,0:T(8,128)(2,1)} %vd_ref.1) | copy-start | bytes 1572868
